TPU v7x, 32 devices: a whole 2x2x4 slice. The times are simulated.
32 devices in a mesh: grp: 2 (over y), row: 4 (over z), col: 2 (over x), vec: 2 (over core).
Axes of the slice: x: 2, y: 2, z: 4, core: 2. Of those that a mesh axis runs over, the one named last changes fastest.
Arguments:
- start: float32 [64, 2048], P('vec', ('grp', 'row')), parts along dimension 1, may hold values from -6 to 6
- tiles: bfloat16 [16, 32, 128, 128], P(('grp', 'row'), 'col'), parts along dimension 0, may hold values from -6 to 6
- pattern: int32 [16, 32], P(('grp', 'row')), parts along dimension 0, may hold values from 0 to 7
- counts: int32 [16], P(('grp', 'row')), parts along dimension 0, may hold values from 1 to 32
Outputs:
- basis: float32 [64, 2048], P('vec', ('grp', 'row')), parts along dimension 1
There are 2 independent parts, one for each index of `grp`. A program takes and returns all parts, laid end to end along the dimension named above; each array names one. Nothing has to cross between parts.
Inputs may be any that keep to these rules, and one draw needn't show every extreme that they name: pattern may name a block column more than once in a block row; such tiles add.
All inputs are finite; a program needn't handle non-finite values.
Results may differ from a plain program's by a relative error of at most 0.03.
Values may be sent and summed in bfloat16 or wider, within the bound.
No kernel may reach another device: no remote copies, remote signals or barrier semaphores. Data moves between devices by JAX's collectives and lax.ppermute only.
A program may use at most 64 MiB of HBM per device.

v0:
```python
import jax
import jax.numpy as jnp
from jax import lax
from jax.sharding import PartitionSpec as P

DEGREE = 8
ITERS = 2


HALF_WIDTH = 2.0
EPSILON = 1e-06


def row_scaling(square_sums, live_counts, block):
    entries = (live_counts * block).astype(jnp.float32)[:, None]
    scaled = lax.rsqrt(square_sums / entries + EPSILON) / jnp.sqrt(entries)
    return (scaled / HALF_WIDTH).reshape(1, -1)


def chebyshev(first, apply):
    previous = first
    present = apply(first)
    for step in range(DEGREE - 1):
        previous, present = (present, 2.0 * apply(present) - previous)
    return present


def orthonormal(mine, total_rows):
    both = lax.all_gather(mine.astype(jnp.bfloat16), "vec", axis=0, tiled=True).astype(mine.dtype)
    part_gram = jnp.dot(both, both.T, precision=lax.Precision.HIGHEST)
    gram = lax.psum(part_gram, "row") / total_rows
    lower = jnp.linalg.cholesky(gram)
    solved = jax.scipy.linalg.solve_triangular(lower, both, lower=True)
    width = mine.shape[0]
    return lax.dynamic_slice_in_dim(solved, lax.axis_index("vec") * width, width, 0)


def per_device(start, tiles, pattern, counts):
    nb_dev = tiles.shape[0]
    block = tiles.shape[2]
    total_rows = nb_dev * block * lax.axis_size("row")
    vec_cols = start.shape[0]
    col_index = lax.axis_index("col")
    kb_dev = tiles.shape[1]
    slot_ids = col_index * kb_dev + jnp.arange(kb_dev, dtype=jnp.int32)
    live = (slot_ids[None, :] < counts[:, None]).astype(jnp.bfloat16)
    masked = tiles * live[:, :, None, None]
    local_pattern = lax.dynamic_slice_in_dim(pattern, col_index * kb_dev, kb_dev, 1)
    partial_squares = jnp.einsum(
        "bkmn,bkmn->bm", masked, masked, preferred_element_type=jnp.float32
    )
    square_sums = lax.psum(partial_squares, "col")
    scaling = row_scaling(square_sums, counts, block)

    def apply_slots(current):
        whole = lax.all_gather(current.astype(jnp.bfloat16), "row", axis=1, tiled=True)
        blocks = whole.reshape(vec_cols, -1, block)
        picked = jnp.take(blocks, local_pattern, axis=1)
        product = jnp.einsum("cbkn,bkmn->cbm", picked, masked, preferred_element_type=jnp.float32)
        total = lax.psum(product.astype(jnp.bfloat16), "col").astype(jnp.float32)
        return total.reshape(vec_cols, -1) * scaling

    current = start
    for outer in range(ITERS):
        filtered = chebyshev(current, apply_slots)
        current = orthonormal(filtered, total_rows)
    return current


def solution(mesh):
    in_specs = (
        P("vec", ("grp", "row")),
        P(("grp", "row"), "col", None, None),
        P(("grp", "row"), None),
        P(("grp", "row")),
    )
    out_specs = P("vec", ("grp", "row"))
    return jax.shard_map(
        per_device, mesh=mesh, in_specs=in_specs, out_specs=out_specs, check_vma=False
    )
```

profile of v0, /device:TPU:0, one launch (start us, length us, event | category | flops | bytes accessed | tf_op | source)
XLA Modules:
  0.0 427.7 jit_solution(17464882422868183498)
XLA Ops:
  9.9 14.0 %all_gather.54 = bf16[32,1024]{1,0:T(8,128)(2,1)S(1)} all-gather(bf16[32,256]{1,0:T(8,128)(2,1)S(1)} %convert_element_type.183), channel_id=1, replica_groups=mesh['grp'=2,'row'=4,'col'=2,'vec'=2] {'row'}, dimensions={1}, use_global_device_ids=true | all-gather | bytes 81920 | tf_op jit(solution)/shard_map/all_gather | solution.py:56
  25.1 8.2 %psum.133 = bf16[32,256]{1,0:T(8,128)(2,1)S(1)} all-reduce(bf16[32,256]{1,0:T(8,128)(2,1)S(1)} %bitcast.395), channel_id=1, replica_groups=mesh['grp'=2,'row'=4,'col'=2,'vec'=2] {'col'}, use_global_device_ids=true, to_apply=%region_0.2 | all-reduce | flops 8192 | bytes 32768 | tf_op jit(solution)/shard_map/psum | solution.py:60
  33.3 13.2 %all_gather.55 = bf16[32,1024]{1,0:T(8,128)(2,1)S(1)} all-gather(bf16[32,256]{1,0:T(8,128)(2,1)S(1)} %fusion.110), channel_id=1, replica_groups=mesh['grp'=2,'row'=4,'col'=2,'vec'=2] {'row'}, dimensions={1}, use_global_device_ids=true | all-gather | bytes 81920 | tf_op jit(solution)/shard_map/all_gather | solution.py:56
  54.8 13.2 %all_gather.56 = bf16[32,1024]{1,0:T(8,128)(2,1)S(1)} all-gather(bf16[32,256]{1,0:T(8,128)(2,1)S(1)} %fusion.113), channel_id=1, replica_groups=mesh['grp'=2,'row'=4,'col'=2,'vec'=2] {'row'}, dimensions={1}, use_global_device_ids=true | all-gather | bytes 81920 | tf_op jit(solution)/shard_map/all_gather | solution.py:56
  69.2 8.1 %psum.136 = bf16[32,256]{1,0:T(8,128)(2,1)S(1)} all-reduce(bf16[32,256]{1,0:T(8,128)(2,1)S(1)} %bitcast.397), channel_id=1, replica_groups=mesh['grp'=2,'row'=4,'col'=2,'vec'=2] {'col'}, use_global_device_ids=true, to_apply=%region_3.5 | all-reduce | flops 8192 | bytes 32768 | tf_op jit(solution)/shard_map/psum | solution.py:60
  77.4 13.2 %all_gather.57 = bf16[32,1024]{1,0:T(8,128)(2,1)S(1)} all-gather(bf16[32,256]{1,0:T(8,128)(2,1)S(1)} %fusion.111), channel_id=1, replica_groups=mesh['grp'=2,'row'=4,'col'=2,'vec'=2] {'row'}, dimensions={1}, use_global_device_ids=true | all-gather | bytes 81920 | tf_op jit(solution)/shard_map/all_gather | solution.py:56
  98.9 13.2 %all_gather.58 = bf16[32,1024]{1,0:T(8,128)(2,1)S(1)} all-gather(bf16[32,256]{1,0:T(8,128)(2,1)S(1)} %fusion.137), channel_id=1, replica_groups=mesh['grp'=2,'row'=4,'col'=2,'vec'=2] {'row'}, dimensions={1}, use_global_device_ids=true | all-gather | bytes 81920 | tf_op jit(solution)/shard_map/all_gather | solution.py:56
  113.3 8.1 %psum.138 = bf16[32,256]{1,0:T(8,128)(2,1)S(1)} all-reduce(bf16[32,256]{1,0:T(8,128)(2,1)S(1)} %bitcast.399), channel_id=1, replica_groups=mesh['grp'=2,'row'=4,'col'=2,'vec'=2] {'col'}, use_global_device_ids=true, to_apply=%region_5.7 | all-reduce | flops 8192 | bytes 32768 | tf_op jit(solution)/shard_map/psum | solution.py:60
  121.5 13.1 %all_gather.59 = bf16[32,1024]{1,0:T(8,128)(2,1)S(1)} all-gather(bf16[32,256]{1,0:T(8,128)(2,1)S(1)} %fusion.116), channel_id=1, replica_groups=mesh['grp'=2,'row'=4,'col'=2,'vec'=2] {'row'}, dimensions={1}, use_global_device_ids=true | all-gather | bytes 81920 | tf_op jit(solution)/shard_map/all_gather | solution.py:56
  143.1 13.2 %all_gather.60 = bf16[32,1024]{1,0:T(8,128)(2,1)S(1)} all-gather(bf16[32,256]{1,0:T(8,128)(2,1)S(1)} %fusion.114), channel_id=1, replica_groups=mesh['grp'=2,'row'=4,'col'=2,'vec'=2] {'row'}, dimensions={1}, use_global_device_ids=true | all-gather | bytes 81920 | tf_op jit(solution)/shard_map/all_gather | solution.py:56
  157.4 8.0 %psum.140 = bf16[32,256]{1,0:T(8,128)(2,1)S(1)} all-reduce(bf16[32,256]{1,0:T(8,128)(2,1)S(1)} %bitcast.401), channel_id=1, replica_groups=mesh['grp'=2,'row'=4,'col'=2,'vec'=2] {'col'}, use_global_device_ids=true, to_apply=%region_7.9 | all-reduce | flops 8192 | bytes 32768 | tf_op jit(solution)/shard_map/psum | solution.py:60
  165.5 13.1 %all_gather.61 = bf16[32,1024]{1,0:T(8,128)(2,1)S(1)} all-gather(bf16[32,256]{1,0:T(8,128)(2,1)S(1)} %subtract_convert_fusion.3), channel_id=1, replica_groups=mesh['grp'=2,'row'=4,'col'=2,'vec'=2] {'row'}, dimensions={1}, use_global_device_ids=true | all-gather | bytes 81920 | tf_op jit(solution)/shard_map/all_gather | solution.py:56
  189.1 18.8 %psum.142 = f32[64,64]{0,1:T(8,128)S(1)} all-reduce(f32[64,64]{0,1:T(8,128)S(1)} %fusion.138), channel_id=1, replica_groups=mesh['grp'=2,'row'=4,'col'=2,'vec'=2] {'row'}, use_global_device_ids=true, to_apply=%region_9.11 | all-reduce | flops 4096 | bytes 32768 | tf_op jit(solution)/shard_map/psum | solution.py:31
  220.4 13.1 %all_gather.63 = bf16[32,1024]{1,0:T(8,128)(2,1)S(1)} all-gather(bf16[32,256]{1,0:T(8,128)(2,1)S(1)} %dynamic-slice_convert_fusion), channel_id=1, replica_groups=mesh['grp'=2,'row'=4,'col'=2,'vec'=2] {'row'}, dimensions={1}, use_global_device_ids=true | all-gather | bytes 81920 | tf_op jit(solution)/shard_map/all_gather | solution.py:56
  234.7 8.0 %psum.143 = bf16[32,256]{1,0:T(8,128)(2,1)S(1)} all-reduce(bf16[32,256]{1,0:T(8,128)(2,1)S(1)} %bitcast.403), channel_id=1, replica_groups=mesh['grp'=2,'row'=4,'col'=2,'vec'=2] {'col'}, use_global_device_ids=true, to_apply=%region_12.16 | all-reduce | flops 8192 | bytes 32768 | tf_op jit(solution)/shard_map/psum | solution.py:60
  242.8 13.2 %all_gather.64 = bf16[32,1024]{1,0:T(8,128)(2,1)S(1)} all-gather(bf16[32,256]{1,0:T(8,128)(2,1)S(1)} %fusion.109), channel_id=1, replica_groups=mesh['grp'=2,'row'=4,'col'=2,'vec'=2] {'row'}, dimensions={1}, use_global_device_ids=true | all-gather | bytes 81920 | tf_op jit(solution)/shard_map/all_gather | solution.py:56
  264.4 13.1 %all_gather.65 = bf16[32,1024]{1,0:T(8,128)(2,1)S(1)} all-gather(bf16[32,256]{1,0:T(8,128)(2,1)S(1)} %fusion.136), channel_id=1, replica_groups=mesh['grp'=2,'row'=4,'col'=2,'vec'=2] {'row'}, dimensions={1}, use_global_device_ids=true | all-gather | bytes 81920 | tf_op jit(solution)/shard_map/all_gather | solution.py:56
  278.8 8.0 %psum.145 = bf16[32,256]{1,0:T(8,128)(2,1)S(1)} all-reduce(bf16[32,256]{1,0:T(8,128)(2,1)S(1)} %bitcast.405), channel_id=1, replica_groups=mesh['grp'=2,'row'=4,'col'=2,'vec'=2] {'col'}, use_global_device_ids=true, to_apply=%region_14.18 | all-reduce | flops 8192 | bytes 32768 | tf_op jit(solution)/shard_map/psum | solution.py:60
  286.8 13.1 %all_gather.66 = bf16[32,1024]{1,0:T(8,128)(2,1)S(1)} all-gather(bf16[32,256]{1,0:T(8,128)(2,1)S(1)} %fusion.112), channel_id=1, replica_groups=mesh['grp'=2,'row'=4,'col'=2,'vec'=2] {'row'}, dimensions={1}, use_global_device_ids=true | all-gather | bytes 81920 | tf_op jit(solution)/shard_map/all_gather | solution.py:56
  308.5 13.2 %all_gather.67 = bf16[32,1024]{1,0:T(8,128)(2,1)S(1)} all-gather(bf16[32,256]{1,0:T(8,128)(2,1)S(1)} %fusion.115), channel_id=1, replica_groups=mesh['grp'=2,'row'=4,'col'=2,'vec'=2] {'row'}, dimensions={1}, use_global_device_ids=true | all-gather | bytes 81920 | tf_op jit(solution)/shard_map/all_gather | solution.py:56
  330.8 13.3 %all_gather.68 = bf16[32,1024]{1,0:T(8,128)(2,1)S(1)} all-gather(bf16[32,256]{1,0:T(8,128)(2,1)S(1)} %fusion.117), channel_id=1, replica_groups=mesh['grp'=2,'row'=4,'col'=2,'vec'=2] {'row'}, dimensions={1}, use_global_device_ids=true | all-gather | bytes 81920 | tf_op jit(solution)/shard_map/all_gather | solution.py:56
  352.7 13.1 %all_gather.69 = bf16[32,1024]{1,0:T(8,128)(2,1)S(1)} all-gather(bf16[32,256]{1,0:T(8,128)(2,1)S(1)} %fusion.118), channel_id=1, replica_groups=mesh['grp'=2,'row'=4,'col'=2,'vec'=2] {'row'}, dimensions={1}, use_global_device_ids=true | all-gather | bytes 81920 | tf_op jit(solution)/shard_map/all_gather | solution.py:56
  375.0 13.1 %all_gather.70 = bf16[32,1024]{1,0:T(8,128)(2,1)S(1)} all-gather(bf16[32,256]{1,0:T(8,128)(2,1)S(1)} %subtract_convert_fusion.1), channel_id=1, replica_groups=mesh['grp'=2,'row'=4,'col'=2,'vec'=2] {'row'}, dimensions={1}, use_global_device_ids=true | all-gather | bytes 81920 | tf_op jit(solution)/shard_map/all_gather | solution.py:56
  398.7 15.9 %psum.151 = f32[64,64]{0,1:T(8,128)S(1)} all-reduce(f32[64,64]{0,1:T(8,128)S(1)} %fusion.139), channel_id=1, replica_groups=mesh['grp'=2,'row'=4,'col'=2,'vec'=2] {'row'}, use_global_device_ids=true, to_apply=%region_20.24 | all-reduce | flops 4096 | bytes 32768 | tf_op jit(solution)/shard_map/psum | solution.py:31
  (131 shorter events, 132.4 us)
Async XLA Ops:
  0.0 24.5 %copy-start = (bf16[2,16,128,128]{3,2,1,0:T(8,128)(2,1)S(1)}, bf16[2,16,128,128]{3,2,1,0:T(8,128)(2,1)}, u32[]{:S(2)}) copy-start(bf16[2,16,128,128]{3,2,1,0:T(8,128)(2,1)} %param.10) | copy-start | bytes 3145732
  0.0 9.9 %copy-start.1 = (f32[32,256]{1,0:T(8,128)S(1)}, f32[32,256]{1,0:T(8,128)}, u32[]{:S(2)}) copy-start(f32[32,256]{1,0:T(8,128)} %param.9) | copy-start | bytes 98308
  0.0 9.7 %copy-start.2 = (s32[2,32]{1,0:T(2,128)S(1)}, s32[2,32]{1,0:T(2,128)}, u32[]{:S(2)}) copy-start(s32[2,32]{1,0:T(2,128)} %param.11) | copy-start | bytes 772
where the time goes:
time: 429 us; the launch traced here: 428 us
  blocking collectives  379 us (88%)
  other arithmetic  28.4 us (7%)
  local copies, waits for them, and re-layouts  11 us (3%)
  matrix products  9.04 us (2%)
    all_gather x16, blocking collectives, apply_slots(): lax.all_gather(current.astype(jnp.bfloat16), 'row', axis=1, tiled=True)  212 us
    psum x16, blocking collectives, apply_slots(): total = lax.psum(product.astype(jnp.bfloat16), 'col').astype(jnp.float32)  123 us
    psum x2, blocking collectives, orthonormal(): gram = lax.psum(part_gram, 'row') / total_rows  34.8 us
    another operation x6, other arithmetic, orthonormal(): lower = jnp.linalg.cholesky(gram)  13 us
    another operation x4, other arithmetic, orthonormal(): solved = jax.scipy.linalg.solve_triangular(lower, both, lower=True)  11.1 us
    gather x16, local copies, waits for them, and re-layouts, apply_slots(): picked = jnp.take(blocks, local_pattern, axis=1)  9.65 us

commit v1 on v0

--- a/solution.py
+++ b/solution.py
@@ -9,6 +9,7 @@
 
 HALF_WIDTH = 2.0
 EPSILON = 1e-06
+DENSE_BUDGET = 16 * 1024 * 1024
 
 
 def row_scaling(square_sums, live_counts, block):
@@ -35,7 +36,7 @@
     return lax.dynamic_slice_in_dim(solved, lax.axis_index("vec") * width, width, 0)
 
 
-def per_device(start, tiles, pattern, counts):
+def distributed(start, tiles, pattern, counts):
     nb_dev = tiles.shape[0]
     block = tiles.shape[2]
     total_rows = nb_dev * block * lax.axis_size("row")
@@ -67,6 +68,105 @@
     return current
 
 
+def split_bf16(values):
+    high = values.astype(jnp.bfloat16)
+    low = (values - high.astype(jnp.float32)).astype(jnp.bfloat16)
+    return high, low
+
+
+def replicated(start, tiles, pattern, counts):
+    nb_dev, kb_dev, block = tiles.shape[0], tiles.shape[1], tiles.shape[2]
+    n_row, n_col = lax.axis_size("row"), lax.axis_size("col")
+    nblk = nb_dev * n_row
+    total_rows = nblk * block
+    share = block // n_col
+    vec_cols = start.shape[0]
+    cols = 2 * vec_cols
+    row_index = lax.axis_index("row")
+    col_index = lax.axis_index("col")
+    vec_index = lax.axis_index("vec")
+
+    own_tiles = lax.dynamic_index_in_dim(tiles, vec_index, 0, keepdims=False)
+    own_pattern = lax.dynamic_slice_in_dim(
+        lax.dynamic_index_in_dim(pattern, vec_index, 0, keepdims=False), col_index * kb_dev, kb_dev, 0
+    )
+    own_count = lax.dynamic_index_in_dim(counts, vec_index, 0, keepdims=False)
+    slot_ids = col_index * kb_dev + jnp.arange(kb_dev, dtype=jnp.int32)
+    live = slot_ids < own_count
+    position = (own_pattern % nb_dev) * n_row + own_pattern // nb_dev
+    onehot = (position[:, None] == jnp.arange(nblk, dtype=jnp.int32)) & live[:, None]
+    dense = jnp.einsum(
+        "kj,kmn->mjn", onehot.astype(jnp.bfloat16), own_tiles, preferred_element_type=jnp.float32
+    ).reshape(block, total_rows)
+    masked = own_tiles * live.astype(jnp.bfloat16)[:, None, None]
+    squares = jnp.einsum("kmn,kmn->m", masked, masked, preferred_element_type=jnp.float32)
+    squares = jnp.broadcast_to(squares[:, None], (block, 128))
+    partial = jnp.concatenate([dense, squares], axis=1)
+    summed = lax.psum_scatter(partial, "col", scatter_dimension=0, tiled=True)
+
+    entries = (own_count * block).astype(jnp.float32)
+    scale = lax.rsqrt(summed[:, total_rows] / entries + EPSILON) / jnp.sqrt(entries) / HALF_WIDTH
+    scale_hi, scale_lo = split_bf16(scale)
+
+    piece = start.reshape(vec_cols, nb_dev, block)
+    piece = lax.dynamic_slice_in_dim(piece, col_index * share, share, 2).reshape(vec_cols, nb_dev * share)
+    start_hi, start_lo = split_bf16(piece)
+    extra = jnp.concatenate([start_hi, start_lo], axis=0)
+    extra = jnp.concatenate(
+        [extra, scale_hi[:, None], scale_lo[:, None], jnp.zeros((share, 254 - nb_dev * share), jnp.bfloat16)],
+        axis=1,
+    )
+    packed = jnp.concatenate([summed[:, :total_rows].astype(jnp.bfloat16), extra], axis=1)
+    across = lax.all_gather(packed, ("row", "col"), axis=0, tiled=False)
+    whole = lax.all_gather(across, "vec", axis=0, tiled=False)
+    whole = whole.reshape(total_rows, total_rows + 256)
+    weights = whole[:, :total_rows]
+    scaling = (
+        whole[:, total_rows + nb_dev * share].astype(jnp.float32)
+        + whole[:, total_rows + nb_dev * share + 1].astype(jnp.float32)
+    )[None, :]
+    coded = whole[:, total_rows : total_rows + nb_dev * share].astype(jnp.float32)
+    coded = coded.reshape(2, n_row, n_col, 2, vec_cols, nb_dev, share)
+    coded = coded[:, :, :, 0] + coded[:, :, :, 1]
+    current = coded.transpose(0, 3, 4, 1, 2, 5).reshape(cols, total_rows)
+
+    def apply_dense(values):
+        product = jnp.einsum(
+            "cj,ij->ci", values.astype(jnp.bfloat16), weights, preferred_element_type=jnp.float32
+        )
+        return product * scaling
+
+    for outer in range(ITERS):
+        filtered = chebyshev(current, apply_dense)
+        gram = jnp.dot(filtered, filtered.T, precision=lax.Precision.HIGHEST) / total_rows
+        lower = jnp.linalg.cholesky(gram)
+        if outer < ITERS - 1:
+            current = jax.scipy.linalg.solve_triangular(lower, filtered, lower=True)
+        else:
+            mine = filtered.reshape(cols, nb_dev, n_row, block)
+            mine = lax.dynamic_index_in_dim(mine, row_index, 2, keepdims=False).reshape(cols, nb_dev * block)
+            solved = jax.scipy.linalg.solve_triangular(lower, mine, lower=True)
+            current = lax.dynamic_slice_in_dim(solved, vec_index * vec_cols, vec_cols, 0)
+    return current
+
+
+def per_device(start, tiles, pattern, counts):
+    total_rows = tiles.shape[0] * tiles.shape[2] * lax.axis_size("row")
+    n_col, n_vec = lax.axis_size("col"), lax.axis_size("vec")
+    block = tiles.shape[2]
+    fits = (
+        total_rows * total_rows * 2 <= DENSE_BUDGET
+        and n_vec == 2
+        and tiles.shape[0] == n_vec
+        and block % n_col == 0
+        and block // n_col == 2 * start.shape[0]
+        and tiles.shape[0] * (block // n_col) <= 254
+    )
+    if fits:
+        return replicated(start, tiles, pattern, counts)
+    return distributed(start, tiles, pattern, counts)
+
+
 def solution(mesh):
     in_specs = (
         P("vec", ("grp", "row")),

time: 429 us -> 145 us (0.34)
  blocking collectives: 379 us -> 0 us
  waiting for transfers between devices: 0 us -> 70.8 us
  between operations: 0.46 us -> 14.1 us
  matrix products: 9.04 us -> 21.7 us
    all_gather x18 -> x0, blocking collectives: 215 us -> none  [the longest x16 212 us: apply_slots(): lax.all_gather(current.astype(jnp.bfloat16), 'row', axis=1, tiled=True)]
    psum x19 -> x0, blocking collectives: 164 us -> none  [the longest x16 123 us: apply_slots(): total = lax.psum(product.astype(jnp.bfloat16), 'col').astype(jnp.float32)]
    all_gather x0 -> x2, waiting for transfers between devices: none -> 53.6 us  [the longest x1 42 us: replicated(): across = lax.all_gather(packed, ('row', 'col'), axis=0, tiled=False)]
    unnamed x0 -> x4, waiting for transfers between devices: none -> 17.2 us
    dot_general x18 -> x17, matrix products: 8.5 us -> 21 us  [the longest x14 19.9 us: apply_dense(): jnp.einsum('cj,ij->ci', values.astype(jnp.bfloat16), weights, preferred_e...]
    gather x16 -> x0, local copies, waits for them, and re-layouts: 9.65 us -> none  [apply_slots(): picked = jnp.take(blocks, local_pattern, axis=1)]
  transfers between devices with their start and end apart: 0 -> 3, of which waited for: 0 -> 3; matrix products, arithmetic and copies ran while one was open for 0% -> 0% of each run, Pallas kernels for 0% -> 0%
where the time goes in v1:
time: 145 us
  waiting for transfers between devices  70.8 us (49%)
  other arithmetic  29.6 us (20%)
  matrix products  21.7 us (15%)
  between operations  14.1 us (10%)
  local copies, waits for them, and re-layouts  8.63 us (6%)
    all_gather x1, waiting for transfers between devices, replicated(): across = lax.all_gather(packed, ('row', 'col'), axis=0, tiled=False)  42 us
    dot_general x14, matrix products, apply_dense(): jnp.einsum('cj,ij->ci', values.astype(jnp.bfloat16), weights, preferred_e...  19.9 us
    unnamed x4, waiting for transfers between devices  17.2 us
    another operation x6, other arithmetic, replicated(): lower = jnp.linalg.cholesky(gram)  13 us
    all_gather x1, waiting for transfers between devices, replicated(): whole = lax.all_gather(across, 'vec', axis=0, tiled=False)  11.6 us
    another operation x2, other arithmetic, replicated(): current = jax.scipy.linalg.solve_triangular(lower, filtered, lower=True)  5.55 us
    another operation x2, other arithmetic, replicated(): solved = jax.scipy.linalg.solve_triangular(lower, mine, lower=True)  5.55 us
  transfers between devices with their start and end apart: 3, of which 3 were waited for; matrix products, arithmetic and copies ran while one was open for 0% of the time, Pallas kernels for 0%

profile of v1, /device:TPU:0, one launch (start us, length us, event | category | flops | bytes accessed | tf_op | source)
XLA Modules:
  0.0 145.1 jit_solution(6267587869377987998)
XLA Ops:
  6.5 1.3 dynamic_slice.28
  8.6 0.8 fusion.74
  10.0 1.3 fusion.30
  11.3 1.0 copy.67
  13.4 17.2 %reduce-scatter.4.cloned.1.call-done = f32[64,1152]{1,0:T(8,128)} async-done(((f32[128,1152]{1,0:T(8,128)}), f32[64,1152]{1,0:T(8,128)}) %reduce-scatter.4.cloned.1.call-update) | async-done | bytes 294928
  30.5 0.8 slice.50
  31.4 1.0 slice.49
  33.0 0.8 copy.51
  34.0 42.0 %all-gather.5.cloned.1.call-done = bf16[512,1280]{1,0:T(8,128)(2,1)} async-done(((bf16[64,1280]{1,0:T(8,128)(2,1)}), bf16[512,1280]{1,0:T(8,128)(2,1)}) %all-gather.5.cloned.1.call-update) | async-done | bytes 1310736 | tf_op jit(solution)/shard_map/all_gather | solution.py:120
  76.1 11.6 %all-gather.7.cloned.1.call-done = bf16[16,64,1280]{2,1,0:T(8,128)(2,1)} async-done(((bf16[8,64,1280]{2,1,0:T(8,128)(2,1)}), bf16[16,64,1280]{2,1,0:T(8,128)(2,1)}) %all-gather.7.cloned.1.call-update) | async-done | bytes 2621456 | tf_op jit(solution)/shard_map/all_gather | solution.py:121
  87.7 1.0 slice_convert_fusion
  88.7 1.3 add_reduce_fusion
  91.9 2.5 %convolution_multiply_fusion.15 = f32[64,1024]{1,0:T(8,128)S(1)} fusion(f32[1024]{0:T(1024)S(1)} %add_reduce_fusion, f32[64,1024]{1,0:T(8,128)S(1)} %reshape.125, bf16[1024,1280]{1,0:T(8,128)(2,1)} %bitcast.76), kind=kOutput, calls=%fused_computation.44 | convolution fusion | flops 134348800 | bytes 2625536 | tf_op jit(solution)/shard_map/cj,ij->ci/dot_general | solution.py:134
  95.9 0.8 fusion.23
  96.7 0.8 fusion.21
  97.4 0.8 fusion.19
  98.2 3.6 %fusion.15 = f32[64,1024]{1,0:T(8,128)S(1)} fusion(f32[64,1024]{1,0:T(8,128)S(1)} %fusion.19, f32[64,1024]{1,0:T(8,128)S(1)} %fusion.21, f32[1024]{0:T(1024)S(1)} %add_reduce_fusion, bf16[1024,1280]{1,0:T(8,128)(2,1)} %bitcast.77), kind=kOutput, calls=%fused_computation.25 | convolution fusion | flops 268959744 | bytes 5251072 | tf_op jit(solution)/shard_map/cj,ij->ci/dot_general | solution.py:134
  102.3 5.8 %cholesky.44 = f32[64,64]{1,0:T(8,128)S(1)} custom-call(f32[64,64]{1,0:T(8,128)S(1)} %fusion.65), custom_call_target="Cholesky" | custom-call | tf_op jit(solution)/shard_map/jit(cholesky)/cholesky | solution.py:142
  109.5 4.9 %custom-call.10 = f32[1,64,64]{1,2,0:T(8,128)S(1)} custom-call(f32[1,64,64]{2,1,0:T(8,128)S(1)} %fusion.59), custom_call_target="InvertDiagBlocksLowerTriangular" | custom-call | tf_op jit(solution)/shard_map/jit(_solve_triangular)/triangular_solve | solution.py:144
  114.8 2.6 %convolution_multiply_fusion.7 = f32[64,1024]{1,0:T(8,128)S(1)} fusion(f32[64,1024]{1,0:T(8,128)S(1)} %fusion.63, f32[1024]{0:T(1024)S(1)} %add_reduce_fusion, bf16[1024,1280]{1,0:T(8,128)(2,1)} %bitcast.78), kind=kOutput, calls=%fused_computation.22 | convolution fusion | flops 134348800 | bytes 2625536 | tf_op jit(solution)/shard_map/cj,ij->ci/dot_general | solution.py:134
  118.9 0.8 fusion.9
  121.2 3.6 %fusion.1 = f32[64,1024]{1,0:T(8,128)S(1)} fusion(f32[64,1024]{1,0:T(8,128)S(1)} %fusion.5, f32[64,1024]{1,0:T(8,128)S(1)} %fusion.7, f32[1024]{0:T(1024)S(1)} %add_reduce_fusion, bf16[1024,1280]{1,0:T(8,128)(2,1)} %bitcast.79), kind=kOutput, calls=%fused_computation.3 | convolution fusion | flops 268959744 | bytes 5251072 | tf_op jit(solution)/shard_map/cj,ij->ci/dot_general | solution.py:134
  125.4 5.8 %cholesky.55 = f32[64,64]{1,0:T(8,128)S(1)} custom-call(f32[64,64]{1,0:T(8,128)S(1)} %fusion.62), custom_call_target="Cholesky" | custom-call | tf_op jit(solution)/shard_map/jit(cholesky)/cholesky | solution.py:142
  132.6 4.9 %custom-call.11 = f32[1,64,64]{1,2,0:T(8,128)S(1)} custom-call(f32[1,64,64]{2,1,0:T(8,128)S(1)} %fusion.60), custom_call_target="InvertDiagBlocksLowerTriangular" | custom-call | tf_op jit(solution)/shard_map/jit(_solve_triangular)/triangular_solve | solution.py:148
  (56 shorter events, 14.1 us)
Async XLA Ops:
  6.5 2.0 %copy-start = (bf16[2,16,128,128]{3,2,1,0:T(8,128)(2,1)S(1)}, bf16[2,16,128,128]{3,2,1,0:T(8,128)(2,1)}, u32[]{:S(2)}) copy-start(bf16[2,16,128,128]{3,2,1,0:T(8,128)(2,1)} %param.6) | copy-start | bytes 3145732
  6.5 24.0 %reduce-scatter.4.cloned.1.call-start = ((), (), s32[]{:S(2)}) async-start(), calls=%async_computation.3 | async-start | bytes 884736
  9.4 3.8 %copy-start.3 = (f32[32,256]{1,0:T(8,128)S(1)}, f32[32,256]{1,0:T(8,128)}, u32[]{:S(2)}) copy-start(f32[32,256]{1,0:T(8,128)} %param.5) | copy-start | bytes 98308
  12.4 63.6 %all-gather.5.cloned.1.call-start = ((), (), s32[]{:S(2)}) async-start(), calls=%async_computation.1 | async-start | bytes 1474560 | tf_op jit(solution)/shard_map/all_gather | solution.py:120
  33.8 53.9 %all-gather.7.cloned.1.call-start = ((), (), s32[]{:S(2)}) async-start(), calls=%async_computation.2 | async-start | bytes 3932160 | tf_op jit(solution)/shard_map/all_gather | solution.py:121
  91.9 2.5 %copy-start.1 = (bf16[16,64,1280]{2,1,0:T(8,128)(2,1)S(1)}, bf16[16,64,1280]{2,1,0:T(8,128)(2,1)}, u32[]{:S(2)}) copy-start(bf16[16,64,1280]{2,1,0:T(8,128)(2,1)} %all-gather.7.cloned.1.call-done) | copy-start | bytes 7864324
  114.4 3.0 %copy-start.2 = (bf16[16,64,1280]{2,1,0:T(8,128)(2,1)S(1)}, bf16[16,64,1280]{2,1,0:T(8,128)(2,1)}, u32[]{:S(2)}) copy-start(bf16[16,64,1280]{2,1,0:T(8,128)(2,1)} %all-gather.7.cloned.1.call-done) | copy-start | bytes 7864324
Sparse Core Ops, SparseCore 0:
  12.5 17.9 reduce-scatter.3
  33.9 42.0 all-gather.4
  77.6 10.0 all-gather.6

commit v2 on v1

--- a/solution.py
+++ b/solution.py
@@ -102,7 +102,11 @@
     squares = jnp.einsum("kmn,kmn->m", masked, masked, preferred_element_type=jnp.float32)
     squares = jnp.broadcast_to(squares[:, None], (block, 128))
     partial = jnp.concatenate([dense, squares], axis=1)
-    summed = lax.psum_scatter(partial, "col", scatter_dimension=0, tiled=True)
+    chunks = partial.reshape(n_col, share, total_rows + 128)
+    summed = lax.dynamic_index_in_dim(chunks, col_index, 0, keepdims=False)
+    for shift in range(1, n_col):
+        sent = lax.dynamic_index_in_dim(chunks, (col_index + shift) % n_col, 0, keepdims=False)
+        summed = summed + lax.ppermute(sent, "col", [(i, (i + shift) % n_col) for i in range(n_col)])
 
     entries = (own_count * block).astype(jnp.float32)
     scale = lax.rsqrt(summed[:, total_rows] / entries + EPSILON) / jnp.sqrt(entries) / HALF_WIDTH
@@ -113,19 +117,27 @@
     start_hi, start_lo = split_bf16(piece)
     extra = jnp.concatenate([start_hi, start_lo], axis=0)
     extra = jnp.concatenate(
-        [extra, scale_hi[:, None], scale_lo[:, None], jnp.zeros((share, 254 - nb_dev * share), jnp.bfloat16)],
-        axis=1,
+        [extra, scale_hi[:, None], scale_lo[:, None], jnp.zeros((share, 126), jnp.bfloat16)], axis=1
     )
-    packed = jnp.concatenate([summed[:, :total_rows].astype(jnp.bfloat16), extra], axis=1)
-    across = lax.all_gather(packed, ("row", "col"), axis=0, tiled=False)
-    whole = lax.all_gather(across, "vec", axis=0, tiled=False)
-    whole = whole.reshape(total_rows, total_rows + 256)
-    weights = whole[:, :total_rows]
+    rows_bf16 = summed[:, :total_rows].astype(jnp.bfloat16)
+
+    n_rc = n_row * n_col
+    rc_index = row_index * n_col + col_index
+    received = [(rows_bf16, extra)]
+    for shift in range(1, n_rc):
+        perm = [(i, (i + shift) % n_rc) for i in range(n_rc)]
+        received.append(lax.ppermute((rows_bf16, extra), ("row", "col"), perm))
+    order = (rc_index - jnp.arange(n_rc, dtype=jnp.int32)) % n_rc
+    half_rows = jnp.take(jnp.stack([r[0] for r in received]), order, axis=0)
+    half_extra = jnp.take(jnp.stack([r[1] for r in received]), order, axis=0)
+    other_rows, other_extra = lax.ppermute((half_rows, half_extra), "vec", [(0, 1), (1, 0)])
+    pair = (jnp.arange(2, dtype=jnp.int32) - vec_index) % 2
+    weights = jnp.take(jnp.stack([half_rows, other_rows]), pair, axis=0).reshape(total_rows, total_rows)
+    extras = jnp.take(jnp.stack([half_extra, other_extra]), pair, axis=0).reshape(total_rows, 256)
     scaling = (
-        whole[:, total_rows + nb_dev * share].astype(jnp.float32)
-        + whole[:, total_rows + nb_dev * share + 1].astype(jnp.float32)
+        extras[:, nb_dev * share].astype(jnp.float32) + extras[:, nb_dev * share + 1].astype(jnp.float32)
     )[None, :]
-    coded = whole[:, total_rows : total_rows + nb_dev * share].astype(jnp.float32)
+    coded = extras[:, : nb_dev * share].astype(jnp.float32)
     coded = coded.reshape(2, n_row, n_col, 2, vec_cols, nb_dev, share)
     coded = coded[:, :, :, 0] + coded[:, :, :, 1]
     current = coded.transpose(0, 3, 4, 1, 2, 5).reshape(cols, total_rows)
@@ -160,7 +172,7 @@
         and tiles.shape[0] == n_vec
         and block % n_col == 0
         and block // n_col == 2 * start.shape[0]
-        and tiles.shape[0] * (block // n_col) <= 254
+        and tiles.shape[0] * (block // n_col) <= 128
     )
     if fits:
         return replicated(start, tiles, pattern, counts)

time: 145 us -> 184 us (1.27)
  the two profiles are of different devices: /device:TPU:0 before, /device:TPU:19 now
where the time goes in v2:
time: 184 us; the launch traced here: 183 us
  starting transfers between devices  51 us (28%)
  other arithmetic  43.9 us (24%)
  local copies, waits for them, and re-layouts  40.9 us (22%)
  waiting for transfers between devices  26.9 us (15%)
  matrix products  19.1 us (10%)
    ppermute x14, starting transfers between devices, replicated(): received.append(lax.ppermute((rows_bf16, extra), ('row', 'col'), perm))  48.6 us
    ppermute x14, waiting for transfers between devices, replicated(): received.append(lax.ppermute((rows_bf16, extra), ('row', 'col'), perm))  20.6 us
    dot_general x14, matrix products, apply_dense(): jnp.einsum('cj,ij->ci', values.astype(jnp.bfloat16), weights, preferred_e...  17.3 us
    another operation x6, other arithmetic, replicated(): lower = jnp.linalg.cholesky(gram)  13 us
    gather x2, local copies, waits for them, and re-layouts, replicated(): jnp.take(jnp.stack([half_rows, other_rows]), pair, axis=0)  10 us
    unnamed x27, local copies, waits for them, and re-layouts  8.25 us
    ppermute x1, waiting for transfers between devices, replicated(): lax.ppermute(sent, 'col', [(i, (i + shift) % n_col) for i in range(n_col)])  6.34 us
    another operation x2, other arithmetic, replicated(): current = jax.scipy.linalg.solve_triangular(lower, filtered, lower=True)  5.55 us
  transfers between devices with their start and end apart: 17, of which 5 were waited for; matrix products, arithmetic and copies ran while one was open for 13% of the time, Pallas kernels for 0%

profile of v2, /device:TPU:19, one launch (start us, length us, event | category | flops | bytes accessed | tf_op | source)
XLA Modules:
  0.0 182.9 jit_solution(7046526568558240360)
XLA Ops:
  6.9 6.3 %collective-permute-done = f32[64,1152]{1,0:T(8,128)S(1)} collective-permute-done((f32[64,1152]{1,0:T(8,128)S(1)}, f32[64,1152]{1,0:T(8,128)S(1)}, u32[]{:S(2)}, u32[]{:S(2)}) %collective-permute-start) | collective-permute-done | bytes 294944 | tf_op jit(solution)/shard_map/ppermute | solution.py:109
  14.3 3.1 %collective-permute-start.4 = (bf16[64,256]{1,0:T(8,128)(2,1)S(1)}, bf16[64,256]{1,0:T(8,128)(2,1)S(1)}, u32[]{:S(2)}, u32[]{:S(2)}) collective-permute-start(bf16[64,256]{1,0:T(8,128)(2,1)S(1)} %get-tuple-element.11), channel_id=1, source_target_pairs={{0,8},{2,10},{4,12},{6,14},{8,0},{10,2},{12,4},{14,6},{1,9},{3,11}... | collective-permute-start | bytes 98312 | tf_op jit(solution)/shard_map/ppermute | solution.py:129
  17.4 3.1 %collective-permute-start.3 = (bf16[64,256]{1,0:T(8,128)(2,1)S(1)}, bf16[64,256]{1,0:T(8,128)(2,1)S(1)}, u32[]{:S(2)}, u32[]{:S(2)}) collective-permute-start(bf16[64,256]{1,0:T(8,128)(2,1)S(1)} %get-tuple-element.11), channel_id=1, source_target_pairs={{0,6},{2,8},{4,10},{6,12},{8,14},{10,0},{12,2},{14,4},{1,7},{3,9},... | collective-permute-start | bytes 98312 | tf_op jit(solution)/shard_map/ppermute | solution.py:129
  23.3 2.8 %collective-permute-done.2 = bf16[64,256]{1,0:T(8,128)(2,1)S(1)} collective-permute-done((bf16[64,256]{1,0:T(8,128)(2,1)S(1)}, bf16[64,256]{1,0:T(8,128)(2,1)S(1)}, u32[]{:S(2)}, u32[]{:S(2)}) %collective-permute-start.2) | collective-permute-done | bytes 32800 | tf_op jit(solution)/shard_map/ppermute | solution.py:129
  27.0 2.5 %collective-permute-start.13 = (bf16[64,1024]{0,1:T(8,128)(2,1)S(1)}, bf16[64,1024]{0,1:T(8,128)(2,1)S(1)}, u32[]{:S(2)}, u32[]{:S(2)}) collective-permute-start(bf16[64,1024]{0,1:T(8,128)(2,1)S(1)} %get-tuple-element.9), channel_id=1, source_target_pairs={{0,10},{2,12},{4,14},{6,0},{8,2},{10,4},{12,6},{14,8},{1,11},{3,13... | collective-permute-start | bytes 393224 | tf_op jit(solution)/shard_map/ppermute | solution.py:129
  31.3 3.2 %collective-permute-start.11 = (bf16[64,1024]{0,1:T(8,128)(2,1)S(1)}, bf16[64,1024]{0,1:T(8,128)(2,1)S(1)}, u32[]{:S(2)}, u32[]{:S(2)}) collective-permute-start(bf16[64,1024]{0,1:T(8,128)(2,1)S(1)} %get-tuple-element.9), channel_id=1, source_target_pairs={{0,6},{2,8},{4,10},{6,12},{8,14},{10,0},{12,2},{14,4},{1,7},{3,9},... | collective-permute-start | bytes 393224 | tf_op jit(solution)/shard_map/ppermute | solution.py:129
  37.2 9.1 %collective-permute-done.9 = bf16[64,1024]{0,1:T(8,128)(2,1)} collective-permute-done((bf16[64,1024]{0,1:T(8,128)(2,1)S(1)}, bf16[64,1024]{0,1:T(8,128)(2,1)}, u32[]{:S(2)}, u32[]{:S(2)}) %collective-permute-start.9) | collective-permute-done | bytes 131104 | tf_op jit(solution)/shard_map/ppermute | solution.py:129
  46.4 30.3 %collective-permute-start.14 = (bf16[64,1024]{0,1:T(8,128)(2,1)S(1)}, bf16[64,1024]{0,1:T(8,128)(2,1)S(1)}, u32[]{:S(2)}, u32[]{:S(2)}) collective-permute-start(bf16[64,1024]{0,1:T(8,128)(2,1)S(1)} %get-tuple-element.9), channel_id=1, source_target_pairs={{0,12},{2,14},{4,0},{6,2},{8,4},{10,6},{12,8},{14,10},{1,13},{3,15... | collective-permute-start | bytes 393224 | tf_op jit(solution)/shard_map/ppermute | solution.py:129
  84.7 6.7 %collective-permute-done.15 = bf16[64,1024]{0,1:T(8,128)(2,1)S(1)} collective-permute-done((bf16[64,1024]{0,1:T(8,128)(2,1)S(1)}, bf16[64,1024]{0,1:T(8,128)(2,1)S(1)}, u32[]{:S(2)}, u32[]{:S(2)}) %collective-permute-start.15) | collective-permute-done | bytes 131104 | tf_op jit(solution)/shard_map/ppermute | solution.py:129
  92.1 2.5 %gather_fusion.2 = bf16[8,64,1024]{1,2,0:T(8,128)(2,1)S(1)} fusion(bf16[8,64,1024]{1,2,0:T(8,128)(2,1)} %bitcast_dynamic-update-slice_fusion, s32[1024]{0:T(1024)S(1)} %pad_clamp_fusion.1), kind=kCustom, calls=%fused_computation.2 | custom fusion | bytes 2097184 | tf_op jit(solution)/shard_map/jit(_take)/gather | solution.py:131
  96.2 2.7 %copy.53 = bf16[8,64,1024]{2,1,0:T(8,128)(2,1)} copy(bf16[8,64,1024]{1,2,0:T(8,128)(2,1)} %broadcast_select_fusion.1) | data formatting | bytes 2097152 | tf_op jit(solution)/shard_map/jit(_take)/select_n | solution.py:131
  110.2 2.7 %copy.54 = bf16[8,64,1024]{1,2,0:T(8,128)(2,1)} copy(bf16[8,64,1024]{2,1,0:T(8,128)(2,1)} %collective-permute-done.16) | data formatting | bytes 2097152 | tf_op jit(solution)/shard_map/ppermute | solution.py:133
  113.0 4.5 %pad_maximum_fusion = bf16[2,8,64,1024]{2,3,1,0:T(8,128)(2,1)} fusion(bf16[1,8,64,1024]{2,3,1,0:T(8,128)(2,1)} %bitcast.134, bf16[1,8,64,1024]{2,3,1,0:T(8,128)(2,1)S(1)} %copy-done.2), kind=kLoop, calls=%fused_computation.4 | loop fusion | flops 1048576 | bytes 4194304 | tf_op jit(solution)/shard_map/stack | solution.py:135
  117.5 5.2 %gather_fusion.3 = bf16[2,8,64,1024]{2,3,1,0:T(8,128)(2,1)} fusion(bf16[2,8,64,1024]{2,3,1,0:T(8,128)(2,1)} %pad_maximum_fusion, s32[1024]{0:T(1024)S(1)} %pad_clamp_fusion), kind=kCustom, calls=%fused_computation.3 | custom fusion | bytes 4194312 | tf_op jit(solution)/shard_map/jit(_take)/gather | solution.py:135
  122.7 4.8 %copy.56 = bf16[2,8,64,1024]{3,2,1,0:T(8,128)(2,1)} copy(bf16[2,8,64,1024]{2,3,1,0:T(8,128)(2,1)} %gather_fusion.3) | data formatting | bytes 4194304 | tf_op jit(solution)/shard_map/jit(_take)/gather | solution.py:135
  127.5 4.8 %broadcast_select_fusion = bf16[2,8,64,1024]{2,3,1,0:T(8,128)(2,1)} fusion(bf16[2,8,64,1024]{2,3,1,0:T(8,128)(2,1)} %gather_fusion.3, pred[2]{0:T(512)(128)(4,1)S(1)} %compare_and_fusion.1), kind=kLoop, calls=%fused_computation.5 | loop fusion | flops 1048576 | bytes 4194306 | tf_op jit(solution)/shard_map/jit(_take)/select_n | solution.py:135
  132.6 4.8 %copy.55 = bf16[2,8,64,1024]{3,2,1,0:T(8,128)(2,1)} copy(bf16[2,8,64,1024]{2,3,1,0:T(8,128)(2,1)} %broadcast_select_fusion) | data formatting | bytes 4194304 | tf_op jit(solution)/shard_map/jit(_take)/select_n | solution.py:135
  137.4 2.4 %convolution_multiply_fusion.15 = f32[64,1024]{1,0:T(8,128)S(1)} fusion(bf16[64,1024]{1,0:T(8,128)(2,1)S(1)} %convert_element_type.111, bf16[1024,1024]{1,0:T(8,128)(2,1)} %bitcast.133, f32[1024]{0:T(1024)S(1)} %add_reduce_fusion), kind=kOutput, calls=%fused_computation.57 | convolution fusion | flops 134283264 | bytes 2494464 | tf_op jit(solution)/shard_map/cj,ij->ci/dot_general | solution.py:146
  145.0 2.5 %fusion.15 = f32[64,1024]{1,0:T(8,128)S(1)} fusion(f32[64,1024]{1,0:T(8,128)} %fusion.19, bf16[1024,1024]{1,0:T(8,128)(2,1)S(1)} %bitcast_select_fusion, f32[64,1024]{1,0:T(8,128)} %copy-done.5, f32[1024]{0:T(1024)S(1)} %add_reduce_fusion), kind=kOutput, calls=%fused_computation.38 | convolution fusion | flops 268959744 | bytes 2887680 | tf_op jit(solution)/shard_map/cj,ij->ci/dot_general | solution.py:146
  148.0 5.8 %cholesky.44 = f32[64,64]{1,0:T(8,128)S(1)} custom-call(f32[64,64]{1,0:T(8,128)S(1)} %fusion.67), custom_call_target="Cholesky" | custom-call | tf_op jit(solution)/shard_map/jit(cholesky)/cholesky | solution.py:154
  155.2 4.9 %custom-call.10 = f32[1,64,64]{1,2,0:T(8,128)S(1)} custom-call(f32[1,64,64]{2,1,0:T(8,128)S(1)} %fusion.61), custom_call_target="InvertDiagBlocksLowerTriangular" | custom-call | tf_op jit(solution)/shard_map/jit(_solve_triangular)/triangular_solve | solution.py:156
  166.6 2.5 %fusion.1 = f32[64,1024]{1,0:T(8,128)S(1)} fusion(f32[64,1024]{1,0:T(8,128)} %fusion.5, bf16[1024,1024]{1,0:T(8,128)(2,1)S(1)} %bitcast_select_fusion, f32[64,1024]{1,0:T(8,128)} %copy-done.4, f32[1024]{0:T(1024)S(1)} %add_reduce_fusion), kind=kOutput, calls=%fused_computation.16 | convolution fusion | flops 268959744 | bytes 2887680 | tf_op jit(solution)/shard_map/cj,ij->ci/dot_general | solution.py:146
  169.7 5.8 %cholesky.55 = f32[64,64]{1,0:T(8,128)S(1)} custom-call(f32[64,64]{1,0:T(8,128)S(1)} %fusion.64), custom_call_target="Cholesky" | custom-call | tf_op jit(solution)/shard_map/jit(cholesky)/cholesky | solution.py:154
  176.9 4.9 %custom-call.11 = f32[1,64,64]{1,2,0:T(8,128)S(1)} custom-call(f32[1,64,64]{2,1,0:T(8,128)S(1)} %fusion.62), custom_call_target="InvertDiagBlocksLowerTriangular" | custom-call | tf_op jit(solution)/shard_map/jit(_solve_triangular)/triangular_solve | solution.py:160
  (132 shorter events, 53.8 us)
Async XLA Ops:
  0.0 2.0 %copy-start = (bf16[2,16,128,128]{3,2,1,0:T(8,128)(2,1)S(1)}, bf16[2,16,128,128]{3,2,1,0:T(8,128)(2,1)}, u32[]{:S(2)}) copy-start(bf16[2,16,128,128]{3,2,1,0:T(8,128)(2,1)} %param.6) | copy-start | bytes 3145732
  4.6 1.9 %copy-start.6 = (f32[32,256]{1,0:T(8,128)S(1)}, f32[32,256]{1,0:T(8,128)}, u32[]{:S(2)}) copy-start(f32[32,256]{1,0:T(8,128)} %param.5) | copy-start | bytes 98308
  5.3 7.9 %collective-permute-start = (f32[64,1152]{1,0:T(8,128)S(1)}, f32[64,1152]{1,0:T(8,128)S(1)}, u32[]{:S(2)}, u32[]{:S(2)}) collective-permute-start(f32[64,1152]{1,0:T(8,128)S(1)} %bitcast.135), channel_id=1, source_target_pairs={{0,2},{2,0},{1,3},{3,1},{4,6},{6,4},{5,7},{7,5},{8,10},{10,8},{9,1... | collective-permute-start | bytes 884744 | tf_op jit(solution)/shard_map/ppermute | solution.py:109
  13.9 20.6 %collective-permute-start.6 = (bf16[64,256]{1,0:T(8,128)(2,1)S(1)}, bf16[64,256]{1,0:T(8,128)(2,1)S(1)}, u32[]{:S(2)}, u32[]{:S(2)}) collective-permute-start(bf16[64,256]{1,0:T(8,128)(2,1)S(1)} %get-tuple-element.11), channel_id=1, source_target_pairs={{0,12},{2,14},{4,0},{6,2},{8,4},{10,6},{12,8},{14,10},{1,13},{3,15... | collective-permute-start | bytes 98312 | tf_op jit(solution)/shard_map/ppermute | solution.py:129
  14.1 17.2 %collective-permute-start.5 = (bf16[64,256]{1,0:T(8,128)(2,1)S(1)}, bf16[64,256]{1,0:T(8,128)(2,1)S(1)}, u32[]{:S(2)}, u32[]{:S(2)}) collective-permute-start(bf16[64,256]{1,0:T(8,128)(2,1)S(1)} %get-tuple-element.11), channel_id=1, source_target_pairs={{0,10},{2,12},{4,14},{6,0},{8,2},{10,4},{12,6},{14,8},{1,11},{3,13... | collective-permute-start | bytes 98312 | tf_op jit(solution)/shard_map/ppermute | solution.py:129
  14.3 15.2 %collective-permute-start.4 = (bf16[64,256]{1,0:T(8,128)(2,1)S(1)}, bf16[64,256]{1,0:T(8,128)(2,1)S(1)}, u32[]{:S(2)}, u32[]{:S(2)}) collective-permute-start(bf16[64,256]{1,0:T(8,128)(2,1)S(1)} %get-tuple-element.11), channel_id=1, source_target_pairs={{0,8},{2,10},{4,12},{6,14},{8,0},{10,2},{12,4},{14,6},{1,9},{3,11}... | collective-permute-start | bytes 98312 | tf_op jit(solution)/shard_map/ppermute | solution.py:129
  17.4 9.6 %collective-permute-start.3 = (bf16[64,256]{1,0:T(8,128)(2,1)S(1)}, bf16[64,256]{1,0:T(8,128)(2,1)S(1)}, u32[]{:S(2)}, u32[]{:S(2)}) collective-permute-start(bf16[64,256]{1,0:T(8,128)(2,1)S(1)} %get-tuple-element.11), channel_id=1, source_target_pairs={{0,6},{2,8},{4,10},{6,12},{8,14},{10,0},{12,2},{14,4},{1,7},{3,9},... | collective-permute-start | bytes 98312 | tf_op jit(solution)/shard_map/ppermute | solution.py:129
  20.5 2.8 %collective-permute-start.1 = (bf16[64,256]{1,0:T(8,128)(2,1)S(1)}, bf16[64,256]{1,0:T(8,128)(2,1)S(1)}, u32[]{:S(2)}, u32[]{:S(2)}) collective-permute-start(bf16[64,256]{1,0:T(8,128)(2,1)S(1)} %get-tuple-element.11), channel_id=1, source_target_pairs={{0,2},{2,4},{4,6},{6,8},{8,10},{10,12},{12,14},{14,0},{1,3},{3,5},... | collective-permute-start | bytes 98312 | tf_op jit(solution)/shard_map/ppermute | solution.py:129
  23.3 2.8 %collective-permute-start.2 = (bf16[64,256]{1,0:T(8,128)(2,1)S(1)}, bf16[64,256]{1,0:T(8,128)(2,1)S(1)}, u32[]{:S(2)}, u32[]{:S(2)}) collective-permute-start(bf16[64,256]{1,0:T(8,128)(2,1)S(1)} %get-tuple-element.11), channel_id=1, source_target_pairs={{0,4},{2,6},{4,8},{6,10},{8,12},{10,14},{12,0},{14,2},{1,5},{3,7},... | collective-permute-start | bytes 98312 | tf_op jit(solution)/shard_map/ppermute | solution.py:129
  26.1 8.4 %collective-permute-start.7 = (bf16[64,256]{1,0:T(8,128)(2,1)S(1)}, bf16[64,256]{1,0:T(8,128)(2,1)S(1)}, u32[]{:S(2)}, u32[]{:S(2)}) collective-permute-start(bf16[64,256]{1,0:T(8,128)(2,1)S(1)} %get-tuple-element.11), channel_id=1, source_target_pairs={{0,14},{2,0},{4,2},{6,4},{8,6},{10,8},{12,10},{14,12},{1,15},{3,1}... | collective-permute-start | bytes 98312 | tf_op jit(solution)/shard_map/ppermute | solution.py:129
  27.0 56.3 %collective-permute-start.13 = (bf16[64,1024]{0,1:T(8,128)(2,1)S(1)}, bf16[64,1024]{0,1:T(8,128)(2,1)S(1)}, u32[]{:S(2)}, u32[]{:S(2)}) collective-permute-start(bf16[64,1024]{0,1:T(8,128)(2,1)S(1)} %get-tuple-element.9), channel_id=1, source_target_pairs={{0,10},{2,12},{4,14},{6,0},{8,2},{10,4},{12,6},{14,8},{1,11},{3,13... | collective-permute-start | bytes 393224 | tf_op jit(solution)/shard_map/ppermute | solution.py:129
  29.5 53.0 %collective-permute-start.12 = (bf16[64,1024]{0,1:T(8,128)(2,1)S(1)}, bf16[64,1024]{0,1:T(8,128)(2,1)S(1)}, u32[]{:S(2)}, u32[]{:S(2)}) collective-permute-start(bf16[64,1024]{0,1:T(8,128)(2,1)S(1)} %get-tuple-element.9), channel_id=1, source_target_pairs={{0,8},{2,10},{4,12},{6,14},{8,0},{10,2},{12,4},{14,6},{1,9},{3,11}... | collective-permute-start | bytes 393224 | tf_op jit(solution)/shard_map/ppermute | solution.py:129
  31.3 49.7 %collective-permute-start.11 = (bf16[64,1024]{0,1:T(8,128)(2,1)S(1)}, bf16[64,1024]{0,1:T(8,128)(2,1)S(1)}, u32[]{:S(2)}, u32[]{:S(2)}) collective-permute-start(bf16[64,1024]{0,1:T(8,128)(2,1)S(1)} %get-tuple-element.9), channel_id=1, source_target_pairs={{0,6},{2,8},{4,10},{6,12},{8,14},{10,0},{12,2},{14,4},{1,7},{3,9},... | collective-permute-start | bytes 393224 | tf_op jit(solution)/shard_map/ppermute | solution.py:129
  34.5 43.8 %collective-permute-start.10 = (bf16[64,1024]{0,1:T(8,128)(2,1)S(1)}, bf16[64,1024]{0,1:T(8,128)(2,1)S(1)}, u32[]{:S(2)}, u32[]{:S(2)}) collective-permute-start(bf16[64,1024]{0,1:T(8,128)(2,1)S(1)} %get-tuple-element.9), channel_id=1, source_target_pairs={{0,4},{2,6},{4,8},{6,10},{8,12},{10,14},{12,0},{14,2},{1,5},{3,7},... | collective-permute-start | bytes 393224 | tf_op jit(solution)/shard_map/ppermute | solution.py:129
  34.5 11.8 %collective-permute-start.9 = (bf16[64,1024]{0,1:T(8,128)(2,1)S(1)}, bf16[64,1024]{0,1:T(8,128)(2,1)}, u32[]{:S(2)}, u32[]{:S(2)}) collective-permute-start(bf16[64,1024]{0,1:T(8,128)(2,1)S(1)} %get-tuple-element.9), channel_id=1, source_target_pairs={{0,2},{2,4},{4,6},{6,8},{8,10},{10,12},{12,14},{14,0},{1,3},{3,5},... | collective-permute-start | bytes 393224 | tf_op jit(solution)/shard_map/ppermute | solution.py:129
  46.4 37.6 %collective-permute-start.14 = (bf16[64,1024]{0,1:T(8,128)(2,1)S(1)}, bf16[64,1024]{0,1:T(8,128)(2,1)S(1)}, u32[]{:S(2)}, u32[]{:S(2)}) collective-permute-start(bf16[64,1024]{0,1:T(8,128)(2,1)S(1)} %get-tuple-element.9), channel_id=1, source_target_pairs={{0,12},{2,14},{4,0},{6,2},{8,4},{10,6},{12,8},{14,10},{1,13},{3,15... | collective-permute-start | bytes 393224 | tf_op jit(solution)/shard_map/ppermute | solution.py:129
  78.3 13.1 %collective-permute-start.15 = (bf16[64,1024]{0,1:T(8,128)(2,1)S(1)}, bf16[64,1024]{0,1:T(8,128)(2,1)S(1)}, u32[]{:S(2)}, u32[]{:S(2)}) collective-permute-start(bf16[64,1024]{0,1:T(8,128)(2,1)S(1)} %get-tuple-element.9), channel_id=1, source_target_pairs={{0,14},{2,0},{4,2},{6,4},{8,6},{10,8},{12,10},{14,12},{1,15},{3,1}... | collective-permute-start | bytes 393224 | tf_op jit(solution)/shard_map/ppermute | solution.py:129
  81.0 20.8 %collective-permute-start.8 = (bf16[8,64,256]{2,1,0:T(8,128)(2,1)}, bf16[8,64,256]{2,1,0:T(8,128)(2,1)}, u32[]{:S(2)}, u32[]{:S(2)}) collective-permute-start(bf16[8,64,256]{2,1,0:T(8,128)(2,1)} %broadcast_select_fusion.2), channel_id=1, source_target_pairs={{0,1},{1,0},{2,3},{3,2},{4,5},{5,4},{6,7},{7,6},{8,9},{9,8},{10,11... | collective-permute-start | bytes 786440 | tf_op jit(solution)/shard_map/ppermute | solution.py:133
  98.9 11.3 %collective-permute-start.16 = (bf16[8,64,1024]{2,1,0:T(8,128)(2,1)}, bf16[8,64,1024]{2,1,0:T(8,128)(2,1)}, u32[]{:S(2)}, u32[]{:S(2)}) collective-permute-start(bf16[8,64,1024]{2,1,0:T(8,128)(2,1)} %copy.53), channel_id=1, source_target_pairs={{0,1},{1,0},{2,3},{3,2},{4,5},{5,4},{6,7},{7,6},{8,9},{9,8},{10,11... | collective-permute-start | bytes 3145736 | tf_op jit(solution)/shard_map/ppermute | solution.py:133
  103.7 0.8 copy-start.3
  107.2 5.8 %copy-start.2 = (bf16[1,8,64,1024]{2,3,1,0:T(8,128)(2,1)S(1)}, bf16[1,8,64,1024]{2,3,1,0:T(8,128)(2,1)}, u32[]{:S(2)}) copy-start(bf16[1,8,64,1024]{2,3,1,0:T(8,128)(2,1)} %bitcast_select_fusion.1) | copy-start | bytes 3145732
  127.5 4.8 %copy-start.1 = (bf16[2,8,64,1024]{3,2,1,0:T(8,128)(2,1)S(1)}, bf16[2,8,64,1024]{3,2,1,0:T(8,128)(2,1)}, u32[]{:S(2)}) copy-start(bf16[2,8,64,1024]{3,2,1,0:T(8,128)(2,1)} %copy.56) | copy-start | bytes 6291460
  142.9 0.7 copy-start.5
  164.4 0.7 copy-start.4

commit v3 on v1

--- a/solution.py
+++ b/solution.py
@@ -102,7 +102,8 @@
     squares = jnp.einsum("kmn,kmn->m", masked, masked, preferred_element_type=jnp.float32)
     squares = jnp.broadcast_to(squares[:, None], (block, 128))
     partial = jnp.concatenate([dense, squares], axis=1)
-    summed = lax.psum_scatter(partial, "col", scatter_dimension=0, tiled=True)
+    chunks = partial.reshape(n_col, share, total_rows + 128)
+    summed = jnp.sum(lax.all_to_all(chunks, "col", 0, 0, tiled=True), axis=0)
 
     entries = (own_count * block).astype(jnp.float32)
     scale = lax.rsqrt(summed[:, total_rows] / entries + EPSILON) / jnp.sqrt(entries) / HALF_WIDTH
@@ -113,19 +114,21 @@
     start_hi, start_lo = split_bf16(piece)
     extra = jnp.concatenate([start_hi, start_lo], axis=0)
     extra = jnp.concatenate(
-        [extra, scale_hi[:, None], scale_lo[:, None], jnp.zeros((share, 254 - nb_dev * share), jnp.bfloat16)],
-        axis=1,
+        [extra, scale_hi[:, None], scale_lo[:, None], jnp.zeros((share, 126), jnp.bfloat16)], axis=1
     )
-    packed = jnp.concatenate([summed[:, :total_rows].astype(jnp.bfloat16), extra], axis=1)
-    across = lax.all_gather(packed, ("row", "col"), axis=0, tiled=False)
-    whole = lax.all_gather(across, "vec", axis=0, tiled=False)
-    whole = whole.reshape(total_rows, total_rows + 256)
+    rows_bf16 = summed[:, :total_rows].astype(jnp.bfloat16)
+
+    packed = jnp.concatenate([rows_bf16, extra], axis=1)
+    copies = jnp.broadcast_to(packed[None], (n_row * n_col,) + packed.shape)
+    half = lax.all_to_all(copies, ("row", "col"), 0, 0, tiled=True)
+    copies = jnp.broadcast_to(half[None], (2,) + half.shape)
+    whole = lax.all_to_all(copies, "vec", 0, 0, tiled=True).reshape(total_rows, total_rows + 256)
     weights = whole[:, :total_rows]
+    extras = whole[:, total_rows:]
     scaling = (
-        whole[:, total_rows + nb_dev * share].astype(jnp.float32)
-        + whole[:, total_rows + nb_dev * share + 1].astype(jnp.float32)
+        extras[:, nb_dev * share].astype(jnp.float32) + extras[:, nb_dev * share + 1].astype(jnp.float32)
     )[None, :]
-    coded = whole[:, total_rows : total_rows + nb_dev * share].astype(jnp.float32)
+    coded = extras[:, : nb_dev * share].astype(jnp.float32)
     coded = coded.reshape(2, n_row, n_col, 2, vec_cols, nb_dev, share)
     coded = coded[:, :, :, 0] + coded[:, :, :, 1]
     current = coded.transpose(0, 3, 4, 1, 2, 5).reshape(cols, total_rows)
@@ -160,7 +163,7 @@
         and tiles.shape[0] == n_vec
         and block % n_col == 0
         and block // n_col == 2 * start.shape[0]
-        and tiles.shape[0] * (block // n_col) <= 254
+        and tiles.shape[0] * (block // n_col) <= 128
     )
     if fits:
         return replicated(start, tiles, pattern, counts)

time: 145 us -> 113 us (0.78)
  waiting for transfers between devices: 70.8 us -> 39.3 us
  between operations: 14.1 us -> 0.97 us
  starting transfers between devices: 0.27 us -> 9.33 us
  blocking collectives: 0 us -> 5.84 us
    all_gather x2 -> x0, waiting for transfers between devices: 53.6 us -> none  [the longest x1 42 us: replicated(): across = lax.all_gather(packed, ('row', 'col'), axis=0, tiled=False)]
    all_to_all x0 -> x2, waiting for transfers between devices: none -> 39.3 us  [the longest x1 30.8 us: replicated(): half = lax.all_to_all(copies, ('row', 'col'), 0, 0, tiled=True)]
    unnamed x4 -> x0, waiting for transfers between devices: 17.2 us -> none
    all_to_all x0 -> x2, starting transfers between devices: none -> 9.33 us  [the longest x1 5.13 us: replicated(): half = lax.all_to_all(copies, ('row', 'col'), 0, 0, tiled=True)]
    all_to_all x0 -> x1, blocking collectives: none -> 5.84 us  [replicated(): lax.all_to_all(copies, 'vec', 0, 0, tiled=True)]
  transfers between devices with their start and end apart: 3 -> 2, of which waited for: 3 -> 2; matrix products, arithmetic and copies ran while one was open for 0% -> 0% of each run, Pallas kernels for 0% -> 0%
where the time goes in v3:
time: 113 us
  waiting for transfers between devices  39.3 us (35%)
  other arithmetic  28.4 us (25%)
  matrix products  21.7 us (19%)
  starting transfers between devices  9.33 us (8%)
  local copies, waits for them, and re-layouts  7.48 us (7%)
  blocking collectives  5.84 us (5%)
    all_to_all x1, waiting for transfers between devices, replicated(): half = lax.all_to_all(copies, ('row', 'col'), 0, 0, tiled=True)  30.8 us
    dot_general x14, matrix products, apply_dense(): jnp.einsum('cj,ij->ci', values.astype(jnp.bfloat16), weights, preferred_e...  19.9 us
    another operation x6, other arithmetic, replicated(): lower = jnp.linalg.cholesky(gram)  13 us
    all_to_all x1, waiting for transfers between devices, replicated(): summed = jnp.sum(lax.all_to_all(chunks, 'col', 0, 0, tiled=True), axis=0)  8.5 us
    all_to_all x1, blocking collectives, replicated(): lax.all_to_all(copies, 'vec', 0, 0, tiled=True)  5.84 us
    another operation x2, other arithmetic, replicated(): current = jax.scipy.linalg.solve_triangular(lower, filtered, lower=True)  5.55 us
    another operation x2, other arithmetic, replicated(): solved = jax.scipy.linalg.solve_triangular(lower, mine, lower=True)  5.55 us
    all_to_all x1, starting transfers between devices, replicated(): half = lax.all_to_all(copies, ('row', 'col'), 0, 0, tiled=True)  5.13 us
  transfers between devices with their start and end apart: 2, of which 2 were waited for; matrix products, arithmetic and copies ran while one was open for 0% of the time, Pallas kernels for 0%

profile of v3, /device:TPU:0, one launch (start us, length us, event | category | flops | bytes accessed | tf_op | source)
XLA Modules:
  0.0 113.0 jit_solution(11110982532951860803)
XLA Ops:
  0.0 1.3 %dynamic_slice.28 = s32[1]{0:T(128)} dynamic-slice(s32[2]{0:T(128)} %param.8, s32[]{:T(128)S(6)} %select_n.48), dynamic_slice_sizes={1} | dynamic-slice | bytes 12 | tf_op jit(solution)/shard_map/jit(dynamic_index_in_dim)/dynamic_slice | solution.py:93
  2.1 1.3 %fusion.30 = f32[128]{0:T(128)S(1)} fusion(bf16[1,16,128,128]{3,2,1,0:T(8,128)(2,1)S(1)} %constant_dynamic-slice_fusion.2, bf16[16]{0:T(256)(128)(2,1)S(1)} %get-tuple-element.10), kind=kLoop, calls=%fused_computation.50 | loop fusion | flops 1048448 | bytes 524832 | tf_op jit(solution)/shard_map/kmn,kmn->m/dot_general | solution.py:102
  3.3 0.8 fusion.73
  4.7 0.9 pad_maximum_fusion
  5.6 4.2 %all-to-all-start = ((f32[2,64,1152]{2,1,0:T(8,128)}), f32[2,64,1152]{2,1,0:T(8,128)S(1)}, u32[]{:S(2)}, u32[]{:S(2)}) async-start(f32[2,64,1152]{2,1,0:T(8,128)} %pad_maximum_fusion), calls=%async_computation | async-start | bytes 1179648 | tf_op jit(solution)/shard_map/all_to_all | solution.py:106
  10.7 8.5 %all-to-all-done = f32[2,64,1152]{2,1,0:T(8,128)S(1)} async-done(((f32[2,64,1152]{2,1,0:T(8,128)}), f32[2,64,1152]{2,1,0:T(8,128)S(1)}, u32[]{:S(2)}, u32[]{:S(2)}) %all-to-all-start) | async-done | bytes 589856 | tf_op jit(solution)/shard_map/all_to_all | solution.py:106
  19.8 1.1 %broadcast_in_dim.13 = bf16[8,64,1280]{2,1,0:T(8,128)(2,1)} broadcast(bf16[64,1280]{1,0:T(8,128)(2,1)S(1)} %concatenate.15), dimensions={1,2} | broadcast | bytes 1474560 | tf_op jit(solution)/shard_map/broadcast_in_dim | solution.py:122
  20.9 5.1 %all-to-all-start.1 = ((bf16[8,64,1280]{2,1,0:T(8,128)(2,1)}), bf16[8,64,1280]{2,1,0:T(8,128)(2,1)S(1)}, u32[]{:S(2)}, u32[]{:S(2)}) async-start(bf16[8,64,1280]{2,1,0:T(8,128)(2,1)} %broadcast_in_dim.13), calls=%async_computation.1 | async-start | bytes 2621440 | tf_op jit(solution)/shard_map/all_to_all | solution.py:123
  26.0 30.8 %all-to-all-done.1 = bf16[8,64,1280]{2,1,0:T(8,128)(2,1)S(1)} async-done(((bf16[8,64,1280]{2,1,0:T(8,128)(2,1)}), bf16[8,64,1280]{2,1,0:T(8,128)(2,1)S(1)}, u32[]{:S(2)}, u32[]{:S(2)}) %all-to-all-start.1) | async-done | bytes 1310752 | tf_op jit(solution)/shard_map/all_to_all | solution.py:123
  57.1 5.8 %all_to_all.15 = bf16[2,8,64,1280]{3,2,1,0:T(8,128)(2,1)S(1)} all-to-all(bf16[2,8,64,1280]{3,2,1,0:T(8,128)(2,1)S(1)} %broadcast_in_dim.14), channel_id=1, replica_groups=mesh['grp'=2,'row'=4,'col'=2,'vec'=2] {'vec'}, dimensions={0} | all-to-all | bytes 5242880 | tf_op jit(solution)/shard_map/all_to_all | solution.py:125
  63.2 1.2 %copy-done.1 = bf16[2,8,64,1280]{3,2,1,0:T(8,128)(2,1)} copy-done((bf16[2,8,64,1280]{3,2,1,0:T(8,128)(2,1)}, bf16[2,8,64,1280]{3,2,1,0:T(8,128)(2,1)S(1)}, u32[]{:S(2)}) %copy-start.1) | copy-done | bytes 2621464
  66.3 2.5 %convolution_multiply_fusion.15 = f32[64,1024]{1,0:T(8,128)S(1)} fusion(f32[1024]{0:T(1024)S(1)} %add_reduce_fusion, f32[64,1024]{1,0:T(8,128)S(1)} %reshape.133, bf16[1024,1280]{1,0:T(8,128)(2,1)} %bitcast.66), kind=kOutput, calls=%fused_computation.44 | convolution fusion | flops 134348800 | bytes 2625536 | tf_op jit(solution)/shard_map/cj,ij->ci/dot_general | solution.py:137
  70.3 0.8 fusion.23
  71.1 0.8 fusion.21
  71.8 0.8 fusion.19
  72.6 3.6 %fusion.15 = f32[64,1024]{1,0:T(8,128)S(1)} fusion(f32[64,1024]{1,0:T(8,128)S(1)} %fusion.19, f32[64,1024]{1,0:T(8,128)S(1)} %fusion.21, f32[1024]{0:T(1024)S(1)} %add_reduce_fusion, bf16[1024,1280]{1,0:T(8,128)(2,1)} %bitcast.67), kind=kOutput, calls=%fused_computation.25 | convolution fusion | flops 268959744 | bytes 5251072 | tf_op jit(solution)/shard_map/cj,ij->ci/dot_general | solution.py:137
  76.7 5.8 %cholesky.44 = f32[64,64]{1,0:T(8,128)S(1)} custom-call(f32[64,64]{1,0:T(8,128)S(1)} %fusion.64), custom_call_target="Cholesky" | custom-call | tf_op jit(solution)/shard_map/jit(cholesky)/cholesky | solution.py:145
  83.8 4.9 %custom-call.10 = f32[1,64,64]{1,2,0:T(8,128)S(1)} custom-call(f32[1,64,64]{2,1,0:T(8,128)S(1)} %fusion.58), custom_call_target="InvertDiagBlocksLowerTriangular" | custom-call | tf_op jit(solution)/shard_map/jit(_solve_triangular)/triangular_solve | solution.py:147
  89.2 2.6 %convolution_multiply_fusion.7 = f32[64,1024]{1,0:T(8,128)S(1)} fusion(f32[64,1024]{1,0:T(8,128)S(1)} %fusion.62, f32[1024]{0:T(1024)S(1)} %add_reduce_fusion, bf16[1024,1280]{1,0:T(8,128)(2,1)} %bitcast.68), kind=kOutput, calls=%fused_computation.22 | convolution fusion | flops 134348800 | bytes 2625536 | tf_op jit(solution)/shard_map/cj,ij->ci/dot_general | solution.py:137
  94.0 0.8 fusion.7
  94.8 0.8 fusion.5
  95.5 3.6 %fusion.1 = f32[64,1024]{1,0:T(8,128)S(1)} fusion(f32[64,1024]{1,0:T(8,128)S(1)} %fusion.5, f32[64,1024]{1,0:T(8,128)S(1)} %fusion.7, f32[1024]{0:T(1024)S(1)} %add_reduce_fusion, bf16[1024,1280]{1,0:T(8,128)(2,1)} %bitcast.69), kind=kOutput, calls=%fused_computation.3 | convolution fusion | flops 268959744 | bytes 5251072 | tf_op jit(solution)/shard_map/cj,ij->ci/dot_general | solution.py:137
  99.8 5.8 %cholesky.55 = f32[64,64]{1,0:T(8,128)S(1)} custom-call(f32[64,64]{1,0:T(8,128)S(1)} %fusion.61), custom_call_target="Cholesky" | custom-call | tf_op jit(solution)/shard_map/jit(cholesky)/cholesky | solution.py:145
  106.9 4.9 %custom-call.11 = f32[1,64,64]{1,2,0:T(8,128)S(1)} custom-call(f32[1,64,64]{2,1,0:T(8,128)S(1)} %fusion.59), custom_call_target="InvertDiagBlocksLowerTriangular" | custom-call | tf_op jit(solution)/shard_map/jit(_solve_triangular)/triangular_solve | solution.py:151
  (58 shorter events, 13.4 us)
Async XLA Ops:
  0.0 2.0 %copy-start = (bf16[2,16,128,128]{3,2,1,0:T(8,128)(2,1)S(1)}, bf16[2,16,128,128]{3,2,1,0:T(8,128)(2,1)}, u32[]{:S(2)}) copy-start(bf16[2,16,128,128]{3,2,1,0:T(8,128)(2,1)} %param.6) | copy-start | bytes 3145732
  2.0 8.5 %copy-start.4 = (f32[32,256]{1,0:T(8,128)S(1)}, f32[32,256]{1,0:T(8,128)}, u32[]{:S(2)}) copy-start(f32[32,256]{1,0:T(8,128)} %param.5) | copy-start | bytes 98308
  5.6 13.6 %all-to-all-start = ((f32[2,64,1152]{2,1,0:T(8,128)}), f32[2,64,1152]{2,1,0:T(8,128)S(1)}, u32[]{:S(2)}, u32[]{:S(2)}) async-start(f32[2,64,1152]{2,1,0:T(8,128)} %pad_maximum_fusion), calls=%async_computation | async-start | bytes 1179648 | tf_op jit(solution)/shard_map/all_to_all | solution.py:106
  20.9 35.9 %all-to-all-start.1 = ((bf16[8,64,1280]{2,1,0:T(8,128)(2,1)}), bf16[8,64,1280]{2,1,0:T(8,128)(2,1)S(1)}, u32[]{:S(2)}, u32[]{:S(2)}) async-start(bf16[8,64,1280]{2,1,0:T(8,128)(2,1)} %broadcast_in_dim.13), calls=%async_computation.1 | async-start | bytes 2621440 | tf_op jit(solution)/shard_map/all_to_all | solution.py:123
  62.9 1.5 %copy-start.1 = (bf16[2,8,64,1280]{3,2,1,0:T(8,128)(2,1)}, bf16[2,8,64,1280]{3,2,1,0:T(8,128)(2,1)S(1)}, u32[]{:S(2)}) copy-start(bf16[2,8,64,1280]{3,2,1,0:T(8,128)(2,1)S(1)} %all_to_all.15) | copy-start | bytes 7864324
  66.3 2.5 %copy-start.2 = (bf16[2,8,64,1280]{3,2,1,0:T(8,128)(2,1)S(1)}, bf16[2,8,64,1280]{3,2,1,0:T(8,128)(2,1)}, u32[]{:S(2)}) copy-start(bf16[2,8,64,1280]{3,2,1,0:T(8,128)(2,1)} %copy-done.1) | copy-start | bytes 7864324
  88.7 3.0 %copy-start.3 = (bf16[2,8,64,1280]{3,2,1,0:T(8,128)(2,1)S(1)}, bf16[2,8,64,1280]{3,2,1,0:T(8,128)(2,1)}, u32[]{:S(2)}) copy-start(bf16[2,8,64,1280]{3,2,1,0:T(8,128)(2,1)} %copy-done.1) | copy-start | bytes 7864324

commit v4 on v3

--- a/solution.py
+++ b/solution.py
@@ -1,6 +1,8 @@
 import jax
 import jax.numpy as jnp
 from jax import lax
+from jax.experimental import pallas as pl
+from jax.experimental.pallas import tpu as pltpu
 from jax.sharding import PartitionSpec as P
 
 DEGREE = 8
@@ -34,6 +36,37 @@
     solved = jax.scipy.linalg.solve_triangular(lower, both, lower=True)
     width = mine.shape[0]
     return lax.dynamic_slice_in_dim(solved, lax.axis_index("vec") * width, width, 0)
+
+
+def orthonormal_kernel(y_ref, x_ref):
+    y = y_ref[...]
+    n, total = y.shape
+    hi = lax.Precision.HIGHEST
+    a = lax.dot_general(y, y, (((1,), (1,)), ((), ())), precision=hi, preferred_element_type=jnp.float32)
+    a = a / total
+    rows = lax.broadcasted_iota(jnp.int32, (n, n), 0)
+    cols = lax.broadcasted_iota(jnp.int32, (n, n), 1)
+    inverse = (rows == cols).astype(jnp.float32)
+    for k in range(n):
+        pivot = jnp.sqrt(a[k : k + 1, k : k + 1])
+        down = jnp.where(rows[:, k : k + 1] >= k, a[:, k : k + 1] / pivot, 0.0)
+        across = jnp.where(cols[k : k + 1, :] >= k, a[k : k + 1, :] / pivot, 0.0)
+        a = a - down * across
+        solved = inverse[k : k + 1, :] / pivot
+        below = jnp.where(rows[:, k : k + 1] > k, down, 0.0)
+        inverse = jnp.where(rows == k, solved, inverse - below * solved)
+    x_ref[...] = lax.dot_general(
+        inverse, y, (((1,), (0,)), ((), ())), precision=hi, preferred_element_type=jnp.float32
+    )
+
+
+def orthonormal_local(y):
+    return pl.pallas_call(
+        orthonormal_kernel,
+        out_shape=jax.ShapeDtypeStruct(y.shape, jnp.float32),
+        in_specs=[pl.BlockSpec(memory_space=pltpu.VMEM)],
+        out_specs=pl.BlockSpec(memory_space=pltpu.VMEM),
+    )(y)
 
 
 def distributed(start, tiles, pattern, counts):
@@ -140,16 +173,10 @@
         return product * scaling
 
     for outer in range(ITERS):
-        filtered = chebyshev(current, apply_dense)
-        gram = jnp.dot(filtered, filtered.T, precision=lax.Precision.HIGHEST) / total_rows
-        lower = jnp.linalg.cholesky(gram)
-        if outer < ITERS - 1:
-            current = jax.scipy.linalg.solve_triangular(lower, filtered, lower=True)
-        else:
-            mine = filtered.reshape(cols, nb_dev, n_row, block)
-            mine = lax.dynamic_index_in_dim(mine, row_index, 2, keepdims=False).reshape(cols, nb_dev * block)
-            solved = jax.scipy.linalg.solve_triangular(lower, mine, lower=True)
-            current = lax.dynamic_slice_in_dim(solved, vec_index * vec_cols, vec_cols, 0)
+        current = orthonormal_local(chebyshev(current, apply_dense))
+    mine = current.reshape(cols, nb_dev, n_row, block)
+    mine = lax.dynamic_index_in_dim(mine, row_index, 2, keepdims=False).reshape(cols, nb_dev * block)
+    current = lax.dynamic_slice_in_dim(mine, vec_index * vec_cols, vec_cols, 0)
     return current
 
 

time: 113 us -> 109 us (0.965)
  other arithmetic: 28.4 us -> 4.26 us
  Pallas kernels: 0 us -> 17.8 us
    another operation x10 -> x0, other arithmetic: 24.1 us -> none  [the longest x6 13 us: replicated(): lower = jnp.linalg.cholesky(gram)]
    pallas_call x0 -> x2, Pallas kernels: none -> 17.8 us  [orthonormal_local(): pl.pallas_call(orthonormal_kernel, out_shape=jax.ShapeDtypeStruct(y.shape...]
    dot_general x14, matrix products: 19.9 us -> 22.4 us  [apply_dense(): jnp.einsum('cj,ij->ci', values.astype(jnp.bfloat16), weights, preferred_e...]
where the time goes in v4:
time: 109 us
  waiting for transfers between devices  39.3 us (36%)
  matrix products  22.8 us (21%)
  Pallas kernels  17.8 us (16%)
  starting transfers between devices  9.33 us (9%)
  local copies, waits for them, and re-layouts  8.29 us (8%)
  blocking collectives  5.84 us (5%)
  other arithmetic  4.26 us (4%)
    all_to_all x1, waiting for transfers between devices, replicated(): half = lax.all_to_all(copies, ('row', 'col'), 0, 0, tiled=True)  30.8 us
    dot_general x14, matrix products, apply_dense(): jnp.einsum('cj,ij->ci', values.astype(jnp.bfloat16), weights, preferred_e...  22.4 us
    pallas_call x2, Pallas kernels, orthonormal_local(): pl.pallas_call(orthonormal_kernel, out_shape=jax.ShapeDtypeStruct(y.shape...  17.8 us
    all_to_all x1, waiting for transfers between devices, replicated(): summed = jnp.sum(lax.all_to_all(chunks, 'col', 0, 0, tiled=True), axis=0)  8.5 us
    all_to_all x1, blocking collectives, replicated(): lax.all_to_all(copies, 'vec', 0, 0, tiled=True)  5.84 us
    all_to_all x1, starting transfers between devices, replicated(): half = lax.all_to_all(copies, ('row', 'col'), 0, 0, tiled=True)  5.13 us
    all_to_all x1, starting transfers between devices, replicated(): summed = jnp.sum(lax.all_to_all(chunks, 'col', 0, 0, tiled=True), axis=0)  4.21 us
  transfers between devices with their start and end apart: 2, of which 2 were waited for; matrix products, arithmetic and copies ran while one was open for 0% of the time, Pallas kernels for 0%

profile of v4, /device:TPU:0, one launch (start us, length us, event | category | flops | bytes accessed | tf_op | source)
XLA Modules:
  0.0 108.5 jit_solution(15215174174179850177)
XLA Ops:
  0.0 1.3 %dynamic_slice.28 = s32[1]{0:T(128)} dynamic-slice(s32[2]{0:T(128)} %param.7, s32[]{:T(128)S(6)} %select_n.45), dynamic_slice_sizes={1} | dynamic-slice | bytes 12 | tf_op jit(solution)/shard_map/jit(dynamic_index_in_dim)/dynamic_slice | solution.py:126
  2.1 1.3 %fusion.30 = f32[128]{0:T(128)S(1)} fusion(bf16[1,16,128,128]{3,2,1,0:T(8,128)(2,1)S(1)} %constant_dynamic-slice_fusion.2, bf16[16]{0:T(256)(128)(2,1)S(1)} %get-tuple-element.9), kind=kLoop, calls=%fused_computation.48 | loop fusion | flops 1048448 | bytes 524832 | tf_op jit(solution)/shard_map/kmn,kmn->m/dot_general | solution.py:135
  3.3 0.8 fusion.61
  4.7 0.9 pad_maximum_fusion
  5.6 4.2 %all-to-all-start = ((f32[2,64,1152]{2,1,0:T(8,128)}), f32[2,64,1152]{2,1,0:T(8,128)S(1)}, u32[]{:S(2)}, u32[]{:S(2)}) async-start(f32[2,64,1152]{2,1,0:T(8,128)} %pad_maximum_fusion), calls=%async_computation | async-start | bytes 1179648 | tf_op jit(solution)/shard_map/all_to_all | solution.py:139
  10.8 8.5 %all-to-all-done = f32[2,64,1152]{2,1,0:T(8,128)S(1)} async-done(((f32[2,64,1152]{2,1,0:T(8,128)}), f32[2,64,1152]{2,1,0:T(8,128)S(1)}, u32[]{:S(2)}, u32[]{:S(2)}) %all-to-all-start) | async-done | bytes 589856 | tf_op jit(solution)/shard_map/all_to_all | solution.py:139
  19.8 1.2 %broadcast_in_dim.13 = bf16[8,64,1280]{2,1,0:T(8,128)(2,1)} broadcast(bf16[64,1280]{1,0:T(8,128)(2,1)S(1)} %concatenate.15), dimensions={1,2} | broadcast | bytes 1474560 | tf_op jit(solution)/shard_map/broadcast_in_dim | solution.py:155
  20.9 5.1 %all-to-all-start.1 = ((bf16[8,64,1280]{2,1,0:T(8,128)(2,1)}), bf16[8,64,1280]{2,1,0:T(8,128)(2,1)S(1)}, u32[]{:S(2)}, u32[]{:S(2)}) async-start(bf16[8,64,1280]{2,1,0:T(8,128)(2,1)} %broadcast_in_dim.13), calls=%async_computation.1 | async-start | bytes 2621440 | tf_op jit(solution)/shard_map/all_to_all | solution.py:156
  26.1 30.8 %all-to-all-done.1 = bf16[8,64,1280]{2,1,0:T(8,128)(2,1)S(1)} async-done(((bf16[8,64,1280]{2,1,0:T(8,128)(2,1)}), bf16[8,64,1280]{2,1,0:T(8,128)(2,1)S(1)}, u32[]{:S(2)}, u32[]{:S(2)}) %all-to-all-start.1) | async-done | bytes 1310752 | tf_op jit(solution)/shard_map/all_to_all | solution.py:156
  57.1 5.8 %all_to_all.15 = bf16[2,8,64,1280]{3,2,1,0:T(8,128)(2,1)S(1)} all-to-all(bf16[2,8,64,1280]{3,2,1,0:T(8,128)(2,1)S(1)} %broadcast_in_dim.14), channel_id=1, replica_groups=mesh['grp'=2,'row'=4,'col'=2,'vec'=2] {'vec'}, dimensions={0} | all-to-all | bytes 5242880 | tf_op jit(solution)/shard_map/all_to_all | solution.py:158
  63.2 1.2 %copy-done.1 = bf16[2,8,64,1280]{3,2,1,0:T(8,128)(2,1)} copy-done((bf16[2,8,64,1280]{3,2,1,0:T(8,128)(2,1)}, bf16[2,8,64,1280]{3,2,1,0:T(8,128)(2,1)S(1)}, u32[]{:S(2)}) %copy-start.1) | copy-done | bytes 2621464
  66.3 2.5 %convolution_multiply_fusion.15 = f32[64,1024]{1,0:T(8,128)S(1)} fusion(f32[1024]{0:T(1024)S(1)} %add_reduce_fusion, f32[64,1024]{1,0:T(8,128)S(1)} %reshape.120, bf16[1024,1280]{1,0:T(8,128)(2,1)} %bitcast.43), kind=kOutput, calls=%fused_computation.44 | convolution fusion | flops 134348800 | bytes 2625536 | tf_op jit(solution)/shard_map/cj,ij->ci/dot_general | solution.py:170
  69.6 0.8 fusion.25
  70.3 0.8 fusion.23
  71.1 0.8 fusion.21
  72.6 4.4 %fusion.15.y_ref = f32[64,1024]{1,0:T(8,128)} fusion(f32[64,1024]{1,0:T(8,128)S(1)} %fusion.19, f32[64,1024]{1,0:T(8,128)S(1)} %fusion.21, f32[1024]{0:T(1024)S(1)} %add_reduce_fusion, bf16[1024,1280]{1,0:T(8,128)(2,1)} %bitcast.44), kind=kOutput, calls=%fused_computation.25 | convolution fusion | flops 268959744 | bytes 5251072 | tf_op jit(solution)/shard_map/cj,ij->ci/dot_general | solution.py:170
  77.0 8.9 %shard_map.46 = f32[64,1024]{1,0:T(8,128)} custom-call(f32[64,1024]{1,0:T(8,128)} %fusion.15.y_ref), custom_call_target="tpu_custom_call" | custom-call | tf_op jit(solution)/shard_map/pallas_call | solution.py:64
  86.0 2.6 %convolution_multiply_fusion.7 = f32[64,1024]{1,0:T(8,128)S(1)} fusion(f32[64,1024]{1,0:T(8,128)} %shard_map.46, f32[1024]{0:T(1024)S(1)} %add_reduce_fusion, bf16[1024,1280]{1,0:T(8,128)(2,1)} %bitcast.45), kind=kOutput, calls=%fused_computation.22 | convolution fusion | flops 134348800 | bytes 2625536 | tf_op jit(solution)/shard_map/cj,ij->ci/dot_general | solution.py:170
  88.6 1.7 %fusion.13 = f32[64,1024]{1,0:T(8,128)S(1)} fusion(f32[64,1024]{1,0:T(8,128)} %shard_map.46, f32[64,1024]{1,0:T(8,128)S(1)} %convolution_multiply_fusion.7, f32[1024]{0:T(1024)S(1)} %add_reduce_fusion, bf16[1024,1280]{1,0:T(8,128)(2,1)S(1)} %bitcast.52), kind=kOutput, calls=%fused_computation.21 | convolution fusion | flops 134479872 | bytes 2887680 | tf_op jit(solution)/shard_map/cj,ij->ci/dot_general | solution.py:170
  91.8 0.8 fusion.7
  92.5 0.8 fusion.5
  93.3 4.4 %fusion.1.y_ref = f32[64,1024]{1,0:T(8,128)} fusion(f32[64,1024]{1,0:T(8,128)S(1)} %fusion.5, f32[64,1024]{1,0:T(8,128)S(1)} %fusion.7, f32[1024]{0:T(1024)S(1)} %add_reduce_fusion, bf16[1024,1280]{1,0:T(8,128)(2,1)} %bitcast.46), kind=kOutput, calls=%fused_computation.3 | convolution fusion | flops 268959744 | bytes 5251072 | tf_op jit(solution)/shard_map/cj,ij->ci/dot_general | solution.py:170
  97.7 8.9 %shard_map.47 = f32[64,1024]{1,0:T(8,128)} custom-call(f32[64,1024]{1,0:T(8,128)} %fusion.1.y_ref), custom_call_target="tpu_custom_call" | custom-call | tf_op jit(solution)/shard_map/pallas_call | solution.py:64
  106.6 1.1 reshape.121
  (43 shorter events, 8.3 us)
Async XLA Ops:
  0.0 2.0 %copy-start = (bf16[2,16,128,128]{3,2,1,0:T(8,128)(2,1)S(1)}, bf16[2,16,128,128]{3,2,1,0:T(8,128)(2,1)}, u32[]{:S(2)}) copy-start(bf16[2,16,128,128]{3,2,1,0:T(8,128)(2,1)} %param.5) | copy-start | bytes 3145732
  2.0 8.5 %copy-start.4 = (f32[32,256]{1,0:T(8,128)S(1)}, f32[32,256]{1,0:T(8,128)}, u32[]{:S(2)}) copy-start(f32[32,256]{1,0:T(8,128)} %param.4) | copy-start | bytes 98308
  5.6 13.6 %all-to-all-start = ((f32[2,64,1152]{2,1,0:T(8,128)}), f32[2,64,1152]{2,1,0:T(8,128)S(1)}, u32[]{:S(2)}, u32[]{:S(2)}) async-start(f32[2,64,1152]{2,1,0:T(8,128)} %pad_maximum_fusion), calls=%async_computation | async-start | bytes 1179648 | tf_op jit(solution)/shard_map/all_to_all | solution.py:139
  20.9 35.9 %all-to-all-start.1 = ((bf16[8,64,1280]{2,1,0:T(8,128)(2,1)}), bf16[8,64,1280]{2,1,0:T(8,128)(2,1)S(1)}, u32[]{:S(2)}, u32[]{:S(2)}) async-start(bf16[8,64,1280]{2,1,0:T(8,128)(2,1)} %broadcast_in_dim.13), calls=%async_computation.1 | async-start | bytes 2621440 | tf_op jit(solution)/shard_map/all_to_all | solution.py:156
  62.9 1.5 %copy-start.1 = (bf16[2,8,64,1280]{3,2,1,0:T(8,128)(2,1)}, bf16[2,8,64,1280]{3,2,1,0:T(8,128)(2,1)S(1)}, u32[]{:S(2)}) copy-start(bf16[2,8,64,1280]{3,2,1,0:T(8,128)(2,1)S(1)} %all_to_all.15) | copy-start | bytes 7864324
  66.3 2.5 %copy-start.2 = (bf16[2,8,64,1280]{3,2,1,0:T(8,128)(2,1)S(1)}, bf16[2,8,64,1280]{3,2,1,0:T(8,128)(2,1)}, u32[]{:S(2)}) copy-start(bf16[2,8,64,1280]{3,2,1,0:T(8,128)(2,1)} %copy-done.1) | copy-start | bytes 7864324
  86.0 2.6 %copy-start.3 = (bf16[2,8,64,1280]{3,2,1,0:T(8,128)(2,1)S(1)}, bf16[2,8,64,1280]{3,2,1,0:T(8,128)(2,1)}, u32[]{:S(2)}) copy-start(bf16[2,8,64,1280]{3,2,1,0:T(8,128)(2,1)} %copy-done.1) | copy-start | bytes 7864324

commit v5 on v4

--- a/solution.py
+++ b/solution.py
@@ -38,8 +38,7 @@
     return lax.dynamic_slice_in_dim(solved, lax.axis_index("vec") * width, width, 0)
 
 
-def orthonormal_kernel(y_ref, x_ref):
-    y = y_ref[...]
+def orthonormal_value(y):
     n, total = y.shape
     hi = lax.Precision.HIGHEST
     a = lax.dot_general(y, y, (((1,), (1,)), ((), ())), precision=hi, preferred_element_type=jnp.float32)
@@ -55,19 +54,37 @@
         solved = inverse[k : k + 1, :] / pivot
         below = jnp.where(rows[:, k : k + 1] > k, down, 0.0)
         inverse = jnp.where(rows == k, solved, inverse - below * solved)
-    x_ref[...] = lax.dot_general(
+    return lax.dot_general(
         inverse, y, (((1,), (0,)), ((), ())), precision=hi, preferred_element_type=jnp.float32
     )
 
 
-def orthonormal_local(y):
+def filter_kernel(w_ref, s_ref, y_ref, x_ref):
+    total = y_ref.shape[1]
+    scaling = s_ref[...]
+
+    def apply(values):
+        product = lax.dot_general(
+            values.astype(jnp.bfloat16),
+            w_ref[:, :total],
+            (((1,), (1,)), ((), ())),
+            preferred_element_type=jnp.float32,
+        )
+        return product * scaling
+
+    current = y_ref[...]
+    for outer in range(ITERS):
+        current = orthonormal_value(chebyshev(current, apply))
+    x_ref[...] = current
+
+
+def filter_local(packed_weights, scaling, start):
     return pl.pallas_call(
-        orthonormal_kernel,
-        out_shape=jax.ShapeDtypeStruct(y.shape, jnp.float32),
-        in_specs=[pl.BlockSpec(memory_space=pltpu.VMEM)],
+        filter_kernel,
+        out_shape=jax.ShapeDtypeStruct(start.shape, jnp.float32),
+        in_specs=[pl.BlockSpec(memory_space=pltpu.VMEM)] * 3,
         out_specs=pl.BlockSpec(memory_space=pltpu.VMEM),
-    )(y)
-
+    )(packed_weights, scaling, start)
 
 def distributed(start, tiles, pattern, counts):
     nb_dev = tiles.shape[0]
@@ -156,7 +173,6 @@
     half = lax.all_to_all(copies, ("row", "col"), 0, 0, tiled=True)
     copies = jnp.broadcast_to(half[None], (2,) + half.shape)
     whole = lax.all_to_all(copies, "vec", 0, 0, tiled=True).reshape(total_rows, total_rows + 256)
-    weights = whole[:, :total_rows]
     extras = whole[:, total_rows:]
     scaling = (
         extras[:, nb_dev * share].astype(jnp.float32) + extras[:, nb_dev * share + 1].astype(jnp.float32)
@@ -166,14 +182,7 @@
     coded = coded[:, :, :, 0] + coded[:, :, :, 1]
     current = coded.transpose(0, 3, 4, 1, 2, 5).reshape(cols, total_rows)
 
-    def apply_dense(values):
-        product = jnp.einsum(
-            "cj,ij->ci", values.astype(jnp.bfloat16), weights, preferred_element_type=jnp.float32
-        )
-        return product * scaling
-
-    for outer in range(ITERS):
-        current = orthonormal_local(chebyshev(current, apply_dense))
+    current = filter_local(whole, scaling, current)
     mine = current.reshape(cols, nb_dev, n_row, block)
     mine = lax.dynamic_index_in_dim(mine, row_index, 2, keepdims=False).reshape(cols, nb_dev * block)
     current = lax.dynamic_slice_in_dim(mine, vec_index * vec_cols, vec_cols, 0)

time: 109 us -> 95.6 us (0.88)
  matrix products: 22.8 us -> 0.39 us
  Pallas kernels: 17.8 us -> 26.3 us
  other arithmetic: 4.26 us -> 5.45 us
    dot_general x14 -> x0, matrix products: 22.4 us -> none  [apply_dense(): jnp.einsum('cj,ij->ci', values.astype(jnp.bfloat16), weights, preferred_e...]
    pallas_call x2 -> x1, Pallas kernels: 17.8 us -> 26.3 us  [filter_local(): pl.pallas_call(filter_kernel, out_shape=jax.ShapeDtypeStruct(start.shape,...]
where the time goes in v5:
time: 95.6 us; the launch traced here: 95.2 us
  waiting for transfers between devices  39.3 us (41%)
  Pallas kernels  26.3 us (28%)
  starting transfers between devices  9.33 us (10%)
  local copies, waits for them, and re-layouts  7.82 us (8%)
  blocking collectives  5.84 us (6%)
  other arithmetic  5.45 us (6%)
    all_to_all x1, waiting for transfers between devices, replicated(): half = lax.all_to_all(copies, ('row', 'col'), 0, 0, tiled=True)  30.8 us
    pallas_call x1, Pallas kernels, filter_local(): pl.pallas_call(filter_kernel, out_shape=jax.ShapeDtypeStruct(start.shape,...  26.3 us
    all_to_all x1, waiting for transfers between devices, replicated(): summed = jnp.sum(lax.all_to_all(chunks, 'col', 0, 0, tiled=True), axis=0)  8.5 us
    all_to_all x1, blocking collectives, replicated(): lax.all_to_all(copies, 'vec', 0, 0, tiled=True)  5.84 us
    all_to_all x1, starting transfers between devices, replicated(): half = lax.all_to_all(copies, ('row', 'col'), 0, 0, tiled=True)  5.13 us
    all_to_all x1, starting transfers between devices, replicated(): summed = jnp.sum(lax.all_to_all(chunks, 'col', 0, 0, tiled=True), axis=0)  4.21 us
  transfers between devices with their start and end apart: 2, of which 2 were waited for; matrix products, arithmetic and copies ran while one was open for 0% of the time, Pallas kernels for 0%

profile of v5, /device:TPU:0, one launch (start us, length us, event | category | flops | bytes accessed | tf_op | source)
XLA Modules:
  0.0 95.2 jit_solution(41896854773090595)
XLA Ops:
  0.0 1.3 %dynamic_slice.28 = s32[1]{0:T(128)} dynamic-slice(s32[2]{0:T(128)} %param.7, s32[]{:T(128)S(6)} %select_n.45), dynamic_slice_sizes={1} | dynamic-slice | bytes 12 | tf_op jit(solution)/shard_map/jit(dynamic_index_in_dim)/dynamic_slice | solution.py:143
  1.3 0.7 fusion.12
  2.1 1.3 %fusion = f32[128]{0:T(128)S(1)} fusion(bf16[1,16,128,128]{3,2,1,0:T(8,128)(2,1)S(1)} %constant_dynamic-slice_fusion.2, bf16[16]{0:T(256)(128)(2,1)S(1)} %get-tuple-element.9), kind=kLoop, calls=%fused_computation.2 | loop fusion | flops 1048448 | bytes 524832 | tf_op jit(solution)/shard_map/kmn,kmn->m/dot_general | solution.py:152
  3.3 0.8 fusion.11
  4.1 0.4 convolution_bitcast_fusion
  4.7 0.9 pad_maximum_fusion
  5.6 4.2 %all-to-all-start = ((f32[2,64,1152]{2,1,0:T(8,128)}), f32[2,64,1152]{2,1,0:T(8,128)S(1)}, u32[]{:S(2)}, u32[]{:S(2)}) async-start(f32[2,64,1152]{2,1,0:T(8,128)} %pad_maximum_fusion), calls=%async_computation | async-start | bytes 1179648 | tf_op jit(solution)/shard_map/all_to_all | solution.py:156
  10.7 8.5 %all-to-all-done = f32[2,64,1152]{2,1,0:T(8,128)S(1)} async-done(((f32[2,64,1152]{2,1,0:T(8,128)}), f32[2,64,1152]{2,1,0:T(8,128)S(1)}, u32[]{:S(2)}, u32[]{:S(2)}) %all-to-all-start) | async-done | bytes 589856 | tf_op jit(solution)/shard_map/all_to_all | solution.py:156
  19.4 0.1 copy.19
  19.5 0.1 copy.18
  19.8 1.1 %broadcast_in_dim.13 = bf16[8,64,1280]{2,1,0:T(8,128)(2,1)} broadcast(bf16[64,1280]{1,0:T(8,128)(2,1)S(1)} %concatenate.15), dimensions={1,2} | broadcast | bytes 1474560 | tf_op jit(solution)/shard_map/broadcast_in_dim | solution.py:172
  20.9 5.1 %all-to-all-start.1 = ((bf16[8,64,1280]{2,1,0:T(8,128)(2,1)}), bf16[8,64,1280]{2,1,0:T(8,128)(2,1)S(1)}, u32[]{:S(2)}, u32[]{:S(2)}) async-start(bf16[8,64,1280]{2,1,0:T(8,128)(2,1)} %broadcast_in_dim.13), calls=%async_computation.1 | async-start | bytes 2621440 | tf_op jit(solution)/shard_map/all_to_all | solution.py:173
  26.0 30.8 %all-to-all-done.1 = bf16[8,64,1280]{2,1,0:T(8,128)(2,1)S(1)} async-done(((bf16[8,64,1280]{2,1,0:T(8,128)(2,1)}), bf16[8,64,1280]{2,1,0:T(8,128)(2,1)S(1)}, u32[]{:S(2)}, u32[]{:S(2)}) %all-to-all-start.1) | async-done | bytes 1310752 | tf_op jit(solution)/shard_map/all_to_all | solution.py:173
  56.8 0.2 broadcast_in_dim.14
  57.1 5.8 %all_to_all.15 = bf16[2,8,64,1280]{3,2,1,0:T(8,128)(2,1)S(1)} all-to-all(bf16[2,8,64,1280]{3,2,1,0:T(8,128)(2,1)S(1)} %broadcast_in_dim.14), channel_id=1, replica_groups=mesh['grp'=2,'row'=4,'col'=2,'vec'=2] {'vec'}, dimensions={0} | all-to-all | bytes 5242880 | tf_op jit(solution)/shard_map/all_to_all | solution.py:175
  62.9 1.1 %add_reduce_fusion = f32[1024]{0:T(1024)} fusion(bf16[1024,1280]{1,0:T(8,128)(2,1)S(1)} %bitcast.42), kind=kLoop, calls=%fused_computation.9 | loop fusion | flops 3072 | bytes 8192 | tf_op jit(solution)/shard_map/add | solution.py:178
  64.0 0.4 copy-done.1
  64.5 0.6 reshape.136
  65.2 0.7 fusion.1
  65.9 1.2 %reshape.132.y_ref = f32[64,1024]{1,0:T(8,128)} reshape(f32[2,32,2,4,2,64]{5,4,3,2,1,0:T(2,128)S(1)} %fusion.1) | data formatting | bytes 524288 | tf_op jit(solution)/shard_map/reshape | solution.py:183
  67.0 26.3 %shard_map.46 = f32[64,1024]{1,0:T(8,128)} custom-call(bf16[1024,1280]{1,0:T(8,128)(2,1)} %bitcast.44, f32[1,1024]{1,0:T(1,128)} %bitcast.47, f32[64,1024]{1,0:T(8,128)} %reshape.132.y_ref), custom_call_target="tpu_custom_call" | custom-call | tf_op jit(solution)/shard_map/pallas_call | solution.py:82
  93.3 1.1 %reshape.133 = f32[64,2,4,128]{3,2,1,0:T(4,128)S(1)} reshape(f32[64,1024]{1,0:T(8,128)} %shard_map.46) | data formatting | bytes 524288 | tf_op jit(solution)/shard_map/reshape | solution.py:186
  94.4 0.2 dynamic-slice_reduce_fusion
  94.6 0.6 constant_dynamic-slice_fusion
  (24 shorter events, 0.9 us)
Async XLA Ops:
  0.0 2.0 %copy-start = (bf16[2,16,128,128]{3,2,1,0:T(8,128)(2,1)S(1)}, bf16[2,16,128,128]{3,2,1,0:T(8,128)(2,1)}, u32[]{:S(2)}) copy-start(bf16[2,16,128,128]{3,2,1,0:T(8,128)(2,1)} %param.5) | copy-start | bytes 3145732
  2.0 8.5 %copy-start.2 = (f32[32,256]{1,0:T(8,128)S(1)}, f32[32,256]{1,0:T(8,128)}, u32[]{:S(2)}) copy-start(f32[32,256]{1,0:T(8,128)} %param.4) | copy-start | bytes 98308
  5.6 13.6 %all-to-all-start = ((f32[2,64,1152]{2,1,0:T(8,128)}), f32[2,64,1152]{2,1,0:T(8,128)S(1)}, u32[]{:S(2)}, u32[]{:S(2)}) async-start(f32[2,64,1152]{2,1,0:T(8,128)} %pad_maximum_fusion), calls=%async_computation | async-start | bytes 1179648 | tf_op jit(solution)/shard_map/all_to_all | solution.py:156
  20.9 35.9 %all-to-all-start.1 = ((bf16[8,64,1280]{2,1,0:T(8,128)(2,1)}), bf16[8,64,1280]{2,1,0:T(8,128)(2,1)S(1)}, u32[]{:S(2)}, u32[]{:S(2)}) async-start(bf16[8,64,1280]{2,1,0:T(8,128)(2,1)} %broadcast_in_dim.13), calls=%async_computation.1 | async-start | bytes 2621440 | tf_op jit(solution)/shard_map/all_to_all | solution.py:173
  62.9 1.5 %copy-start.1 = (bf16[2,8,64,1280]{3,2,1,0:T(8,128)(2,1)}, bf16[2,8,64,1280]{3,2,1,0:T(8,128)(2,1)S(1)}, u32[]{:S(2)}) copy-start(bf16[2,8,64,1280]{3,2,1,0:T(8,128)(2,1)S(1)} %all_to_all.15) | copy-start | bytes 7864324

commit v6 on v5

--- a/solution.py
+++ b/solution.py
@@ -46,14 +46,15 @@
     rows = lax.broadcasted_iota(jnp.int32, (n, n), 0)
     cols = lax.broadcasted_iota(jnp.int32, (n, n), 1)
     inverse = (rows == cols).astype(jnp.float32)
+    diagonal = jnp.zeros((n, 1), jnp.float32)
     for k in range(n):
-        pivot = jnp.sqrt(a[k : k + 1, k : k + 1])
-        down = jnp.where(rows[:, k : k + 1] >= k, a[:, k : k + 1] / pivot, 0.0)
-        across = jnp.where(cols[k : k + 1, :] >= k, a[k : k + 1, :] / pivot, 0.0)
+        pivot = a[k : k + 1, k : k + 1]
+        down = jnp.where(rows[:, k : k + 1] > k, a[:, k : k + 1] * (1.0 / pivot), 0.0)
+        across = jnp.where(cols[k : k + 1, :] > k, a[k : k + 1, :], 0.0)
         a = a - down * across
-        solved = inverse[k : k + 1, :] / pivot
-        below = jnp.where(rows[:, k : k + 1] > k, down, 0.0)
-        inverse = jnp.where(rows == k, solved, inverse - below * solved)
+        inverse = inverse - down * inverse[k : k + 1, :]
+        diagonal = jnp.where(rows[:, :1] == k, pivot, diagonal)
+    inverse = inverse / jnp.sqrt(diagonal)
     return lax.dot_general(
         inverse, y, (((1,), (0,)), ((), ())), precision=hi, preferred_element_type=jnp.float32
     )
@@ -119,9 +120,8 @@
 
 
 def split_bf16(values):
-    high = values.astype(jnp.bfloat16)
-    low = (values - high.astype(jnp.float32)).astype(jnp.bfloat16)
-    return high, low
+    rounded = lax.reduce_precision(values, exponent_bits=8, mantissa_bits=7)
+    return rounded.astype(jnp.bfloat16), (values - rounded).astype(jnp.bfloat16)
 
 
 def replicated(start, tiles, pattern, counts):

time: 95.6 us -> 94.8 us (level)
  no operation moved by 1% of the time
where the time goes in v6:
time: 94.8 us; the launch traced here: 94.4 us
  waiting for transfers between devices  39.3 us (41%)
  Pallas kernels  25.5 us (27%)
  starting transfers between devices  9.33 us (10%)
  local copies, waits for them, and re-layouts  7.82 us (8%)
  blocking collectives  5.84 us (6%)
  other arithmetic  5.47 us (6%)
    all_to_all x1, waiting for transfers between devices, replicated(): half = lax.all_to_all(copies, ('row', 'col'), 0, 0, tiled=True)  30.8 us
    pallas_call x1, Pallas kernels, filter_local(): pl.pallas_call(filter_kernel, out_shape=jax.ShapeDtypeStruct(start.shape,...  25.5 us
    all_to_all x1, waiting for transfers between devices, replicated(): summed = jnp.sum(lax.all_to_all(chunks, 'col', 0, 0, tiled=True), axis=0)  8.49 us
    all_to_all x1, blocking collectives, replicated(): lax.all_to_all(copies, 'vec', 0, 0, tiled=True)  5.84 us
    all_to_all x1, starting transfers between devices, replicated(): half = lax.all_to_all(copies, ('row', 'col'), 0, 0, tiled=True)  5.13 us
    all_to_all x1, starting transfers between devices, replicated(): summed = jnp.sum(lax.all_to_all(chunks, 'col', 0, 0, tiled=True), axis=0)  4.21 us
  transfers between devices with their start and end apart: 2, of which 2 were waited for; matrix products, arithmetic and copies ran while one was open for 0% of the time, Pallas kernels for 0%

profile of v6, /device:TPU:0, one launch (start us, length us, event | category | flops | bytes accessed | tf_op | source)
XLA Modules:
  0.0 94.4 jit_solution(8166740553379501454)
XLA Ops:
  0.0 1.3 %dynamic_slice.28 = s32[1]{0:T(128)} dynamic-slice(s32[2]{0:T(128)} %param.7, s32[]{:T(128)S(6)} %select_n.45), dynamic_slice_sizes={1} | dynamic-slice | bytes 12 | tf_op jit(solution)/shard_map/jit(dynamic_index_in_dim)/dynamic_slice | solution.py:143
  1.3 0.7 fusion.14
  2.1 1.3 %fusion = f32[128]{0:T(128)S(1)} fusion(bf16[1,16,128,128]{3,2,1,0:T(8,128)(2,1)S(1)} %constant_dynamic-slice_fusion.2, bf16[16]{0:T(256)(128)(2,1)S(1)} %get-tuple-element.7), kind=kLoop, calls=%fused_computation.2 | loop fusion | flops 1048448 | bytes 524832 | tf_op jit(solution)/shard_map/kmn,kmn->m/dot_general | solution.py:152
  3.3 0.8 fusion.13
  4.1 0.4 convolution_bitcast_fusion
  4.7 0.9 pad_maximum_fusion
  5.6 4.2 %all-to-all-start = ((f32[2,64,1152]{2,1,0:T(8,128)}), f32[2,64,1152]{2,1,0:T(8,128)S(1)}, u32[]{:S(2)}, u32[]{:S(2)}) async-start(f32[2,64,1152]{2,1,0:T(8,128)} %pad_maximum_fusion), calls=%async_computation | async-start | bytes 1179648 | tf_op jit(solution)/shard_map/all_to_all | solution.py:156
  10.8 8.5 %all-to-all-done = f32[2,64,1152]{2,1,0:T(8,128)S(1)} async-done(((f32[2,64,1152]{2,1,0:T(8,128)}), f32[2,64,1152]{2,1,0:T(8,128)S(1)}, u32[]{:S(2)}, u32[]{:S(2)}) %all-to-all-start) | async-done | bytes 589856 | tf_op jit(solution)/shard_map/all_to_all | solution.py:156
  19.4 0.1 copy.18
  19.5 0.1 copy.19
  19.8 1.1 %broadcast_in_dim.13 = bf16[8,64,1280]{2,1,0:T(8,128)(2,1)} broadcast(bf16[64,1280]{1,0:T(8,128)(2,1)S(1)} %concatenate.15), dimensions={1,2} | broadcast | bytes 1474560 | tf_op jit(solution)/shard_map/broadcast_in_dim | solution.py:172
  20.9 5.1 %all-to-all-start.1 = ((bf16[8,64,1280]{2,1,0:T(8,128)(2,1)}), bf16[8,64,1280]{2,1,0:T(8,128)(2,1)S(1)}, u32[]{:S(2)}, u32[]{:S(2)}) async-start(bf16[8,64,1280]{2,1,0:T(8,128)(2,1)} %broadcast_in_dim.13), calls=%async_computation.1 | async-start | bytes 2621440 | tf_op jit(solution)/shard_map/all_to_all | solution.py:173
  26.0 30.8 %all-to-all-done.1 = bf16[8,64,1280]{2,1,0:T(8,128)(2,1)S(1)} async-done(((bf16[8,64,1280]{2,1,0:T(8,128)(2,1)}), bf16[8,64,1280]{2,1,0:T(8,128)(2,1)S(1)}, u32[]{:S(2)}, u32[]{:S(2)}) %all-to-all-start.1) | async-done | bytes 1310752 | tf_op jit(solution)/shard_map/all_to_all | solution.py:173
  56.8 0.2 broadcast_in_dim.14
  57.1 5.8 %all_to_all.15 = bf16[2,8,64,1280]{3,2,1,0:T(8,128)(2,1)S(1)} all-to-all(bf16[2,8,64,1280]{3,2,1,0:T(8,128)(2,1)S(1)} %broadcast_in_dim.14), channel_id=1, replica_groups=mesh['grp'=2,'row'=4,'col'=2,'vec'=2] {'vec'}, dimensions={0} | all-to-all | bytes 5242880 | tf_op jit(solution)/shard_map/all_to_all | solution.py:175
  62.9 1.1 %add_reduce_fusion = f32[1024]{0:T(1024)} fusion(bf16[1024,1280]{1,0:T(8,128)(2,1)S(1)} %bitcast.42), kind=kLoop, calls=%fused_computation.9 | loop fusion | flops 3072 | bytes 8192 | tf_op jit(solution)/shard_map/add | solution.py:178
  64.1 0.4 copy-done.1
  64.5 0.6 reshape.136
  65.2 0.7 fusion.1
  65.9 1.2 %reshape.132.y_ref = f32[64,1024]{1,0:T(8,128)} reshape(f32[2,32,2,4,2,64]{5,4,3,2,1,0:T(2,128)S(1)} %fusion.1) | data formatting | bytes 524288 | tf_op jit(solution)/shard_map/reshape | solution.py:183
  67.1 25.5 %shard_map.46 = f32[64,1024]{1,0:T(8,128)} custom-call(bf16[1024,1280]{1,0:T(8,128)(2,1)} %bitcast.44, f32[1,1024]{1,0:T(1,128)} %bitcast.47, f32[64,1024]{1,0:T(8,128)} %reshape.132.y_ref), custom_call_target="tpu_custom_call" | custom-call | tf_op jit(solution)/shard_map/pallas_call | solution.py:83
  92.5 1.1 %reshape.133 = f32[64,2,4,128]{3,2,1,0:T(4,128)S(1)} reshape(f32[64,1024]{1,0:T(8,128)} %shard_map.46) | data formatting | bytes 524288 | tf_op jit(solution)/shard_map/reshape | solution.py:186
  93.6 0.2 dynamic-slice_reduce_fusion
  93.8 0.6 constant_dynamic-slice_fusion
  (25 shorter events, 0.9 us)
Async XLA Ops:
  0.0 2.0 %copy-start = (bf16[2,16,128,128]{3,2,1,0:T(8,128)(2,1)S(1)}, bf16[2,16,128,128]{3,2,1,0:T(8,128)(2,1)}, u32[]{:S(2)}) copy-start(bf16[2,16,128,128]{3,2,1,0:T(8,128)(2,1)} %param.5) | copy-start | bytes 3145732
  2.0 8.5 %copy-start.2 = (f32[32,256]{1,0:T(8,128)S(1)}, f32[32,256]{1,0:T(8,128)}, u32[]{:S(2)}) copy-start(f32[32,256]{1,0:T(8,128)} %param.4) | copy-start | bytes 98308
  5.6 13.6 %all-to-all-start = ((f32[2,64,1152]{2,1,0:T(8,128)}), f32[2,64,1152]{2,1,0:T(8,128)S(1)}, u32[]{:S(2)}, u32[]{:S(2)}) async-start(f32[2,64,1152]{2,1,0:T(8,128)} %pad_maximum_fusion), calls=%async_computation | async-start | bytes 1179648 | tf_op jit(solution)/shard_map/all_to_all | solution.py:156
  20.9 35.9 %all-to-all-start.1 = ((bf16[8,64,1280]{2,1,0:T(8,128)(2,1)}), bf16[8,64,1280]{2,1,0:T(8,128)(2,1)S(1)}, u32[]{:S(2)}, u32[]{:S(2)}) async-start(bf16[8,64,1280]{2,1,0:T(8,128)(2,1)} %broadcast_in_dim.13), calls=%async_computation.1 | async-start | bytes 2621440 | tf_op jit(solution)/shard_map/all_to_all | solution.py:173
  62.9 1.5 %copy-start.1 = (bf16[2,8,64,1280]{3,2,1,0:T(8,128)(2,1)}, bf16[2,8,64,1280]{3,2,1,0:T(8,128)(2,1)S(1)}, u32[]{:S(2)}) copy-start(bf16[2,8,64,1280]{3,2,1,0:T(8,128)(2,1)S(1)} %all_to_all.15) | copy-start | bytes 7864324

commit v7 on v6

--- a/solution.py
+++ b/solution.py
@@ -48,11 +48,17 @@
     inverse = (rows == cols).astype(jnp.float32)
     diagonal = jnp.zeros((n, 1), jnp.float32)
     for k in range(n):
+        top = (k // 8) * 8
         pivot = a[k : k + 1, k : k + 1]
-        down = jnp.where(rows[:, k : k + 1] > k, a[:, k : k + 1] * (1.0 / pivot), 0.0)
+        down = jnp.where(rows[top:, k : k + 1] > k, a[top:, k : k + 1] * (1.0 / pivot), 0.0)
         across = jnp.where(cols[k : k + 1, :] > k, a[k : k + 1, :], 0.0)
-        a = a - down * across
-        inverse = inverse - down * inverse[k : k + 1, :]
+        lower_a = a[top:] - down * across
+        lower_inverse = inverse[top:] - down * inverse[k : k + 1, :]
+        if top:
+            a = jnp.concatenate([a[:top], lower_a], axis=0)
+            inverse = jnp.concatenate([inverse[:top], lower_inverse], axis=0)
+        else:
+            a, inverse = lower_a, lower_inverse
         diagonal = jnp.where(rows[:, :1] == k, pivot, diagonal)
     inverse = inverse / jnp.sqrt(diagonal)
     return lax.dot_general(

time: 94.8 us -> 94.2 us (level)
  no operation moved by 1% of the time
where the time goes in v7:
time: 94.2 us; the launch traced here: 93.9 us
  waiting for transfers between devices  39.3 us (42%)
  Pallas kernels  24.9 us (26%)
  starting transfers between devices  9.33 us (10%)
  local copies, waits for them, and re-layouts  7.82 us (8%)
  blocking collectives  5.84 us (6%)
  other arithmetic  5.47 us (6%)
    all_to_all x1, waiting for transfers between devices, replicated(): half = lax.all_to_all(copies, ('row', 'col'), 0, 0, tiled=True)  30.8 us
    pallas_call x1, Pallas kernels, filter_local(): pl.pallas_call(filter_kernel, out_shape=jax.ShapeDtypeStruct(start.shape,...  24.9 us
    all_to_all x1, waiting for transfers between devices, replicated(): summed = jnp.sum(lax.all_to_all(chunks, 'col', 0, 0, tiled=True), axis=0)  8.49 us
    all_to_all x1, blocking collectives, replicated(): lax.all_to_all(copies, 'vec', 0, 0, tiled=True)  5.84 us
    all_to_all x1, starting transfers between devices, replicated(): half = lax.all_to_all(copies, ('row', 'col'), 0, 0, tiled=True)  5.13 us
    all_to_all x1, starting transfers between devices, replicated(): summed = jnp.sum(lax.all_to_all(chunks, 'col', 0, 0, tiled=True), axis=0)  4.21 us
  transfers between devices with their start and end apart: 2, of which 2 were waited for; matrix products, arithmetic and copies ran while one was open for 0% of the time, Pallas kernels for 0%

profile of v7, /device:TPU:0, one launch (start us, length us, event | category | flops | bytes accessed | tf_op | source)
XLA Modules:
  0.0 93.9 jit_solution(7241864502537020696)
XLA Ops:
  0.0 1.3 %dynamic_slice.28 = s32[1]{0:T(128)} dynamic-slice(s32[2]{0:T(128)} %param.7, s32[]{:T(128)S(6)} %select_n.45), dynamic_slice_sizes={1} | dynamic-slice | bytes 12 | tf_op jit(solution)/shard_map/jit(dynamic_index_in_dim)/dynamic_slice | solution.py:149
  1.3 0.7 fusion.14
  2.1 1.3 %fusion = f32[128]{0:T(128)S(1)} fusion(bf16[1,16,128,128]{3,2,1,0:T(8,128)(2,1)S(1)} %constant_dynamic-slice_fusion.2, bf16[16]{0:T(256)(128)(2,1)S(1)} %get-tuple-element.7), kind=kLoop, calls=%fused_computation.2 | loop fusion | flops 1048448 | bytes 524832 | tf_op jit(solution)/shard_map/kmn,kmn->m/dot_general | solution.py:158
  3.3 0.8 fusion.13
  4.1 0.4 convolution_bitcast_fusion
  4.7 0.9 pad_maximum_fusion
  5.6 4.2 %all-to-all-start = ((f32[2,64,1152]{2,1,0:T(8,128)}), f32[2,64,1152]{2,1,0:T(8,128)S(1)}, u32[]{:S(2)}, u32[]{:S(2)}) async-start(f32[2,64,1152]{2,1,0:T(8,128)} %pad_maximum_fusion), calls=%async_computation | async-start | bytes 1179648 | tf_op jit(solution)/shard_map/all_to_all | solution.py:162
  10.8 8.5 %all-to-all-done = f32[2,64,1152]{2,1,0:T(8,128)S(1)} async-done(((f32[2,64,1152]{2,1,0:T(8,128)}), f32[2,64,1152]{2,1,0:T(8,128)S(1)}, u32[]{:S(2)}, u32[]{:S(2)}) %all-to-all-start) | async-done | bytes 589856 | tf_op jit(solution)/shard_map/all_to_all | solution.py:162
  19.4 0.1 copy.18
  19.5 0.1 copy.19
  19.8 1.1 %broadcast_in_dim.13 = bf16[8,64,1280]{2,1,0:T(8,128)(2,1)} broadcast(bf16[64,1280]{1,0:T(8,128)(2,1)S(1)} %concatenate.15), dimensions={1,2} | broadcast | bytes 1474560 | tf_op jit(solution)/shard_map/broadcast_in_dim | solution.py:178
  20.9 5.1 %all-to-all-start.1 = ((bf16[8,64,1280]{2,1,0:T(8,128)(2,1)}), bf16[8,64,1280]{2,1,0:T(8,128)(2,1)S(1)}, u32[]{:S(2)}, u32[]{:S(2)}) async-start(bf16[8,64,1280]{2,1,0:T(8,128)(2,1)} %broadcast_in_dim.13), calls=%async_computation.1 | async-start | bytes 2621440 | tf_op jit(solution)/shard_map/all_to_all | solution.py:179
  26.0 30.8 %all-to-all-done.1 = bf16[8,64,1280]{2,1,0:T(8,128)(2,1)S(1)} async-done(((bf16[8,64,1280]{2,1,0:T(8,128)(2,1)}), bf16[8,64,1280]{2,1,0:T(8,128)(2,1)S(1)}, u32[]{:S(2)}, u32[]{:S(2)}) %all-to-all-start.1) | async-done | bytes 1310752 | tf_op jit(solution)/shard_map/all_to_all | solution.py:179
  56.8 0.2 broadcast_in_dim.14
  57.1 5.8 %all_to_all.15 = bf16[2,8,64,1280]{3,2,1,0:T(8,128)(2,1)S(1)} all-to-all(bf16[2,8,64,1280]{3,2,1,0:T(8,128)(2,1)S(1)} %broadcast_in_dim.14), channel_id=1, replica_groups=mesh['grp'=2,'row'=4,'col'=2,'vec'=2] {'vec'}, dimensions={0} | all-to-all | bytes 5242880 | tf_op jit(solution)/shard_map/all_to_all | solution.py:181
  62.9 1.1 %add_reduce_fusion = f32[1024]{0:T(1024)} fusion(bf16[1024,1280]{1,0:T(8,128)(2,1)S(1)} %bitcast.42), kind=kLoop, calls=%fused_computation.9 | loop fusion | flops 3072 | bytes 8192 | tf_op jit(solution)/shard_map/add | solution.py:184
  64.1 0.4 copy-done.1
  64.5 0.6 reshape.136
  65.2 0.7 fusion.1
  65.9 1.2 %reshape.132.y_ref = f32[64,1024]{1,0:T(8,128)} reshape(f32[2,32,2,4,2,64]{5,4,3,2,1,0:T(2,128)S(1)} %fusion.1) | data formatting | bytes 524288 | tf_op jit(solution)/shard_map/reshape | solution.py:189
  67.1 24.9 %shard_map.46 = f32[64,1024]{1,0:T(8,128)} custom-call(bf16[1024,1280]{1,0:T(8,128)(2,1)} %bitcast.44, f32[1,1024]{1,0:T(1,128)} %bitcast.47, f32[64,1024]{1,0:T(8,128)} %reshape.132.y_ref), custom_call_target="tpu_custom_call" | custom-call | tf_op jit(solution)/shard_map/pallas_call | solution.py:89
  91.9 1.1 %reshape.133 = f32[64,2,4,128]{3,2,1,0:T(4,128)S(1)} reshape(f32[64,1024]{1,0:T(8,128)} %shard_map.46) | data formatting | bytes 524288 | tf_op jit(solution)/shard_map/reshape | solution.py:192
  93.0 0.2 dynamic-slice_reduce_fusion
  93.2 0.6 constant_dynamic-slice_fusion
  (25 shorter events, 0.9 us)
Async XLA Ops:
  0.0 2.0 %copy-start = (bf16[2,16,128,128]{3,2,1,0:T(8,128)(2,1)S(1)}, bf16[2,16,128,128]{3,2,1,0:T(8,128)(2,1)}, u32[]{:S(2)}) copy-start(bf16[2,16,128,128]{3,2,1,0:T(8,128)(2,1)} %param.5) | copy-start | bytes 3145732
  2.0 8.5 %copy-start.2 = (f32[32,256]{1,0:T(8,128)S(1)}, f32[32,256]{1,0:T(8,128)}, u32[]{:S(2)}) copy-start(f32[32,256]{1,0:T(8,128)} %param.4) | copy-start | bytes 98308
  5.6 13.6 %all-to-all-start = ((f32[2,64,1152]{2,1,0:T(8,128)}), f32[2,64,1152]{2,1,0:T(8,128)S(1)}, u32[]{:S(2)}, u32[]{:S(2)}) async-start(f32[2,64,1152]{2,1,0:T(8,128)} %pad_maximum_fusion), calls=%async_computation | async-start | bytes 1179648 | tf_op jit(solution)/shard_map/all_to_all | solution.py:162
  20.9 35.9 %all-to-all-start.1 = ((bf16[8,64,1280]{2,1,0:T(8,128)(2,1)}), bf16[8,64,1280]{2,1,0:T(8,128)(2,1)S(1)}, u32[]{:S(2)}, u32[]{:S(2)}) async-start(bf16[8,64,1280]{2,1,0:T(8,128)(2,1)} %broadcast_in_dim.13), calls=%async_computation.1 | async-start | bytes 2621440 | tf_op jit(solution)/shard_map/all_to_all | solution.py:179
  62.9 1.5 %copy-start.1 = (bf16[2,8,64,1280]{3,2,1,0:T(8,128)(2,1)}, bf16[2,8,64,1280]{3,2,1,0:T(8,128)(2,1)S(1)}, u32[]{:S(2)}) copy-start(bf16[2,8,64,1280]{3,2,1,0:T(8,128)(2,1)S(1)} %all_to_all.15) | copy-start | bytes 7864324

commit v8 on v7

--- a/solution.py
+++ b/solution.py
@@ -66,9 +66,8 @@
     )
 
 
-def filter_kernel(w_ref, s_ref, y_ref, x_ref):
+def filter_kernel(w_ref, y_ref, x_ref):
     total = y_ref.shape[1]
-    scaling = s_ref[...]
 
     def apply(values):
         product = lax.dot_general(
@@ -77,7 +76,7 @@
             (((1,), (1,)), ((), ())),
             preferred_element_type=jnp.float32,
         )
-        return product * scaling
+        return product
 
     current = y_ref[...]
     for outer in range(ITERS):
@@ -85,13 +84,13 @@
     x_ref[...] = current
 
 
-def filter_local(packed_weights, scaling, start):
+def filter_local(packed_weights, start):
     return pl.pallas_call(
         filter_kernel,
         out_shape=jax.ShapeDtypeStruct(start.shape, jnp.float32),
-        in_specs=[pl.BlockSpec(memory_space=pltpu.VMEM)] * 3,
+        in_specs=[pl.BlockSpec(memory_space=pltpu.VMEM)] * 2,
         out_specs=pl.BlockSpec(memory_space=pltpu.VMEM),
-    )(packed_weights, scaling, start)
+    )(packed_weights, start)
 
 def distributed(start, tiles, pattern, counts):
     nb_dev = tiles.shape[0]
@@ -163,32 +162,26 @@
 
     entries = (own_count * block).astype(jnp.float32)
     scale = lax.rsqrt(summed[:, total_rows] / entries + EPSILON) / jnp.sqrt(entries) / HALF_WIDTH
-    scale_hi, scale_lo = split_bf16(scale)
 
     piece = start.reshape(vec_cols, nb_dev, block)
     piece = lax.dynamic_slice_in_dim(piece, col_index * share, share, 2).reshape(vec_cols, nb_dev * share)
     start_hi, start_lo = split_bf16(piece)
     extra = jnp.concatenate([start_hi, start_lo], axis=0)
-    extra = jnp.concatenate(
-        [extra, scale_hi[:, None], scale_lo[:, None], jnp.zeros((share, 126), jnp.bfloat16)], axis=1
-    )
-    rows_bf16 = summed[:, :total_rows].astype(jnp.bfloat16)
+    extra = jnp.concatenate([extra, jnp.zeros((share, 128 - nb_dev * share), jnp.bfloat16)], axis=1)
+    rows_bf16 = (summed[:, :total_rows] * scale[:, None]).astype(jnp.bfloat16)
 
     packed = jnp.concatenate([rows_bf16, extra], axis=1)
     copies = jnp.broadcast_to(packed[None], (n_row * n_col,) + packed.shape)
     half = lax.all_to_all(copies, ("row", "col"), 0, 0, tiled=True)
     copies = jnp.broadcast_to(half[None], (2,) + half.shape)
-    whole = lax.all_to_all(copies, "vec", 0, 0, tiled=True).reshape(total_rows, total_rows + 256)
+    whole = lax.all_to_all(copies, "vec", 0, 0, tiled=True).reshape(total_rows, total_rows + 128)
     extras = whole[:, total_rows:]
-    scaling = (
-        extras[:, nb_dev * share].astype(jnp.float32) + extras[:, nb_dev * share + 1].astype(jnp.float32)
-    )[None, :]
     coded = extras[:, : nb_dev * share].astype(jnp.float32)
     coded = coded.reshape(2, n_row, n_col, 2, vec_cols, nb_dev, share)
     coded = coded[:, :, :, 0] + coded[:, :, :, 1]
     current = coded.transpose(0, 3, 4, 1, 2, 5).reshape(cols, total_rows)
 
-    current = filter_local(whole, scaling, current)
+    current = filter_local(whole, current)
     mine = current.reshape(cols, nb_dev, n_row, block)
     mine = lax.dynamic_index_in_dim(mine, row_index, 2, keepdims=False).reshape(cols, nb_dev * block)
     current = lax.dynamic_slice_in_dim(mine, vec_index * vec_cols, vec_cols, 0)

time: 94.2 us -> 95.5 us (1.014)
  local copies, waits for them, and re-layouts: 7.82 us -> 11.5 us
  waiting for transfers between devices: 39.3 us -> 36.5 us
    all_to_all x1, waiting for transfers between devices: 30.8 us -> 28 us  [replicated(): half = lax.all_to_all(copies, ('row', 'col'), 0, 0, tiled=True)]
    reshape x1, local copies, waits for them, and re-layouts: 0.61 us -> 2.7 us  [replicated(): coded = coded.reshape(2, n_row, n_col, 2, vec_cols, nb_dev, share)]
    slice x1, local copies, waits for them, and re-layouts: 0.1 us -> 1.27 us  [replicated(): coded = coded[:, :, :, 0] + coded[:, :, :, 1]]
    add x1 -> x0, other arithmetic: 1.14 us -> none  [replicated(): extras[:, nb_dev * share].astype(jnp.float32)]
    reshape x1, local copies, waits for them, and re-layouts: 1.17 us -> 2.24 us  [replicated(): current = coded.transpose(0, 3, 4, 1, 2, 5).reshape(cols, total_rows)]
where the time goes in v8:
time: 95.5 us; the launch traced here: 95 us
  waiting for transfers between devices  36.5 us (38%)
  Pallas kernels  24.8 us (26%)
  local copies, waits for them, and re-layouts  11.5 us (12%)
  starting transfers between devices  9.33 us (10%)
  other arithmetic  6.1 us (6%)
  blocking collectives  5.63 us (6%)
    all_to_all x1, waiting for transfers between devices, replicated(): half = lax.all_to_all(copies, ('row', 'col'), 0, 0, tiled=True)  28 us
    pallas_call x1, Pallas kernels, filter_local(): pl.pallas_call(filter_kernel, out_shape=jax.ShapeDtypeStruct(start.shape,...  24.8 us
    all_to_all x1, waiting for transfers between devices, replicated(): summed = jnp.sum(lax.all_to_all(chunks, 'col', 0, 0, tiled=True), axis=0)  8.51 us
    all_to_all x1, blocking collectives, replicated(): lax.all_to_all(copies, 'vec', 0, 0, tiled=True)  5.63 us
    all_to_all x1, starting transfers between devices, replicated(): half = lax.all_to_all(copies, ('row', 'col'), 0, 0, tiled=True)  5.13 us
    all_to_all x1, starting transfers between devices, replicated(): summed = jnp.sum(lax.all_to_all(chunks, 'col', 0, 0, tiled=True), axis=0)  4.21 us
    reshape x1, local copies, waits for them, and re-layouts, replicated(): coded = coded.reshape(2, n_row, n_col, 2, vec_cols, nb_dev, share)  2.7 us
    reshape x1, local copies, waits for them, and re-layouts, replicated(): current = coded.transpose(0, 3, 4, 1, 2, 5).reshape(cols, total_rows)  2.24 us
  transfers between devices with their start and end apart: 2, of which 2 were waited for; matrix products, arithmetic and copies ran while one was open for 0% of the time, Pallas kernels for 0%

profile of v8, /device:TPU:0, one launch (start us, length us, event | category | flops | bytes accessed | tf_op | source)
XLA Modules:
  0.0 95.0 jit_solution(652267406144927024)
XLA Ops:
  0.0 1.3 %dynamic_slice.28 = s32[1]{0:T(128)} dynamic-slice(s32[2]{0:T(128)} %param.7, s32[]{:T(128)S(6)} %select_n.45), dynamic_slice_sizes={1} | dynamic-slice | bytes 12 | tf_op jit(solution)/shard_map/jit(dynamic_index_in_dim)/dynamic_slice | solution.py:148
  1.3 0.7 fusion.14
  2.0 1.3 %fusion = f32[128]{0:T(128)S(1)} fusion(bf16[1,16,128,128]{3,2,1,0:T(8,128)(2,1)S(1)} %constant_dynamic-slice_fusion.2, bf16[16]{0:T(256)(128)(2,1)S(1)} %get-tuple-element.5), kind=kLoop, calls=%fused_computation.2 | loop fusion | flops 1048448 | bytes 524832 | tf_op jit(solution)/shard_map/kmn,kmn->m/dot_general | solution.py:157
  3.3 0.8 fusion.13
  4.1 0.4 convolution_bitcast_fusion
  4.7 0.9 pad_maximum_fusion
  5.6 4.2 %all-to-all-start = ((f32[2,64,1152]{2,1,0:T(8,128)}), f32[2,64,1152]{2,1,0:T(8,128)S(1)}, u32[]{:S(2)}, u32[]{:S(2)}) async-start(f32[2,64,1152]{2,1,0:T(8,128)} %pad_maximum_fusion), calls=%async_computation | async-start | bytes 1179648 | tf_op jit(solution)/shard_map/all_to_all | solution.py:161
  10.5 0.1 constant_dynamic-slice_fusion.1
  10.7 8.5 %all-to-all-done = f32[2,64,1152]{2,1,0:T(8,128)S(1)} async-done(((f32[2,64,1152]{2,1,0:T(8,128)}), f32[2,64,1152]{2,1,0:T(8,128)S(1)}, u32[]{:S(2)}, u32[]{:S(2)}) %all-to-all-start) | async-done | bytes 589856 | tf_op jit(solution)/shard_map/all_to_all | solution.py:161
  19.4 0.1 fusion.5
  19.5 1.2 %broadcast_in_dim.10 = bf16[8,64,1152]{2,1,0:T(8,128)(2,1)} broadcast(bf16[64,1152]{1,0:T(8,128)(2,1)S(1)} %maximum_maximum_fusion), dimensions={1,2} | broadcast | bytes 1327104 | tf_op jit(solution)/shard_map/broadcast_in_dim | solution.py:174
  20.7 5.1 %all-to-all-start.1 = ((bf16[8,64,1152]{2,1,0:T(8,128)(2,1)}), bf16[8,64,1152]{2,1,0:T(8,128)(2,1)S(1)}, u32[]{:S(2)}, u32[]{:S(2)}) async-start(bf16[8,64,1152]{2,1,0:T(8,128)(2,1)} %broadcast_in_dim.10), calls=%async_computation.1 | async-start | bytes 2359296 | tf_op jit(solution)/shard_map/all_to_all | solution.py:175
  25.8 28.0 %all-to-all-done.1 = bf16[8,64,1152]{2,1,0:T(8,128)(2,1)S(1)} async-done(((bf16[8,64,1152]{2,1,0:T(8,128)(2,1)}), bf16[8,64,1152]{2,1,0:T(8,128)(2,1)S(1)}, u32[]{:S(2)}, u32[]{:S(2)}) %all-to-all-start.1) | async-done | bytes 1179680 | tf_op jit(solution)/shard_map/all_to_all | solution.py:175
  53.7 0.3 broadcast_in_dim.11
  54.1 5.6 %all_to_all.15 = bf16[2,8,64,1152]{3,2,1,0:T(8,128)(2,1)S(1)} all-to-all(bf16[2,8,64,1152]{3,2,1,0:T(8,128)(2,1)S(1)} %broadcast_in_dim.11), channel_id=1, replica_groups=mesh['grp'=2,'row'=4,'col'=2,'vec'=2] {'vec'}, dimensions={0} | all-to-all | bytes 4718592 | tf_op jit(solution)/shard_map/all_to_all | solution.py:177
  59.7 0.9 slice_convert_fusion
  60.6 2.7 %reshape.110 = f32[2,4,2,2,32,2,64]{6,5,4,3,2,1,0:T(2,128)} reshape(f32[1024,128]{1,0:T(8,128)} %slice_convert_fusion) | data formatting | bytes 1048576 | tf_op jit(solution)/shard_map/reshape | solution.py:180
  63.3 1.3 %fusion.15 = (f32[2,4,2,1,32,2,64]{6,5,4,3,2,1,0:T(2,128)S(1)}, f32[2,4,2,1,32,2,64]{6,5,4,3,2,1,0:T(2,128)S(1)}) fusion(f32[2,4,2,2,32,2,64]{6,5,4,3,2,1,0:T(2,128)} %reshape.110), kind=kLoop, calls=%fused_computation.38 | loop fusion | bytes 1048576 | tf_op jit(solution)/shard_map/slice | solution.py:181
  64.6 1.5 %fusion.1 = f32[2,32,2,4,2,64]{5,4,3,2,1,0:T(2,128)} fusion(f32[2,4,2,1,32,2,64]{6,5,4,3,2,1,0:T(2,128)S(1)} %get-tuple-element.8, f32[2,4,2,1,32,2,64]{6,5,4,3,2,1,0:T(2,128)S(1)} %get-tuple-element.7), kind=kLoop, calls=%fused_computation.5 | loop fusion | flops 65536 | bytes 786432 | tf_op jit(solution)/shard_map/transpose | solution.py:182
  66.1 2.2 %reshape.106.y_ref = f32[64,1024]{1,0:T(8,128)} reshape(f32[2,32,2,4,2,64]{5,4,3,2,1,0:T(2,128)} %fusion.1) | data formatting | bytes 524288 | tf_op jit(solution)/shard_map/reshape | solution.py:182
  68.3 24.8 %shard_map.46 = f32[64,1024]{1,0:T(8,128)} custom-call(bf16[1024,1152]{1,0:T(8,128)(2,1)} %bitcast.43, f32[64,1024]{1,0:T(8,128)} %reshape.106.y_ref), custom_call_target="tpu_custom_call" | custom-call | tf_op jit(solution)/shard_map/pallas_call | solution.py:88
  93.1 1.1 %reshape.107 = f32[64,2,4,128]{3,2,1,0:T(4,128)S(1)} reshape(f32[64,1024]{1,0:T(8,128)} %shard_map.46) | data formatting | bytes 524288 | tf_op jit(solution)/shard_map/reshape | solution.py:185
  94.2 0.2 dynamic-slice_reduce_fusion
  94.4 0.6 constant_dynamic-slice_fusion
  (18 shorter events, 0.6 us)
Async XLA Ops:
  0.0 2.0 %copy-start = (bf16[2,16,128,128]{3,2,1,0:T(8,128)(2,1)S(1)}, bf16[2,16,128,128]{3,2,1,0:T(8,128)(2,1)}, u32[]{:S(2)}) copy-start(bf16[2,16,128,128]{3,2,1,0:T(8,128)(2,1)} %param.5) | copy-start | bytes 3145732
  3.3 7.2 %copy-start.2 = (f32[32,256]{1,0:T(8,128)S(1)}, f32[32,256]{1,0:T(8,128)}, u32[]{:S(2)}) copy-start(f32[32,256]{1,0:T(8,128)} %param.4) | copy-start | bytes 98308
  5.6 13.6 %all-to-all-start = ((f32[2,64,1152]{2,1,0:T(8,128)}), f32[2,64,1152]{2,1,0:T(8,128)S(1)}, u32[]{:S(2)}, u32[]{:S(2)}) async-start(f32[2,64,1152]{2,1,0:T(8,128)} %pad_maximum_fusion), calls=%async_computation | async-start | bytes 1179648 | tf_op jit(solution)/shard_map/all_to_all | solution.py:161
  20.7 33.1 %all-to-all-start.1 = ((bf16[8,64,1152]{2,1,0:T(8,128)(2,1)}), bf16[8,64,1152]{2,1,0:T(8,128)(2,1)S(1)}, u32[]{:S(2)}, u32[]{:S(2)}) async-start(bf16[8,64,1152]{2,1,0:T(8,128)(2,1)} %broadcast_in_dim.10), calls=%async_computation.1 | async-start | bytes 2359296 | tf_op jit(solution)/shard_map/all_to_all | solution.py:175
  59.7 6.4 %copy-start.1 = (bf16[2,8,64,1152]{3,2,1,0:T(8,128)(2,1)}, bf16[2,8,64,1152]{3,2,1,0:T(8,128)(2,1)S(1)}, u32[]{:S(2)}) copy-start(bf16[2,8,64,1152]{3,2,1,0:T(8,128)(2,1)S(1)} %all_to_all.15) | copy-start | bytes 7077892

commit v9 on v8

--- a/solution.py
+++ b/solution.py
@@ -1,3 +1,5 @@
+import functools
+
 import jax
 import jax.numpy as jnp
 from jax import lax
@@ -66,31 +68,52 @@
     )
 
 
-def filter_kernel(w_ref, y_ref, x_ref):
-    total = y_ref.shape[1]
+def filter_kernel(index_ref, w_ref, x_ref, whole_ref, *, n_row, n_col, vec_cols):
+    total = w_ref.shape[0]
+    block = w_ref.shape[1] - total
+    nb_dev = total // (block * n_row)
+    share = 2 * vec_cols
+    halves = []
+    for half in range(2):
+        parts = []
+        for place in range(total // block):
+            local, row = divmod(place, n_row)
+            base = half * n_row * n_col * share + (row * n_col + local) * share
+            high = w_ref[base : base + vec_cols, total:].astype(jnp.float32)
+            low = w_ref[base + vec_cols : base + share, total:].astype(jnp.float32)
+            parts.append(high + low)
+        halves.append(jnp.concatenate(parts, axis=1))
+    current = jnp.concatenate(halves, axis=0)
 
     def apply(values):
-        product = lax.dot_general(
+        return lax.dot_general(
             values.astype(jnp.bfloat16),
             w_ref[:, :total],
             (((1,), (1,)), ((), ())),
             preferred_element_type=jnp.float32,
         )
-        return product
-
-    current = y_ref[...]
+
     for outer in range(ITERS):
         current = orthonormal_value(chebyshev(current, apply))
-    x_ref[...] = current
-
-
-def filter_local(packed_weights, start):
+    whole_ref[...] = current
+    row = index_ref[0]
+    first = pl.multiple_of(index_ref[1] * vec_cols, 8)
+    for local in range(nb_dev):
+        place = pl.multiple_of((local * n_row + row) * block, 128)
+        x_ref[:, local * block : (local + 1) * block] = whole_ref[pl.ds(first, vec_cols), pl.ds(place, block)]
+
+
+def filter_local(packed, index, n_row, n_col, vec_cols):
+    total = packed.shape[0]
+    block = packed.shape[1] - total
+    nb_dev = total // (block * n_row)
     return pl.pallas_call(
-        filter_kernel,
-        out_shape=jax.ShapeDtypeStruct(start.shape, jnp.float32),
-        in_specs=[pl.BlockSpec(memory_space=pltpu.VMEM)] * 2,
+        functools.partial(filter_kernel, n_row=n_row, n_col=n_col, vec_cols=vec_cols),
+        out_shape=jax.ShapeDtypeStruct((vec_cols, nb_dev * block), jnp.float32),
+        in_specs=[pl.BlockSpec(memory_space=pltpu.SMEM), pl.BlockSpec(memory_space=pltpu.VMEM)],
         out_specs=pl.BlockSpec(memory_space=pltpu.VMEM),
-    )(packed_weights, start)
+        scratch_shapes=[pltpu.VMEM((2 * vec_cols, total), jnp.float32)],
+    )(index, packed)
 
 def distributed(start, tiles, pattern, counts):
     nb_dev = tiles.shape[0]
@@ -163,28 +186,18 @@
     entries = (own_count * block).astype(jnp.float32)
     scale = lax.rsqrt(summed[:, total_rows] / entries + EPSILON) / jnp.sqrt(entries) / HALF_WIDTH
 
-    piece = start.reshape(vec_cols, nb_dev, block)
-    piece = lax.dynamic_slice_in_dim(piece, col_index * share, share, 2).reshape(vec_cols, nb_dev * share)
+    piece = lax.dynamic_slice_in_dim(start, col_index * block, block, 1)
     start_hi, start_lo = split_bf16(piece)
     extra = jnp.concatenate([start_hi, start_lo], axis=0)
-    extra = jnp.concatenate([extra, jnp.zeros((share, 128 - nb_dev * share), jnp.bfloat16)], axis=1)
     rows_bf16 = (summed[:, :total_rows] * scale[:, None]).astype(jnp.bfloat16)
 
     packed = jnp.concatenate([rows_bf16, extra], axis=1)
     copies = jnp.broadcast_to(packed[None], (n_row * n_col,) + packed.shape)
     half = lax.all_to_all(copies, ("row", "col"), 0, 0, tiled=True)
     copies = jnp.broadcast_to(half[None], (2,) + half.shape)
-    whole = lax.all_to_all(copies, "vec", 0, 0, tiled=True).reshape(total_rows, total_rows + 128)
-    extras = whole[:, total_rows:]
-    coded = extras[:, : nb_dev * share].astype(jnp.float32)
-    coded = coded.reshape(2, n_row, n_col, 2, vec_cols, nb_dev, share)
-    coded = coded[:, :, :, 0] + coded[:, :, :, 1]
-    current = coded.transpose(0, 3, 4, 1, 2, 5).reshape(cols, total_rows)
-
-    current = filter_local(whole, current)
-    mine = current.reshape(cols, nb_dev, n_row, block)
-    mine = lax.dynamic_index_in_dim(mine, row_index, 2, keepdims=False).reshape(cols, nb_dev * block)
-    current = lax.dynamic_slice_in_dim(mine, vec_index * vec_cols, vec_cols, 0)
+    whole = lax.all_to_all(copies, "vec", 0, 0, tiled=True).reshape(total_rows, total_rows + block)
+    index = jnp.stack([row_index, vec_index]).astype(jnp.int32)
+    current = filter_local(whole, index, n_row, n_col, vec_cols)
     return current
 
 
@@ -198,7 +211,7 @@
         and tiles.shape[0] == n_vec
         and block % n_col == 0
         and block // n_col == 2 * start.shape[0]
-        and tiles.shape[0] * (block // n_col) <= 128
+        and tiles.shape[0] == n_col
     )
     if fits:
         return replicated(start, tiles, pattern, counts)

time: 95.5 us -> 85.6 us (0.90)
  local copies, waits for them, and re-layouts: 11.5 us -> 3.18 us
  other arithmetic: 6.1 us -> 4.23 us
    reshape x5 -> x0, local copies, waits for them, and re-layouts: 6.12 us -> none  [the longest x1 2.7 us: replicated(): coded = coded.reshape(2, n_row, n_col, 2, vec_cols, nb_dev, share)]
    transpose x1 -> x0, other arithmetic: 1.49 us -> none  [replicated(): current = coded.transpose(0, 3, 4, 1, 2, 5).reshape(cols, total_rows)]
    slice x1 -> x0, local copies, waits for them, and re-layouts: 1.27 us -> none  [replicated(): coded = coded[:, :, :, 0] + coded[:, :, :, 1]]
  transfers between devices with their start and end apart: 2 -> 2, of which waited for: 2 -> 2; matrix products, arithmetic and copies ran while one was open for 0% -> 1% of each run, Pallas kernels for 0% -> 0%
where the time goes in v9:
time: 85.6 us; the launch traced here: 85.2 us
  waiting for transfers between devices  36.2 us (42%)
  Pallas kernels  24.7 us (29%)
  starting transfers between devices  9.33 us (11%)
  blocking collectives  6.53 us (8%)
  other arithmetic  4.23 us (5%)
  local copies, waits for them, and re-layouts  3.18 us (4%)
    all_to_all x1, waiting for transfers between devices, replicated(): half = lax.all_to_all(copies, ('row', 'col'), 0, 0, tiled=True)  27.4 us
    pallas_call x1, Pallas kernels, filter_local(): pl.pallas_call(functools.partial(filter_kernel, n_row=n_row, n_col=n_col,...  24.7 us
    all_to_all x1, waiting for transfers between devices, replicated(): summed = jnp.sum(lax.all_to_all(chunks, 'col', 0, 0, tiled=True), axis=0)  8.79 us
    all_to_all x1, blocking collectives, replicated(): lax.all_to_all(copies, 'vec', 0, 0, tiled=True)  6.53 us
    all_to_all x1, starting transfers between devices, replicated(): half = lax.all_to_all(copies, ('row', 'col'), 0, 0, tiled=True)  5.13 us
    all_to_all x1, starting transfers between devices, replicated(): summed = jnp.sum(lax.all_to_all(chunks, 'col', 0, 0, tiled=True), axis=0)  4.21 us
  transfers between devices with their start and end apart: 2, of which 2 were waited for; matrix products, arithmetic and copies ran while one was open for 1% of the time, Pallas kernels for 0%

profile of v9, /device:TPU:0, one launch (start us, length us, event | category | flops | bytes accessed | tf_op | source)
XLA Modules:
  0.0 85.2 jit_solution(9194286929247111356)
XLA Ops:
  0.0 0.0 copy-start
  0.0 1.3 %dynamic_slice.21 = s32[1]{0:T(128)} dynamic-slice(s32[2]{0:T(128)} %param.7, s32[]{:T(128)S(6)} %select_n.38), dynamic_slice_sizes={1} | dynamic-slice | bytes 12 | tf_op jit(solution)/shard_map/jit(dynamic_index_in_dim)/dynamic_slice | solution.py:171
  1.3 0.6 fusion.13
  1.9 0.0 copy-done
  2.0 1.3 %fusion = f32[128]{0:T(128)S(1)} fusion(bf16[1,16,128,128]{3,2,1,0:T(8,128)(2,1)S(1)} %constant_dynamic-slice_fusion, bf16[16]{0:T(256)(128)(2,1)S(1)} %get-tuple-element.5), kind=kLoop, calls=%fused_computation.2 | loop fusion | flops 1048448 | bytes 524832 | tf_op jit(solution)/shard_map/kmn,kmn->m/dot_general | solution.py:180
  3.2 0.0 copy-start.1
  3.2 0.8 fusion.12
  4.0 0.4 convolution_bitcast_fusion
  4.4 0.1 concatenate.12
  4.5 0.1 broadcast_in_dim.8
  4.6 0.1 broadcast_in_dim.9
  4.7 0.9 %pad_maximum_fusion = f32[2,64,1152]{2,1,0:T(8,128)} fusion(f32[2,64,128]{2,1,0:T(8,128)S(1)} %broadcast_in_dim.9, f32[2,64,1024]{2,1,0:T(8,128)S(1)} %concatenate.12), kind=kLoop, calls=%fused_computation.3 | loop fusion | flops 147456 | bytes 1179648 | tf_op jit(solution)/shard_map/concatenate | solution.py:182
  5.5 4.2 %all-to-all-start = ((f32[2,64,1152]{2,1,0:T(8,128)}), f32[2,64,1152]{2,1,0:T(8,128)S(1)}, u32[]{:S(2)}, u32[]{:S(2)}) async-start(f32[2,64,1152]{2,1,0:T(8,128)} %pad_maximum_fusion), calls=%async_computation | async-start | bytes 1179648 | tf_op jit(solution)/shard_map/all_to_all | solution.py:184
  10.3 0.0 copy-done.1
  10.4 8.8 %all-to-all-done = f32[2,64,1152]{2,1,0:T(8,128)S(1)} async-done(((f32[2,64,1152]{2,1,0:T(8,128)}), f32[2,64,1152]{2,1,0:T(8,128)S(1)}, u32[]{:S(2)}, u32[]{:S(2)}) %all-to-all-start) | async-done | bytes 589856 | tf_op jit(solution)/shard_map/all_to_all | solution.py:184
  19.2 0.1 copy.19
  19.3 0.1 fusion.4
  19.4 1.2 %broadcast_in_dim.10 = bf16[8,64,1152]{2,1,0:T(8,128)(2,1)} broadcast(bf16[64,1152]{1,0:T(8,128)(2,1)S(1)} %maximum_maximum_fusion), dimensions={1,2} | broadcast | bytes 1327104 | tf_op jit(solution)/shard_map/broadcast_in_dim | solution.py:195
  20.6 5.1 %all-to-all-start.1 = ((bf16[8,64,1152]{2,1,0:T(8,128)(2,1)}), bf16[8,64,1152]{2,1,0:T(8,128)(2,1)S(1)}, u32[]{:S(2)}, u32[]{:S(2)}) async-start(bf16[8,64,1152]{2,1,0:T(8,128)(2,1)} %broadcast_in_dim.10), calls=%async_computation.1 | async-start | bytes 2359296 | tf_op jit(solution)/shard_map/all_to_all | solution.py:196
  25.7 0.6 pad_add_fusion.index_ref
  26.3 27.4 %all-to-all-done.1 = bf16[8,64,1152]{2,1,0:T(8,128)(2,1)S(1)} async-done(((bf16[8,64,1152]{2,1,0:T(8,128)(2,1)}), bf16[8,64,1152]{2,1,0:T(8,128)(2,1)S(1)}, u32[]{:S(2)}, u32[]{:S(2)}) %all-to-all-start.1) | async-done | bytes 1179680 | tf_op jit(solution)/shard_map/all_to_all | solution.py:196
  53.7 0.3 broadcast_in_dim.11
  54.0 6.5 %all_to_all.15 = bf16[2,8,64,1152]{3,2,1,0:T(8,128)(2,1)} all-to-all(bf16[2,8,64,1152]{3,2,1,0:T(8,128)(2,1)S(1)} %broadcast_in_dim.11), channel_id=1, replica_groups=mesh['grp'=2,'row'=4,'col'=2,'vec'=2] {'vec'}, dimensions={0} | all-to-all | bytes 4718592 | tf_op jit(solution)/shard_map/all_to_all | solution.py:198
  60.6 24.7 %shard_map.46 = f32[32,256]{1,0:T(8,128)} custom-call(s32[2]{0:T(128)} %pad_add_fusion.index_ref, bf16[1024,1152]{1,0:T(8,128)(2,1)} %bitcast.36), custom_call_target="tpu_custom_call" | custom-call | tf_op jit(solution)/shard_map/pallas_call | solution.py:110
  (5 shorter events, 0.1 us)
Async XLA Ops:
  0.0 1.9 %copy-start = (bf16[2,16,128,128]{3,2,1,0:T(8,128)(2,1)S(1)}, bf16[2,16,128,128]{3,2,1,0:T(8,128)(2,1)}, u32[]{:S(2)}) copy-start(bf16[2,16,128,128]{3,2,1,0:T(8,128)(2,1)} %param.5) | copy-start | bytes 3145732
  3.2 7.1 %copy-start.1 = (f32[32,256]{1,0:T(8,128)S(1)}, f32[32,256]{1,0:T(8,128)}, u32[]{:S(2)}) copy-start(f32[32,256]{1,0:T(8,128)} %param.4) | copy-start | bytes 98308
  5.5 13.6 %all-to-all-start = ((f32[2,64,1152]{2,1,0:T(8,128)}), f32[2,64,1152]{2,1,0:T(8,128)S(1)}, u32[]{:S(2)}, u32[]{:S(2)}) async-start(f32[2,64,1152]{2,1,0:T(8,128)} %pad_maximum_fusion), calls=%async_computation | async-start | bytes 1179648 | tf_op jit(solution)/shard_map/all_to_all | solution.py:184
  20.6 33.1 %all-to-all-start.1 = ((bf16[8,64,1152]{2,1,0:T(8,128)(2,1)}), bf16[8,64,1152]{2,1,0:T(8,128)(2,1)S(1)}, u32[]{:S(2)}, u32[]{:S(2)}) async-start(bf16[8,64,1152]{2,1,0:T(8,128)(2,1)} %broadcast_in_dim.10), calls=%async_computation.1 | async-start | bytes 2359296 | tf_op jit(solution)/shard_map/all_to_all | solution.py:196

commit v10 on v9

--- a/solution.py
+++ b/solution.py
@@ -49,19 +49,28 @@
     cols = lax.broadcasted_iota(jnp.int32, (n, n), 1)
     inverse = (rows == cols).astype(jnp.float32)
     diagonal = jnp.zeros((n, 1), jnp.float32)
-    for k in range(n):
+    for k in range(0, n, 2):
         top = (k // 8) * 8
-        pivot = a[k : k + 1, k : k + 1]
+        first, second = a[k : k + 1, :], a[k + 1 : k + 2, :]
+        pivot = first[:, k : k + 1]
+        coupling = first[:, k + 1 : k + 2]
+        factor = coupling * (1.0 / pivot)
+        pivot_next = second[:, k + 1 : k + 2] - factor * coupling
         down = jnp.where(rows[top:, k : k + 1] > k, a[top:, k : k + 1] * (1.0 / pivot), 0.0)
-        across = jnp.where(cols[k : k + 1, :] > k, a[k : k + 1, :], 0.0)
-        lower_a = a[top:] - down * across
-        lower_inverse = inverse[top:] - down * inverse[k : k + 1, :]
+        next_col = a[top:, k + 1 : k + 2] - down * coupling
+        down_next = jnp.where(rows[top:, k : k + 1] > k + 1, next_col * (1.0 / pivot_next), 0.0)
+        across = jnp.where(cols[k : k + 1, :] > k, first, 0.0)
+        across_next = jnp.where(cols[k : k + 1, :] > k + 1, second - factor * first, 0.0)
+        lower_a = a[top:] - down * across - down_next * across_next
+        inverse_next = inverse[k + 1 : k + 2, :] - factor * inverse[k : k + 1, :]
+        lower_inverse = inverse[top:] - down * inverse[k : k + 1, :] - down_next * inverse_next
         if top:
             a = jnp.concatenate([a[:top], lower_a], axis=0)
             inverse = jnp.concatenate([inverse[:top], lower_inverse], axis=0)
         else:
             a, inverse = lower_a, lower_inverse
         diagonal = jnp.where(rows[:, :1] == k, pivot, diagonal)
+        diagonal = jnp.where(rows[:, :1] == k + 1, pivot_next, diagonal)
     inverse = inverse / jnp.sqrt(diagonal)
     return lax.dot_general(
         inverse, y, (((1,), (0,)), ((), ())), precision=hi, preferred_element_type=jnp.float32

time: 85.6 us -> 88.2 us (1.030)
  Pallas kernels: 24.7 us -> 27.2 us
    pallas_call x1, Pallas kernels: 24.7 us -> 27.2 us  [filter_local(): pl.pallas_call(functools.partial(filter_kernel, n_row=n_row, n_col=n_col,...]
where the time goes in v10:
time: 88.2 us; the launch traced here: 87.8 us
  waiting for transfers between devices  36.2 us (41%)
  Pallas kernels  27.2 us (31%)
  starting transfers between devices  9.33 us (11%)
  blocking collectives  6.53 us (7%)
  other arithmetic  4.23 us (5%)
  local copies, waits for them, and re-layouts  3.18 us (4%)
    all_to_all x1, waiting for transfers between devices, replicated(): half = lax.all_to_all(copies, ('row', 'col'), 0, 0, tiled=True)  27.4 us
    pallas_call x1, Pallas kernels, filter_local(): pl.pallas_call(functools.partial(filter_kernel, n_row=n_row, n_col=n_col,...  27.2 us
    all_to_all x1, waiting for transfers between devices, replicated(): summed = jnp.sum(lax.all_to_all(chunks, 'col', 0, 0, tiled=True), axis=0)  8.79 us
    all_to_all x1, blocking collectives, replicated(): lax.all_to_all(copies, 'vec', 0, 0, tiled=True)  6.53 us
    all_to_all x1, starting transfers between devices, replicated(): half = lax.all_to_all(copies, ('row', 'col'), 0, 0, tiled=True)  5.13 us
    all_to_all x1, starting transfers between devices, replicated(): summed = jnp.sum(lax.all_to_all(chunks, 'col', 0, 0, tiled=True), axis=0)  4.21 us
  transfers between devices with their start and end apart: 2, of which 2 were waited for; matrix products, arithmetic and copies ran while one was open for 1% of the time, Pallas kernels for 0%

profile of v10, /device:TPU:0, one launch (start us, length us, event | category | flops | bytes accessed | tf_op | source)
XLA Modules:
  0.0 87.8 jit_solution(2624210969237164998)
XLA Ops:
  0.0 0.0 copy-start
  0.0 1.3 %dynamic_slice.21 = s32[1]{0:T(128)} dynamic-slice(s32[2]{0:T(128)} %param.7, s32[]{:T(128)S(6)} %select_n.38), dynamic_slice_sizes={1} | dynamic-slice | bytes 12 | tf_op jit(solution)/shard_map/jit(dynamic_index_in_dim)/dynamic_slice | solution.py:180
  1.3 0.6 fusion.13
  1.9 0.0 copy-done
  2.0 1.3 %fusion = f32[128]{0:T(128)S(1)} fusion(bf16[1,16,128,128]{3,2,1,0:T(8,128)(2,1)S(1)} %constant_dynamic-slice_fusion, bf16[16]{0:T(256)(128)(2,1)S(1)} %get-tuple-element.5), kind=kLoop, calls=%fused_computation.2 | loop fusion | flops 1048448 | bytes 524832 | tf_op jit(solution)/shard_map/kmn,kmn->m/dot_general | solution.py:189
  3.2 0.0 copy-start.1
  3.2 0.8 fusion.12
  4.0 0.4 convolution_bitcast_fusion
  4.4 0.1 concatenate.12
  4.5 0.1 broadcast_in_dim.8
  4.6 0.1 broadcast_in_dim.9
  4.7 0.9 pad_maximum_fusion
  5.5 4.2 %all-to-all-start = ((f32[2,64,1152]{2,1,0:T(8,128)}), f32[2,64,1152]{2,1,0:T(8,128)S(1)}, u32[]{:S(2)}, u32[]{:S(2)}) async-start(f32[2,64,1152]{2,1,0:T(8,128)} %pad_maximum_fusion), calls=%async_computation | async-start | bytes 1179648 | tf_op jit(solution)/shard_map/all_to_all | solution.py:193
  10.3 0.0 copy-done.1
  10.4 8.8 %all-to-all-done = f32[2,64,1152]{2,1,0:T(8,128)S(1)} async-done(((f32[2,64,1152]{2,1,0:T(8,128)}), f32[2,64,1152]{2,1,0:T(8,128)S(1)}, u32[]{:S(2)}, u32[]{:S(2)}) %all-to-all-start) | async-done | bytes 589856 | tf_op jit(solution)/shard_map/all_to_all | solution.py:193
  19.2 0.1 copy.19
  19.3 0.1 fusion.4
  19.4 1.2 %broadcast_in_dim.10 = bf16[8,64,1152]{2,1,0:T(8,128)(2,1)} broadcast(bf16[64,1152]{1,0:T(8,128)(2,1)S(1)} %maximum_maximum_fusion), dimensions={1,2} | broadcast | bytes 1327104 | tf_op jit(solution)/shard_map/broadcast_in_dim | solution.py:204
  20.6 5.1 %all-to-all-start.1 = ((bf16[8,64,1152]{2,1,0:T(8,128)(2,1)}), bf16[8,64,1152]{2,1,0:T(8,128)(2,1)S(1)}, u32[]{:S(2)}, u32[]{:S(2)}) async-start(bf16[8,64,1152]{2,1,0:T(8,128)(2,1)} %broadcast_in_dim.10), calls=%async_computation.1 | async-start | bytes 2359296 | tf_op jit(solution)/shard_map/all_to_all | solution.py:205
  25.7 0.6 pad_add_fusion.index_ref
  26.3 27.4 %all-to-all-done.1 = bf16[8,64,1152]{2,1,0:T(8,128)(2,1)S(1)} async-done(((bf16[8,64,1152]{2,1,0:T(8,128)(2,1)}), bf16[8,64,1152]{2,1,0:T(8,128)(2,1)S(1)}, u32[]{:S(2)}, u32[]{:S(2)}) %all-to-all-start.1) | async-done | bytes 1179680 | tf_op jit(solution)/shard_map/all_to_all | solution.py:205
  53.7 0.3 broadcast_in_dim.11
  54.0 6.5 %all_to_all.15 = bf16[2,8,64,1152]{3,2,1,0:T(8,128)(2,1)} all-to-all(bf16[2,8,64,1152]{3,2,1,0:T(8,128)(2,1)S(1)} %broadcast_in_dim.11), channel_id=1, replica_groups=mesh['grp'=2,'row'=4,'col'=2,'vec'=2] {'vec'}, dimensions={0} | all-to-all | bytes 4718592 | tf_op jit(solution)/shard_map/all_to_all | solution.py:207
  60.6 27.2 %shard_map.46 = f32[32,256]{1,0:T(8,128)} custom-call(s32[2]{0:T(128)} %pad_add_fusion.index_ref, bf16[1024,1152]{1,0:T(8,128)(2,1)} %bitcast.36), custom_call_target="tpu_custom_call" | custom-call | tf_op jit(solution)/shard_map/pallas_call | solution.py:119
  (5 shorter events, 0.1 us)
Async XLA Ops:
  0.0 1.9 %copy-start = (bf16[2,16,128,128]{3,2,1,0:T(8,128)(2,1)S(1)}, bf16[2,16,128,128]{3,2,1,0:T(8,128)(2,1)}, u32[]{:S(2)}) copy-start(bf16[2,16,128,128]{3,2,1,0:T(8,128)(2,1)} %param.5) | copy-start | bytes 3145732
  3.2 7.1 %copy-start.1 = (f32[32,256]{1,0:T(8,128)S(1)}, f32[32,256]{1,0:T(8,128)}, u32[]{:S(2)}) copy-start(f32[32,256]{1,0:T(8,128)} %param.4) | copy-start | bytes 98308
  5.5 13.6 %all-to-all-start = ((f32[2,64,1152]{2,1,0:T(8,128)}), f32[2,64,1152]{2,1,0:T(8,128)S(1)}, u32[]{:S(2)}, u32[]{:S(2)}) async-start(f32[2,64,1152]{2,1,0:T(8,128)} %pad_maximum_fusion), calls=%async_computation | async-start | bytes 1179648 | tf_op jit(solution)/shard_map/all_to_all | solution.py:193
  20.6 33.1 %all-to-all-start.1 = ((bf16[8,64,1152]{2,1,0:T(8,128)(2,1)}), bf16[8,64,1152]{2,1,0:T(8,128)(2,1)S(1)}, u32[]{:S(2)}, u32[]{:S(2)}) async-start(bf16[8,64,1152]{2,1,0:T(8,128)(2,1)} %broadcast_in_dim.10), calls=%async_computation.1 | async-start | bytes 2359296 | tf_op jit(solution)/shard_map/all_to_all | solution.py:205

commit v11 on v9

--- a/solution.py
+++ b/solution.py
@@ -181,7 +181,10 @@
     squares = jnp.broadcast_to(squares[:, None], (block, 128))
     partial = jnp.concatenate([dense, squares], axis=1)
     chunks = partial.reshape(n_col, share, total_rows + 128)
-    summed = jnp.sum(lax.all_to_all(chunks, "col", 0, 0, tiled=True), axis=0)
+    summed = lax.dynamic_index_in_dim(chunks, col_index, 0, keepdims=False)
+    for shift in range(1, n_col):
+        sent = lax.dynamic_index_in_dim(chunks, (col_index + shift) % n_col, 0, keepdims=False)
+        summed = summed + lax.ppermute(sent, "col", [(i, (i + shift) % n_col) for i in range(n_col)])
 
     entries = (own_count * block).astype(jnp.float32)
     scale = lax.rsqrt(summed[:, total_rows] / entries + EPSILON) / jnp.sqrt(entries) / HALF_WIDTH

time: 85.6 us -> 82.1 us (0.959)
  waiting for transfers between devices: 36.2 us -> 33.5 us
  other arithmetic: 4.23 us -> 2.83 us
  local copies, waits for them, and re-layouts: 3.18 us -> 4.1 us
    all_to_all x1 -> x0, waiting for transfers between devices: 8.79 us -> none  [replicated(): summed = jnp.sum(lax.all_to_all(chunks, 'col', 0, 0, tiled=True), axis=0)]
    ppermute x0 -> x1, waiting for transfers between devices: none -> 6.25 us  [replicated(): lax.ppermute(sent, 'col', [(i, (i + shift) % n_col) for i in range(n_col)])]
    all_to_all x1 -> x0, starting transfers between devices: 4.21 us -> none  [replicated(): summed = jnp.sum(lax.all_to_all(chunks, 'col', 0, 0, tiled=True), axis=0)]
    ppermute x0 -> x1, starting transfers between devices: none -> 2.99 us  [replicated(): lax.ppermute(sent, 'col', [(i, (i + shift) % n_col) for i in range(n_col)])]
    all_to_all x1, starting transfers between devices: 5.13 us -> 6.05 us  [replicated(): half = lax.all_to_all(copies, ('row', 'col'), 0, 0, tiled=True)]
where the time goes in v11:
time: 82.1 us; the launch traced here: 81.8 us
  waiting for transfers between devices  33.5 us (41%)
  Pallas kernels  24.7 us (30%)
  starting transfers between devices  9.05 us (11%)
  blocking collectives  6.52 us (8%)
  local copies, waits for them, and re-layouts  4.1 us (5%)
  other arithmetic  2.83 us (3%)
    all_to_all x1, waiting for transfers between devices, replicated(): half = lax.all_to_all(copies, ('row', 'col'), 0, 0, tiled=True)  27.3 us
    pallas_call x1, Pallas kernels, filter_local(): pl.pallas_call(functools.partial(filter_kernel, n_row=n_row, n_col=n_col,...  24.7 us
    all_to_all x1, blocking collectives, replicated(): lax.all_to_all(copies, 'vec', 0, 0, tiled=True)  6.52 us
    ppermute x1, waiting for transfers between devices, replicated(): lax.ppermute(sent, 'col', [(i, (i + shift) % n_col) for i in range(n_col)])  6.25 us
    all_to_all x1, starting transfers between devices, replicated(): half = lax.all_to_all(copies, ('row', 'col'), 0, 0, tiled=True)  6.05 us
    ppermute x1, starting transfers between devices, replicated(): lax.ppermute(sent, 'col', [(i, (i + shift) % n_col) for i in range(n_col)])  2.99 us
  transfers between devices with their start and end apart: 2, of which 2 were waited for; matrix products, arithmetic and copies ran while one was open for 1% of the time, Pallas kernels for 0%

profile of v11, /device:TPU:0, one launch (start us, length us, event | category | flops | bytes accessed | tf_op | source)
XLA Modules:
  0.0 81.8 jit_solution(8897612824603696878)
XLA Ops:
  0.0 1.3 %dynamic_slice.28 = s32[1]{0:T(128)} dynamic-slice(s32[2]{0:T(128)} %param.7, s32[]{:T(128)S(6)} %select_n.51), dynamic_slice_sizes={1} | dynamic-slice | bytes 12 | tf_op jit(solution)/shard_map/jit(dynamic_index_in_dim)/dynamic_slice | solution.py:171
  1.3 0.6 fusion.22
  2.0 1.3 %fusion = f32[128]{0:T(128)S(1)} fusion(bf16[1,16,128,128]{3,2,1,0:T(8,128)(2,1)S(1)} %constant_dynamic-slice_fusion.1, bf16[16]{0:T(256)(128)(2,1)S(1)} %get-tuple-element.5), kind=kLoop, calls=%fused_computation.6 | loop fusion | flops 1048448 | bytes 524832 | tf_op jit(solution)/shard_map/kmn,kmn->m/dot_general | solution.py:180
  3.2 0.1 fusion.16
  3.3 0.4 convolution_bitcast_fusion
  3.7 0.1 concatenate.12
  3.8 0.1 broadcast_in_dim.8
  3.9 0.3 copy.13
  4.2 0.0 copy-start.1
  4.3 0.2 copy.14
  4.5 3.0 %collective-permute-start = (f32[64,1152]{1,0:T(8,128)S(1)}, f32[64,1152]{1,0:T(8,128)S(1)}, u32[]{:S(2)}, u32[]{:S(2)}) collective-permute-start(f32[64,1152]{1,0:T(8,128)S(1)} %bitcast.43), channel_id=1, source_target_pairs={{0,2},{2,0},{1,3},{3,1},{4,6},{6,4},{5,7},{7,5},{8,10},{10,8},{9,1... | collective-permute-start | bytes 884744 | tf_op jit(solution)/shard_map/ppermute | solution.py:187
  8.2 0.1 copy.24
  8.3 6.3 %collective-permute-done = f32[64,1152]{1,0:T(8,128)S(1)} collective-permute-done((f32[64,1152]{1,0:T(8,128)S(1)}, f32[64,1152]{1,0:T(8,128)S(1)}, u32[]{:S(2)}, u32[]{:S(2)}) %collective-permute-start) | collective-permute-done | bytes 294944 | tf_op jit(solution)/shard_map/ppermute | solution.py:187
  14.5 0.2 copy.15
  14.8 0.1 fusion.4
  14.9 0.1 maximum_maximum_fusion
  15.0 0.2 copy.17
  15.2 1.2 %broadcast_in_dim.10 = bf16[8,64,1152]{2,1,0:T(8,128)(2,1)} broadcast(bf16[64,1152]{1,0:T(8,128)(2,1)S(1)} %copy.17), dimensions={1,2} | broadcast | bytes 1327104 | tf_op jit(solution)/shard_map/broadcast_in_dim | solution.py:198
  16.3 6.1 %all-to-all-start = ((bf16[8,64,1152]{2,1,0:T(8,128)(2,1)}), bf16[8,64,1152]{2,1,0:T(8,128)(2,1)S(1)}, u32[]{:S(2)}, u32[]{:S(2)}) async-start(bf16[8,64,1152]{2,1,0:T(8,128)(2,1)} %broadcast_in_dim.10), calls=%async_computation | async-start | bytes 2359296 | tf_op jit(solution)/shard_map/all_to_all | solution.py:199
  22.4 0.6 pad_add_fusion.index_ref
  23.0 27.3 %all-to-all-done = bf16[8,64,1152]{2,1,0:T(8,128)(2,1)S(1)} async-done(((bf16[8,64,1152]{2,1,0:T(8,128)(2,1)}), bf16[8,64,1152]{2,1,0:T(8,128)(2,1)S(1)}, u32[]{:S(2)}, u32[]{:S(2)}) %all-to-all-start) | async-done | bytes 1179680 | tf_op jit(solution)/shard_map/all_to_all | solution.py:199
  50.3 0.3 broadcast_in_dim.11
  50.6 6.5 %all_to_all.10 = bf16[2,8,64,1152]{3,2,1,0:T(8,128)(2,1)} all-to-all(bf16[2,8,64,1152]{3,2,1,0:T(8,128)(2,1)S(1)} %broadcast_in_dim.11), channel_id=1, replica_groups=mesh['grp'=2,'row'=4,'col'=2,'vec'=2] {'vec'}, dimensions={0} | all-to-all | bytes 4718592 | tf_op jit(solution)/shard_map/all_to_all | solution.py:201
  57.2 24.7 %shard_map.46 = f32[32,256]{1,0:T(8,128)} custom-call(s32[2]{0:T(128)} %pad_add_fusion.index_ref, bf16[1024,1152]{1,0:T(8,128)(2,1)} %bitcast.42), custom_call_target="tpu_custom_call" | custom-call | tf_op jit(solution)/shard_map/pallas_call | solution.py:110
  (12 shorter events, 0.2 us)
Async XLA Ops:
  0.0 1.9 %copy-start = (bf16[2,16,128,128]{3,2,1,0:T(8,128)(2,1)S(1)}, bf16[2,16,128,128]{3,2,1,0:T(8,128)(2,1)}, u32[]{:S(2)}) copy-start(bf16[2,16,128,128]{3,2,1,0:T(8,128)(2,1)} %param.5) | copy-start | bytes 3145732
  0.0 3.2 %copy-start.2 = (s32[2,32]{1,0:T(2,128)S(1)}, s32[2,32]{1,0:T(2,128)}, u32[]{:S(2)}) copy-start(s32[2,32]{1,0:T(2,128)} %param.6) | copy-start | bytes 772
  4.2 3.9 %copy-start.1 = (f32[32,256]{1,0:T(8,128)S(1)}, f32[32,256]{1,0:T(8,128)}, u32[]{:S(2)}) copy-start(f32[32,256]{1,0:T(8,128)} %param.4) | copy-start | bytes 98308
  4.5 10.0 %collective-permute-start = (f32[64,1152]{1,0:T(8,128)S(1)}, f32[64,1152]{1,0:T(8,128)S(1)}, u32[]{:S(2)}, u32[]{:S(2)}) collective-permute-start(f32[64,1152]{1,0:T(8,128)S(1)} %bitcast.43), channel_id=1, source_target_pairs={{0,2},{2,0},{1,3},{3,1},{4,6},{6,4},{5,7},{7,5},{8,10},{10,8},{9,1... | collective-permute-start | bytes 884744 | tf_op jit(solution)/shard_map/ppermute | solution.py:187
  16.3 34.0 %all-to-all-start = ((bf16[8,64,1152]{2,1,0:T(8,128)(2,1)}), bf16[8,64,1152]{2,1,0:T(8,128)(2,1)S(1)}, u32[]{:S(2)}, u32[]{:S(2)}) async-start(bf16[8,64,1152]{2,1,0:T(8,128)(2,1)} %broadcast_in_dim.10), calls=%async_computation | async-start | bytes 2359296 | tf_op jit(solution)/shard_map/all_to_all | solution.py:199

commit v12 on v11

--- a/solution.py
+++ b/solution.py
@@ -115,6 +115,33 @@
         scratch_shapes=[pltpu.VMEM((2 * vec_cols, total), jnp.float32)],
     )(index, packed)
 
+def partial_kernel(meta_ref, tiles_ref, out_ref, squares_ref):
+    slots, block = tiles_ref.shape[1], tiles_ref.shape[2]
+    total = out_ref.shape[1] - 128
+    own = meta_ref[0]
+    out_ref[...] = jnp.zeros(out_ref.shape, jnp.float32)
+    squares_ref[...] = jnp.zeros(squares_ref.shape, jnp.float32)
+    for slot in range(slots):
+        place = pl.multiple_of(meta_ref[1 + slot] * block, block)
+        live = meta_ref[1 + slots + slot].astype(jnp.float32)
+        tile = tiles_ref[own, slot].astype(jnp.float32) * live
+        out_ref[:, pl.ds(place, block)] += tile
+        squares_ref[...] += tile * tile
+    sums = jnp.sum(squares_ref[...], axis=1, keepdims=True)
+    out_ref[:, total:] = jnp.broadcast_to(sums, (block, 128))
+
+
+def partial_rows(tiles, meta, total_rows):
+    block = tiles.shape[2]
+    return pl.pallas_call(
+        partial_kernel,
+        out_shape=jax.ShapeDtypeStruct((block, total_rows + 128), jnp.float32),
+        in_specs=[pl.BlockSpec(memory_space=pltpu.SMEM), pl.BlockSpec(memory_space=pltpu.VMEM)],
+        out_specs=pl.BlockSpec(memory_space=pltpu.VMEM),
+        scratch_shapes=[pltpu.VMEM((block, block), jnp.float32)],
+    )(meta, tiles)
+
+
 def distributed(start, tiles, pattern, counts):
     nb_dev = tiles.shape[0]
     block = tiles.shape[2]
@@ -164,22 +191,15 @@
     col_index = lax.axis_index("col")
     vec_index = lax.axis_index("vec")
 
-    own_tiles = lax.dynamic_index_in_dim(tiles, vec_index, 0, keepdims=False)
     own_pattern = lax.dynamic_slice_in_dim(
         lax.dynamic_index_in_dim(pattern, vec_index, 0, keepdims=False), col_index * kb_dev, kb_dev, 0
     )
     own_count = lax.dynamic_index_in_dim(counts, vec_index, 0, keepdims=False)
     slot_ids = col_index * kb_dev + jnp.arange(kb_dev, dtype=jnp.int32)
-    live = slot_ids < own_count
-    position = (own_pattern % nb_dev) * n_row + own_pattern // nb_dev
-    onehot = (position[:, None] == jnp.arange(nblk, dtype=jnp.int32)) & live[:, None]
-    dense = jnp.einsum(
-        "kj,kmn->mjn", onehot.astype(jnp.bfloat16), own_tiles, preferred_element_type=jnp.float32
-    ).reshape(block, total_rows)
-    masked = own_tiles * live.astype(jnp.bfloat16)[:, None, None]
-    squares = jnp.einsum("kmn,kmn->m", masked, masked, preferred_element_type=jnp.float32)
-    squares = jnp.broadcast_to(squares[:, None], (block, 128))
-    partial = jnp.concatenate([dense, squares], axis=1)
+    live = (slot_ids < own_count).astype(jnp.int32)
+    position = jnp.clip((own_pattern % nb_dev) * n_row + own_pattern // nb_dev, 0, nblk - 1)
+    meta = jnp.concatenate([vec_index.astype(jnp.int32)[None], position, live])
+    partial = partial_rows(tiles, meta, total_rows)
     chunks = partial.reshape(n_col, share, total_rows + 128)
     summed = lax.dynamic_index_in_dim(chunks, col_index, 0, keepdims=False)
     for shift in range(1, n_col):

time: 82.1 us -> 84.4 us (1.028)
  Pallas kernels: 24.7 us -> 27 us
    pallas_call x0 -> x1, Pallas kernels: none -> 2.36 us  [partial_rows(): pl.pallas_call(partial_kernel, out_shape=jax.ShapeDtypeStruct((block, tot...]
    dot_general x1 -> x0, other arithmetic: 1.27 us -> none  [replicated(): jnp.einsum('kmn,kmn->m', masked, masked, preferred_element_type=jnp.float32)]
    dynamic_slice x2, local copies, waits for them, and re-layouts: 0.26 us -> 1.33 us  [replicated(): summed = lax.dynamic_index_in_dim(chunks, col_index, 0, keepdims=False)]
where the time goes in v12:
time: 84.4 us; the launch traced here: 84.1 us
  waiting for transfers between devices  33.2 us (39%)
  Pallas kernels  27 us (32%)
  starting transfers between devices  9.06 us (11%)
  blocking collectives  6.52 us (8%)
  local copies, waits for them, and re-layouts  4.6 us (5%)
  other arithmetic  2.86 us (3%)
    all_to_all x1, waiting for transfers between devices, replicated(): half = lax.all_to_all(copies, ('row', 'col'), 0, 0, tiled=True)  27.3 us
    pallas_call x1, Pallas kernels, filter_local(): pl.pallas_call(functools.partial(filter_kernel, n_row=n_row, n_col=n_col,...  24.7 us
    all_to_all x1, blocking collectives, replicated(): lax.all_to_all(copies, 'vec', 0, 0, tiled=True)  6.52 us
    all_to_all x1, starting transfers between devices, replicated(): half = lax.all_to_all(copies, ('row', 'col'), 0, 0, tiled=True)  6.06 us
    ppermute x1, waiting for transfers between devices, replicated(): lax.ppermute(sent, 'col', [(i, (i + shift) % n_col) for i in range(n_col)])  5.93 us
    ppermute x1, starting transfers between devices, replicated(): lax.ppermute(sent, 'col', [(i, (i + shift) % n_col) for i in range(n_col)])  3 us
    pallas_call x1, Pallas kernels, partial_rows(): pl.pallas_call(partial_kernel, out_shape=jax.ShapeDtypeStruct((block, tot...  2.36 us
  transfers between devices with their start and end apart: 2, of which 2 were waited for; matrix products, arithmetic and copies ran while one was open for 1% of the time, Pallas kernels for 0%

profile of v12, /device:TPU:0, one launch (start us, length us, event | category | flops | bytes accessed | tf_op | source)
XLA Modules:
  0.0 84.1 jit_solution(2530075007782649474)
XLA Ops:
  0.0 0.0 copy-start
  0.0 1.3 %dynamic_slice.23 = s32[1]{0:T(128)} dynamic-slice(s32[2]{0:T(128)} %param.7, s32[]{:T(128)S(6)} %select_n.41), dynamic_slice_sizes={1} | dynamic-slice | bytes 12 | tf_op jit(solution)/shard_map/jit(dynamic_index_in_dim)/dynamic_slice | solution.py:197
  1.3 0.6 compare_convert_fusion
  1.9 0.8 fusion.9
  2.7 0.6 pad_add_fusion.1.meta_ref
  3.3 2.4 %shard_map.46 = f32[128,1152]{1,0:T(8,128)} custom-call(s32[33]{0:T(128)} %pad_add_fusion.1.meta_ref, bf16[2,16,128,128]{3,2,1,0:T(8,128)(2,1)} %tiles_ref.1), custom_call_target="tpu_custom_call" | custom-call | tf_op jit(solution)/shard_map/pallas_call | solution.py:136
  5.7 1.1 %constant_dynamic-slice_fusion.1 = (f32[1,64,1152]{2,1,0:T(8,128)S(1)}, f32[64,1152]{1,0:T(8,128)S(1)}) fusion(f32[2,64,1152]{2,1,0:T(8,128)} %bitcast.27, s32[]{:T(128)S(6)} %select_n.47, s32[]{:T(128)S(6)} %select_n.49), kind=kLoop, calls=%fused_computation.15 | loop fusion | bytes 1179656 | tf_op jit(solution)/shard_map/jit(dynamic_index_in_dim)/dynamic_slice | solution.py:204
  6.7 3.0 %collective-permute-start = (f32[64,1152]{1,0:T(8,128)S(1)}, f32[64,1152]{1,0:T(8,128)S(1)}, u32[]{:S(2)}, u32[]{:S(2)}) collective-permute-start(f32[64,1152]{1,0:T(8,128)S(1)} %get-tuple-element.6), channel_id=1, source_target_pairs={{0,2},{2,0},{1,3},{3,1},{4,6},{6,4},{5,7},{7,5},{8,10},{10,8},{9,1... | collective-permute-start | bytes 884744 | tf_op jit(solution)/shard_map/ppermute | solution.py:207
  10.4 0.0 copy-done
  10.5 0.1 copy.13
  10.6 0.2 copy.9
  10.8 5.9 %collective-permute-done = f32[64,1152]{1,0:T(8,128)S(1)} collective-permute-done((f32[64,1152]{1,0:T(8,128)S(1)}, f32[64,1152]{1,0:T(8,128)S(1)}, u32[]{:S(2)}, u32[]{:S(2)}) %collective-permute-start) | collective-permute-done | bytes 294944 | tf_op jit(solution)/shard_map/ppermute | solution.py:207
  16.8 0.2 copy.10
  17.0 0.1 bitcast_add_fusion
  17.1 0.1 maximum_maximum_fusion
  17.2 0.2 copy.12
  17.4 1.2 %broadcast_in_dim.4 = bf16[8,64,1152]{2,1,0:T(8,128)(2,1)} broadcast(bf16[64,1152]{1,0:T(8,128)(2,1)S(1)} %copy.12), dimensions={1,2} | broadcast | bytes 1327104 | tf_op jit(solution)/shard_map/broadcast_in_dim | solution.py:218
  18.5 6.1 %all-to-all-start = ((bf16[8,64,1152]{2,1,0:T(8,128)(2,1)}), bf16[8,64,1152]{2,1,0:T(8,128)(2,1)S(1)}, u32[]{:S(2)}, u32[]{:S(2)}) async-start(bf16[8,64,1152]{2,1,0:T(8,128)(2,1)} %broadcast_in_dim.4), calls=%async_computation | async-start | bytes 2359296 | tf_op jit(solution)/shard_map/all_to_all | solution.py:219
  24.6 0.6 pad_add_fusion.index_ref
  25.2 27.3 %all-to-all-done = bf16[8,64,1152]{2,1,0:T(8,128)(2,1)S(1)} async-done(((bf16[8,64,1152]{2,1,0:T(8,128)(2,1)}), bf16[8,64,1152]{2,1,0:T(8,128)(2,1)S(1)}, u32[]{:S(2)}, u32[]{:S(2)}) %all-to-all-start) | async-done | bytes 1179680 | tf_op jit(solution)/shard_map/all_to_all | solution.py:219
  52.5 0.3 broadcast_in_dim.5
  52.9 6.5 %all_to_all.10 = bf16[2,8,64,1152]{3,2,1,0:T(8,128)(2,1)} all-to-all(bf16[2,8,64,1152]{3,2,1,0:T(8,128)(2,1)S(1)} %broadcast_in_dim.5), channel_id=1, replica_groups=mesh['grp'=2,'row'=4,'col'=2,'vec'=2] {'vec'}, dimensions={0} | all-to-all | bytes 4718592 | tf_op jit(solution)/shard_map/all_to_all | solution.py:221
  59.4 24.7 %shard_map.47 = f32[32,256]{1,0:T(8,128)} custom-call(s32[2]{0:T(128)} %pad_add_fusion.index_ref, bf16[1024,1152]{1,0:T(8,128)(2,1)} %bitcast.26), custom_call_target="tpu_custom_call" | custom-call | tf_op jit(solution)/shard_map/pallas_call | solution.py:110
  (4 shorter events, 0.1 us)
Async XLA Ops:
  0.0 10.4 %copy-start = (f32[32,256]{1,0:T(8,128)S(1)}, f32[32,256]{1,0:T(8,128)}, u32[]{:S(2)}) copy-start(f32[32,256]{1,0:T(8,128)} %param.4) | copy-start | bytes 98308
  6.7 10.0 %collective-permute-start = (f32[64,1152]{1,0:T(8,128)S(1)}, f32[64,1152]{1,0:T(8,128)S(1)}, u32[]{:S(2)}, u32[]{:S(2)}) collective-permute-start(f32[64,1152]{1,0:T(8,128)S(1)} %get-tuple-element.6), channel_id=1, source_target_pairs={{0,2},{2,0},{1,3},{3,1},{4,6},{6,4},{5,7},{7,5},{8,10},{10,8},{9,1... | collective-permute-start | bytes 884744 | tf_op jit(solution)/shard_map/ppermute | solution.py:207
  18.5 34.0 %all-to-all-start = ((bf16[8,64,1152]{2,1,0:T(8,128)(2,1)}), bf16[8,64,1152]{2,1,0:T(8,128)(2,1)S(1)}, u32[]{:S(2)}, u32[]{:S(2)}) async-start(bf16[8,64,1152]{2,1,0:T(8,128)(2,1)} %broadcast_in_dim.4), calls=%async_computation | async-start | bytes 2359296 | tf_op jit(solution)/shard_map/all_to_all | solution.py:219

commit v13 on v11

--- a/solution.py
+++ b/solution.py
@@ -68,52 +68,63 @@
     )
 
 
-def filter_kernel(index_ref, w_ref, x_ref, whole_ref, *, n_row, n_col, vec_cols):
-    total = w_ref.shape[0]
-    block = w_ref.shape[1] - total
+def filter_kernel(index_ref, own_ref, other_ref, x_ref, whole_ref, *, n_row, n_col, vec_cols):
+    half_rows = own_ref.shape[0]
+    total = 2 * half_rows
+    block = own_ref.shape[1] - total
     nb_dev = total // (block * n_row)
     share = 2 * vec_cols
-    halves = []
-    for half in range(2):
+    row = index_ref[0]
+    core = index_ref[1]
+    own_first = pl.multiple_of(core * vec_cols, 8)
+    other_first = pl.multiple_of((1 - core) * vec_cols, 8)
+    own_place = pl.multiple_of(core * half_rows, 128)
+    other_place = pl.multiple_of((1 - core) * half_rows, 128)
+
+    def decode(ref):
         parts = []
         for place in range(total // block):
-            local, row = divmod(place, n_row)
-            base = half * n_row * n_col * share + (row * n_col + local) * share
-            high = w_ref[base : base + vec_cols, total:].astype(jnp.float32)
-            low = w_ref[base + vec_cols : base + share, total:].astype(jnp.float32)
+            local, src_row = divmod(place, n_row)
+            base = (src_row * n_col + local) * share
+            high = ref[base : base + vec_cols, total:].astype(jnp.float32)
+            low = ref[base + vec_cols : base + share, total:].astype(jnp.float32)
             parts.append(high + low)
-        halves.append(jnp.concatenate(parts, axis=1))
-    current = jnp.concatenate(halves, axis=0)
+        return jnp.concatenate(parts, axis=1)
+
+    whole_ref[pl.ds(own_first, vec_cols), :] = decode(own_ref)
+    whole_ref[pl.ds(other_first, vec_cols), :] = decode(other_ref)
+    current = whole_ref[...]
 
     def apply(values):
-        return lax.dot_general(
-            values.astype(jnp.bfloat16),
-            w_ref[:, :total],
-            (((1,), (1,)), ((), ())),
-            preferred_element_type=jnp.float32,
+        rounded = values.astype(jnp.bfloat16)
+        dims = (((1,), (1,)), ((), ()))
+        whole_ref[:, pl.ds(own_place, half_rows)] = lax.dot_general(
+            rounded, own_ref[:, :total], dims, preferred_element_type=jnp.float32
         )
+        whole_ref[:, pl.ds(other_place, half_rows)] = lax.dot_general(
+            rounded, other_ref[:, :total], dims, preferred_element_type=jnp.float32
+        )
+        return whole_ref[...]
 
     for outer in range(ITERS):
         current = orthonormal_value(chebyshev(current, apply))
     whole_ref[...] = current
-    row = index_ref[0]
-    first = pl.multiple_of(index_ref[1] * vec_cols, 8)
     for local in range(nb_dev):
         place = pl.multiple_of((local * n_row + row) * block, 128)
-        x_ref[:, local * block : (local + 1) * block] = whole_ref[pl.ds(first, vec_cols), pl.ds(place, block)]
-
-
-def filter_local(packed, index, n_row, n_col, vec_cols):
-    total = packed.shape[0]
-    block = packed.shape[1] - total
+        x_ref[:, local * block : (local + 1) * block] = whole_ref[pl.ds(own_first, vec_cols), pl.ds(place, block)]
+
+
+def filter_local(own, other, index, n_row, n_col, vec_cols):
+    total = 2 * own.shape[0]
+    block = own.shape[1] - total
     nb_dev = total // (block * n_row)
     return pl.pallas_call(
         functools.partial(filter_kernel, n_row=n_row, n_col=n_col, vec_cols=vec_cols),
         out_shape=jax.ShapeDtypeStruct((vec_cols, nb_dev * block), jnp.float32),
-        in_specs=[pl.BlockSpec(memory_space=pltpu.SMEM), pl.BlockSpec(memory_space=pltpu.VMEM)],
+        in_specs=[pl.BlockSpec(memory_space=pltpu.SMEM)] + [pl.BlockSpec(memory_space=pltpu.VMEM)] * 2,
         out_specs=pl.BlockSpec(memory_space=pltpu.VMEM),
         scratch_shapes=[pltpu.VMEM((2 * vec_cols, total), jnp.float32)],
-    )(index, packed)
+    )(index, own, other)
 
 def distributed(start, tiles, pattern, counts):
     nb_dev = tiles.shape[0]
@@ -197,10 +208,10 @@
     packed = jnp.concatenate([rows_bf16, extra], axis=1)
     copies = jnp.broadcast_to(packed[None], (n_row * n_col,) + packed.shape)
     half = lax.all_to_all(copies, ("row", "col"), 0, 0, tiled=True)
-    copies = jnp.broadcast_to(half[None], (2,) + half.shape)
-    whole = lax.all_to_all(copies, "vec", 0, 0, tiled=True).reshape(total_rows, total_rows + block)
+    half = half.reshape(n_row * n_col * share, total_rows + block)
+    other = lax.ppermute(half, "vec", [(0, 1), (1, 0)])
     index = jnp.stack([row_index, vec_index]).astype(jnp.int32)
-    current = filter_local(whole, index, n_row, n_col, vec_cols)
+    current = filter_local(half, other, index, n_row, n_col, vec_cols)
     return current
 
 

time: 82.1 us -> 80 us (0.974)
  blocking collectives: 6.52 us -> 33.9 us
  waiting for transfers between devices: 33.5 us -> 8.29 us
  starting transfers between devices: 9.05 us -> 3 us
  Pallas kernels: 24.7 us -> 26.5 us
    all_to_all x1, blocking collectives: 6.52 us -> 33.9 us  [replicated(): half = lax.all_to_all(copies, ('row', 'col'), 0, 0, tiled=True)]
    all_to_all x1 -> x0, waiting for transfers between devices: 27.3 us -> none  [replicated(): half = lax.all_to_all(copies, ('row', 'col'), 0, 0, tiled=True)]
    all_to_all x1 -> x0, starting transfers between devices: 6.05 us -> none  [replicated(): half = lax.all_to_all(copies, ('row', 'col'), 0, 0, tiled=True)]
    ppermute x0 -> x1, waiting for transfers between devices: none -> 2.16 us  [replicated(): other = lax.ppermute(half, 'vec', [(0, 1), (1, 0)])]
    pallas_call x1, Pallas kernels: 24.7 us -> 26.5 us  [filter_local(): pl.pallas_call(functools.partial(filter_kernel, n_row=n_row, n_col=n_col,...]
    unnamed x7 -> x11, local copies, waits for them, and re-layouts: 0.11 us -> 1.13 us
    broadcast_in_dim x1, local copies, waits for them, and re-layouts: 1.16 us -> 0.15 us  [replicated(): copies = jnp.broadcast_to(packed[None], (n_row * n_col,) + packed.shape)]
where the time goes in v13:
time: 80 us; the launch traced here: 79.8 us
  blocking collectives  33.9 us (42%)
  Pallas kernels  26.5 us (33%)
  waiting for transfers between devices  8.29 us (10%)
  local copies, waits for them, and re-layouts  3.86 us (5%)
  starting transfers between devices  3 us (4%)
  other arithmetic  2.99 us (4%)
  between operations  0.87 us (1%)
    all_to_all x1, blocking collectives, replicated(): half = lax.all_to_all(copies, ('row', 'col'), 0, 0, tiled=True)  33.9 us
    pallas_call x1, Pallas kernels, filter_local(): pl.pallas_call(functools.partial(filter_kernel, n_row=n_row, n_col=n_col,...  26.5 us
    ppermute x1, waiting for transfers between devices, replicated(): lax.ppermute(sent, 'col', [(i, (i + shift) % n_col) for i in range(n_col)])  6.12 us
    ppermute x1, starting transfers between devices, replicated(): lax.ppermute(sent, 'col', [(i, (i + shift) % n_col) for i in range(n_col)])  2.99 us
    ppermute x1, waiting for transfers between devices, replicated(): other = lax.ppermute(half, 'vec', [(0, 1), (1, 0)])  2.16 us
  transfers between devices with their start and end apart: 2, of which 2 were waited for; matrix products, arithmetic and copies ran while one was open for 1% of the time, Pallas kernels for 0%

profile of v13, /device:TPU:0, one launch (start us, length us, event | category | flops | bytes accessed | tf_op | source)
XLA Modules:
  0.0 79.8 jit_solution(2421555580678269443)
XLA Ops:
  0.0 1.4 %dynamic_slice.28 = s32[1]{0:T(128)} dynamic-slice(s32[2]{0:T(128)} %param.7, s32[]{:T(128)S(6)} %select_n.51), dynamic_slice_sizes={1} | dynamic-slice | bytes 12 | tf_op jit(solution)/shard_map/jit(dynamic_index_in_dim)/dynamic_slice | solution.py:182
  1.4 0.7 fusion.22
  2.2 1.3 %fusion = f32[128]{0:T(128)S(1)} fusion(bf16[1,16,128,128]{3,2,1,0:T(8,128)(2,1)S(1)} %constant_dynamic-slice_fusion.1, bf16[16]{0:T(256)(128)(2,1)S(1)} %get-tuple-element.5), kind=kLoop, calls=%fused_computation.6 | loop fusion | flops 1048448 | bytes 524832 | tf_op jit(solution)/shard_map/kmn,kmn->m/dot_general | solution.py:191
  3.5 0.1 fusion.16
  3.5 0.4 convolution_bitcast_fusion
  3.9 0.1 concatenate.12
  4.0 0.1 broadcast_in_dim.6
  4.1 0.3 copy.13
  4.5 0.0 copy-start.3
  4.5 0.2 copy.14
  4.7 3.0 %collective-permute-start = (f32[64,1152]{1,0:T(8,128)S(1)}, f32[64,1152]{1,0:T(8,128)S(1)}, u32[]{:S(2)}, u32[]{:S(2)}) collective-permute-start(f32[64,1152]{1,0:T(8,128)S(1)} %bitcast.44), channel_id=1, source_target_pairs={{0,2},{2,0},{1,3},{3,1},{4,6},{6,4},{5,7},{7,5},{8,10},{10,8},{9,1... | collective-permute-start | bytes 884744 | tf_op jit(solution)/shard_map/ppermute | solution.py:198
  8.5 0.1 copy.24
  8.6 6.1 %collective-permute-done = f32[64,1152]{1,0:T(8,128)S(1)} collective-permute-done((f32[64,1152]{1,0:T(8,128)S(1)}, f32[64,1152]{1,0:T(8,128)S(1)}, u32[]{:S(2)}, u32[]{:S(2)}) %collective-permute-start) | collective-permute-done | bytes 294944 | tf_op jit(solution)/shard_map/ppermute | solution.py:198
  14.7 0.2 copy.15
  15.0 0.1 fusion.4
  15.1 0.1 maximum_maximum_fusion
  15.2 0.2 copy.17
  15.4 0.1 broadcast_in_dim.8
  15.5 33.9 %all_to_all.5 = bf16[8,64,1152]{2,1,0:T(8,128)(2,1)S(1)} all-to-all(bf16[8,64,1152]{2,1,0:T(8,128)(2,1)S(1)} %broadcast_in_dim.8), channel_id=1, replica_groups=mesh['grp'=2,'row'=4,'col'=2,'vec'=2] {'row','col'}, dimensions={0} | all-to-all | bytes 2359296 | tf_op jit(solution)/shard_map/all_to_all | solution.py:210
  49.5 0.0 collective-permute-start.1
  49.5 0.7 pad_add_fusion.index_ref
  50.1 2.2 %collective-permute-done.1.other_ref = bf16[512,1152]{1,0:T(8,128)(2,1)S(1)} collective-permute-done((bf16[512,1152]{1,0:T(8,128)(2,1)S(1)}, bf16[512,1152]{1,0:T(8,128)(2,1)S(1)}, u32[]{:S(2)}, u32[]{:S(2)}) %collective-permute-start.1) | collective-permute-done | bytes 1179680 | tf_op jit(solution)/shard_map/ppermute | solution.py:212
  52.3 1.0 %copy-done.2 = bf16[512,1152]{1,0:T(8,128)(2,1)} copy-done((bf16[512,1152]{1,0:T(8,128)(2,1)}, bf16[512,1152]{1,0:T(8,128)(2,1)S(1)}, u32[]{:S(2)}) %copy-start.2) | copy-done | bytes 1179672
  53.3 26.5 %shard_map.46 = f32[32,256]{1,0:T(8,128)} custom-call(s32[2]{0:T(128)} %pad_add_fusion.index_ref, bf16[512,1152]{1,0:T(8,128)(2,1)} %bitcast.43, bf16[512,1152]{1,0:T(8,128)(2,1)} %copy-done.2), custom_call_target="tpu_custom_call" | custom-call | tf_op jit(solution)/shard_map/pallas_call | solution.py:121
  (15 shorter events, 0.2 us)
Async XLA Ops:
  0.0 2.1 %copy-start = (bf16[2,16,128,128]{3,2,1,0:T(8,128)(2,1)S(1)}, bf16[2,16,128,128]{3,2,1,0:T(8,128)(2,1)}, u32[]{:S(2)}) copy-start(bf16[2,16,128,128]{3,2,1,0:T(8,128)(2,1)} %param.5) | copy-start | bytes 3145732
  0.0 3.5 %copy-start.4 = (s32[2,32]{1,0:T(2,128)S(1)}, s32[2,32]{1,0:T(2,128)}, u32[]{:S(2)}) copy-start(s32[2,32]{1,0:T(2,128)} %param.6) | copy-start | bytes 772
  4.5 4.0 %copy-start.3 = (f32[32,256]{1,0:T(8,128)S(1)}, f32[32,256]{1,0:T(8,128)}, u32[]{:S(2)}) copy-start(f32[32,256]{1,0:T(8,128)} %param.4) | copy-start | bytes 98308
  4.7 10.0 %collective-permute-start = (f32[64,1152]{1,0:T(8,128)S(1)}, f32[64,1152]{1,0:T(8,128)S(1)}, u32[]{:S(2)}, u32[]{:S(2)}) collective-permute-start(f32[64,1152]{1,0:T(8,128)S(1)} %bitcast.44), channel_id=1, source_target_pairs={{0,2},{2,0},{1,3},{3,1},{4,6},{6,4},{5,7},{7,5},{8,10},{10,8},{9,1... | collective-permute-start | bytes 884744 | tf_op jit(solution)/shard_map/ppermute | solution.py:198
  49.5 2.9 %copy-start.1 = (bf16[8,64,1152]{2,1,0:T(8,128)(2,1)}, bf16[8,64,1152]{2,1,0:T(8,128)(2,1)S(1)}, u32[]{:S(2)}) copy-start(bf16[8,64,1152]{2,1,0:T(8,128)(2,1)S(1)} %all_to_all.5) | copy-start | bytes 3538948
  49.5 2.8 %collective-permute-start.1 = (bf16[512,1152]{1,0:T(8,128)(2,1)S(1)}, bf16[512,1152]{1,0:T(8,128)(2,1)S(1)}, u32[]{:S(2)}, u32[]{:S(2)}) collective-permute-start(bf16[512,1152]{1,0:T(8,128)(2,1)S(1)} %bitcast.42), channel_id=1, source_target_pairs={{0,1},{1,0},{2,3},{3,2},{4,5},{5,4},{6,7},{7,6},{8,9},{9,8},{10,11... | collective-permute-start | bytes 3538952 | tf_op jit(solution)/shard_map/ppermute | solution.py:212
  52.3 1.0 %copy-start.2 = (bf16[512,1152]{1,0:T(8,128)(2,1)}, bf16[512,1152]{1,0:T(8,128)(2,1)S(1)}, u32[]{:S(2)}) copy-start(bf16[512,1152]{1,0:T(8,128)(2,1)S(1)} %collective-permute-done.1.other_ref) | copy-start | bytes 3538948

commit v14 on v13

--- a/solution.py
+++ b/solution.py
@@ -68,7 +68,7 @@
     )
 
 
-def filter_kernel(index_ref, own_ref, other_ref, x_ref, whole_ref, *, n_row, n_col, vec_cols):
+def filter_kernel(index_ref, own_ref, other_ref, x_ref, whole_ref, w_ref, *, n_row, n_col, vec_cols):
     half_rows = own_ref.shape[0]
     total = 2 * half_rows
     block = own_ref.shape[1] - total
@@ -93,26 +93,28 @@
 
     whole_ref[pl.ds(own_first, vec_cols), :] = decode(own_ref)
     whole_ref[pl.ds(other_first, vec_cols), :] = decode(other_ref)
-    current = whole_ref[...]
+    w_ref[:half_rows, :half_rows] = own_ref[:, pl.ds(own_place, half_rows)]
+    w_ref[:half_rows, half_rows:] = own_ref[:, pl.ds(other_place, half_rows)]
+    w_ref[half_rows:, :half_rows] = other_ref[:, pl.ds(own_place, half_rows)]
+    w_ref[half_rows:, half_rows:] = other_ref[:, pl.ds(other_place, half_rows)]
+    current = jnp.concatenate(
+        [whole_ref[:, pl.ds(own_place, half_rows)], whole_ref[:, pl.ds(other_place, half_rows)]], axis=1
+    )
 
     def apply(values):
-        rounded = values.astype(jnp.bfloat16)
-        dims = (((1,), (1,)), ((), ()))
-        whole_ref[:, pl.ds(own_place, half_rows)] = lax.dot_general(
-            rounded, own_ref[:, :total], dims, preferred_element_type=jnp.float32
+        return lax.dot_general(
+            values.astype(jnp.bfloat16),
+            w_ref[...],
+            (((1,), (1,)), ((), ())),
+            preferred_element_type=jnp.float32,
         )
-        whole_ref[:, pl.ds(other_place, half_rows)] = lax.dot_general(
-            rounded, other_ref[:, :total], dims, preferred_element_type=jnp.float32
-        )
-        return whole_ref[...]
 
     for outer in range(ITERS):
         current = orthonormal_value(chebyshev(current, apply))
     whole_ref[...] = current
     for local in range(nb_dev):
-        place = pl.multiple_of((local * n_row + row) * block, 128)
+        place = pl.multiple_of((((local + core) % 2) * n_row + row) * block, 128)
         x_ref[:, local * block : (local + 1) * block] = whole_ref[pl.ds(own_first, vec_cols), pl.ds(place, block)]
-
 
 def filter_local(own, other, index, n_row, n_col, vec_cols):
     total = 2 * own.shape[0]
@@ -123,7 +125,10 @@
         out_shape=jax.ShapeDtypeStruct((vec_cols, nb_dev * block), jnp.float32),
         in_specs=[pl.BlockSpec(memory_space=pltpu.SMEM)] + [pl.BlockSpec(memory_space=pltpu.VMEM)] * 2,
         out_specs=pl.BlockSpec(memory_space=pltpu.VMEM),
-        scratch_shapes=[pltpu.VMEM((2 * vec_cols, total), jnp.float32)],
+        scratch_shapes=[
+            pltpu.VMEM((2 * vec_cols, total), jnp.float32),
+            pltpu.VMEM((total, total), jnp.bfloat16),
+        ],
     )(index, own, other)
 
 def distributed(start, tiles, pattern, counts):

time: 80 us -> 78.2 us (0.978)
  Pallas kernels: 26.5 us -> 24.7 us
    pallas_call x1, Pallas kernels: 26.5 us -> 24.7 us  [filter_local(): pl.pallas_call(functools.partial(filter_kernel, n_row=n_row, n_col=n_col,...]
where the time goes in v14:
time: 78.2 us; the launch traced here: 78 us
  blocking collectives  33.9 us (43%)
  Pallas kernels  24.7 us (32%)
  waiting for transfers between devices  8.29 us (11%)
  local copies, waits for them, and re-layouts  3.86 us (5%)
  starting transfers between devices  3 us (4%)
  other arithmetic  2.99 us (4%)
  between operations  0.87 us (1%)
    all_to_all x1, blocking collectives, replicated(): half = lax.all_to_all(copies, ('row', 'col'), 0, 0, tiled=True)  33.9 us
    pallas_call x1, Pallas kernels, filter_local(): pl.pallas_call(functools.partial(filter_kernel, n_row=n_row, n_col=n_col,...  24.7 us
    ppermute x1, waiting for transfers between devices, replicated(): lax.ppermute(sent, 'col', [(i, (i + shift) % n_col) for i in range(n_col)])  6.12 us
    ppermute x1, starting transfers between devices, replicated(): lax.ppermute(sent, 'col', [(i, (i + shift) % n_col) for i in range(n_col)])  2.99 us
    ppermute x1, waiting for transfers between devices, replicated(): other = lax.ppermute(half, 'vec', [(0, 1), (1, 0)])  2.16 us
  transfers between devices with their start and end apart: 2, of which 2 were waited for; matrix products, arithmetic and copies ran while one was open for 1% of the time, Pallas kernels for 0%

profile of v14, /device:TPU:0, one launch (start us, length us, event | category | flops | bytes accessed | tf_op | source)
XLA Modules:
  0.0 78.0 jit_solution(14635028777834124826)
XLA Ops:
  0.0 1.4 %dynamic_slice.28 = s32[1]{0:T(128)} dynamic-slice(s32[2]{0:T(128)} %param.7, s32[]{:T(128)S(6)} %select_n.51), dynamic_slice_sizes={1} | dynamic-slice | bytes 12 | tf_op jit(solution)/shard_map/jit(dynamic_index_in_dim)/dynamic_slice | solution.py:187
  1.4 0.7 fusion.22
  2.2 1.3 %fusion = f32[128]{0:T(128)S(1)} fusion(bf16[1,16,128,128]{3,2,1,0:T(8,128)(2,1)S(1)} %constant_dynamic-slice_fusion.1, bf16[16]{0:T(256)(128)(2,1)S(1)} %get-tuple-element.5), kind=kLoop, calls=%fused_computation.6 | loop fusion | flops 1048448 | bytes 524832 | tf_op jit(solution)/shard_map/kmn,kmn->m/dot_general | solution.py:196
  3.5 0.1 fusion.16
  3.5 0.4 convolution_bitcast_fusion
  3.9 0.1 concatenate.12
  4.0 0.1 broadcast_in_dim.6
  4.1 0.3 copy.13
  4.5 0.0 copy-start.3
  4.5 0.2 copy.14
  4.7 3.0 %collective-permute-start = (f32[64,1152]{1,0:T(8,128)S(1)}, f32[64,1152]{1,0:T(8,128)S(1)}, u32[]{:S(2)}, u32[]{:S(2)}) collective-permute-start(f32[64,1152]{1,0:T(8,128)S(1)} %bitcast.44), channel_id=1, source_target_pairs={{0,2},{2,0},{1,3},{3,1},{4,6},{6,4},{5,7},{7,5},{8,10},{10,8},{9,1... | collective-permute-start | bytes 884744 | tf_op jit(solution)/shard_map/ppermute | solution.py:203
  8.5 0.1 copy.24
  8.6 6.1 %collective-permute-done = f32[64,1152]{1,0:T(8,128)S(1)} collective-permute-done((f32[64,1152]{1,0:T(8,128)S(1)}, f32[64,1152]{1,0:T(8,128)S(1)}, u32[]{:S(2)}, u32[]{:S(2)}) %collective-permute-start) | collective-permute-done | bytes 294944 | tf_op jit(solution)/shard_map/ppermute | solution.py:203
  14.7 0.2 copy.15
  15.0 0.1 fusion.4
  15.1 0.1 maximum_maximum_fusion
  15.2 0.2 copy.17
  15.4 0.1 broadcast_in_dim.8
  15.5 33.9 %all_to_all.5 = bf16[8,64,1152]{2,1,0:T(8,128)(2,1)S(1)} all-to-all(bf16[8,64,1152]{2,1,0:T(8,128)(2,1)S(1)} %broadcast_in_dim.8), channel_id=1, replica_groups=mesh['grp'=2,'row'=4,'col'=2,'vec'=2] {'row','col'}, dimensions={0} | all-to-all | bytes 2359296 | tf_op jit(solution)/shard_map/all_to_all | solution.py:215
  49.5 0.0 collective-permute-start.1
  49.5 0.7 pad_add_fusion.index_ref
  50.1 2.2 %collective-permute-done.1.other_ref = bf16[512,1152]{1,0:T(8,128)(2,1)S(1)} collective-permute-done((bf16[512,1152]{1,0:T(8,128)(2,1)S(1)}, bf16[512,1152]{1,0:T(8,128)(2,1)S(1)}, u32[]{:S(2)}, u32[]{:S(2)}) %collective-permute-start.1) | collective-permute-done | bytes 1179680 | tf_op jit(solution)/shard_map/ppermute | solution.py:217
  52.3 1.0 %copy-done.2 = bf16[512,1152]{1,0:T(8,128)(2,1)} copy-done((bf16[512,1152]{1,0:T(8,128)(2,1)}, bf16[512,1152]{1,0:T(8,128)(2,1)S(1)}, u32[]{:S(2)}) %copy-start.2) | copy-done | bytes 1179672
  53.3 24.7 %shard_map.46 = f32[32,256]{1,0:T(8,128)} custom-call(s32[2]{0:T(128)} %pad_add_fusion.index_ref, bf16[512,1152]{1,0:T(8,128)(2,1)} %bitcast.43, bf16[512,1152]{1,0:T(8,128)(2,1)} %copy-done.2), custom_call_target="tpu_custom_call" | custom-call | tf_op jit(solution)/shard_map/pallas_call | solution.py:123
  (15 shorter events, 0.2 us)
Async XLA Ops:
  0.0 2.1 %copy-start = (bf16[2,16,128,128]{3,2,1,0:T(8,128)(2,1)S(1)}, bf16[2,16,128,128]{3,2,1,0:T(8,128)(2,1)}, u32[]{:S(2)}) copy-start(bf16[2,16,128,128]{3,2,1,0:T(8,128)(2,1)} %param.5) | copy-start | bytes 3145732
  0.0 3.5 %copy-start.4 = (s32[2,32]{1,0:T(2,128)S(1)}, s32[2,32]{1,0:T(2,128)}, u32[]{:S(2)}) copy-start(s32[2,32]{1,0:T(2,128)} %param.6) | copy-start | bytes 772
  4.5 4.0 %copy-start.3 = (f32[32,256]{1,0:T(8,128)S(1)}, f32[32,256]{1,0:T(8,128)}, u32[]{:S(2)}) copy-start(f32[32,256]{1,0:T(8,128)} %param.4) | copy-start | bytes 98308
  4.7 10.0 %collective-permute-start = (f32[64,1152]{1,0:T(8,128)S(1)}, f32[64,1152]{1,0:T(8,128)S(1)}, u32[]{:S(2)}, u32[]{:S(2)}) collective-permute-start(f32[64,1152]{1,0:T(8,128)S(1)} %bitcast.44), channel_id=1, source_target_pairs={{0,2},{2,0},{1,3},{3,1},{4,6},{6,4},{5,7},{7,5},{8,10},{10,8},{9,1... | collective-permute-start | bytes 884744 | tf_op jit(solution)/shard_map/ppermute | solution.py:203
  49.5 2.9 %copy-start.1 = (bf16[8,64,1152]{2,1,0:T(8,128)(2,1)}, bf16[8,64,1152]{2,1,0:T(8,128)(2,1)S(1)}, u32[]{:S(2)}) copy-start(bf16[8,64,1152]{2,1,0:T(8,128)(2,1)S(1)} %all_to_all.5) | copy-start | bytes 3538948
  49.5 2.8 %collective-permute-start.1 = (bf16[512,1152]{1,0:T(8,128)(2,1)S(1)}, bf16[512,1152]{1,0:T(8,128)(2,1)S(1)}, u32[]{:S(2)}, u32[]{:S(2)}) collective-permute-start(bf16[512,1152]{1,0:T(8,128)(2,1)S(1)} %bitcast.42), channel_id=1, source_target_pairs={{0,1},{1,0},{2,3},{3,2},{4,5},{5,4},{6,7},{7,6},{8,9},{9,8},{10,11... | collective-permute-start | bytes 3538952 | tf_op jit(solution)/shard_map/ppermute | solution.py:217
  52.3 1.0 %copy-start.2 = (bf16[512,1152]{1,0:T(8,128)(2,1)}, bf16[512,1152]{1,0:T(8,128)(2,1)S(1)}, u32[]{:S(2)}) copy-start(bf16[512,1152]{1,0:T(8,128)(2,1)S(1)} %collective-permute-done.1.other_ref) | copy-start | bytes 3538948

commit v15 on v14

--- a/solution.py
+++ b/solution.py
@@ -68,14 +68,14 @@
     )
 
 
-def filter_kernel(index_ref, own_ref, other_ref, x_ref, whole_ref, w_ref, *, n_row, n_col, vec_cols):
+def filter_kernel(own_ref, other_ref, x_ref, whole_ref, w_ref, *, n_row, n_col, vec_cols):
     half_rows = own_ref.shape[0]
     total = 2 * half_rows
     block = own_ref.shape[1] - total
     nb_dev = total // (block * n_row)
     share = 2 * vec_cols
-    row = index_ref[0]
-    core = index_ref[1]
+    row = lax.axis_index("row")
+    core = lax.axis_index("vec")
     own_first = pl.multiple_of(core * vec_cols, 8)
     other_first = pl.multiple_of((1 - core) * vec_cols, 8)
     own_place = pl.multiple_of(core * half_rows, 128)
@@ -116,20 +116,20 @@
         place = pl.multiple_of((((local + core) % 2) * n_row + row) * block, 128)
         x_ref[:, local * block : (local + 1) * block] = whole_ref[pl.ds(own_first, vec_cols), pl.ds(place, block)]
 
-def filter_local(own, other, index, n_row, n_col, vec_cols):
+def filter_local(own, other, n_row, n_col, vec_cols):
     total = 2 * own.shape[0]
     block = own.shape[1] - total
     nb_dev = total // (block * n_row)
     return pl.pallas_call(
         functools.partial(filter_kernel, n_row=n_row, n_col=n_col, vec_cols=vec_cols),
         out_shape=jax.ShapeDtypeStruct((vec_cols, nb_dev * block), jnp.float32),
-        in_specs=[pl.BlockSpec(memory_space=pltpu.SMEM)] + [pl.BlockSpec(memory_space=pltpu.VMEM)] * 2,
+        in_specs=[pl.BlockSpec(memory_space=pltpu.VMEM)] * 2,
         out_specs=pl.BlockSpec(memory_space=pltpu.VMEM),
         scratch_shapes=[
             pltpu.VMEM((2 * vec_cols, total), jnp.float32),
             pltpu.VMEM((total, total), jnp.bfloat16),
         ],
-    )(index, own, other)
+    )(own, other)
 
 def distributed(start, tiles, pattern, counts):
     nb_dev = tiles.shape[0]
@@ -215,8 +215,7 @@
     half = lax.all_to_all(copies, ("row", "col"), 0, 0, tiled=True)
     half = half.reshape(n_row * n_col * share, total_rows + block)
     other = lax.ppermute(half, "vec", [(0, 1), (1, 0)])
-    index = jnp.stack([row_index, vec_index]).astype(jnp.int32)
-    current = filter_local(half, other, index, n_row, n_col, vec_cols)
+    current = filter_local(half, other, n_row, n_col, vec_cols)
     return current
 
 

time: 78.2 us -> 78.1 us (level)
  transfers between devices with their start and end apart: 2 -> 2, of which waited for: 2 -> 2; matrix products, arithmetic and copies ran while one was open for 1% -> 0% of each run, Pallas kernels for 0% -> 0%
where the time goes in v15:
time: 78.1 us; the launch traced here: 77.9 us
  blocking collectives  33.9 us (43%)
  Pallas kernels  24.7 us (32%)
  waiting for transfers between devices  9.01 us (12%)
  local copies, waits for them, and re-layouts  3.78 us (5%)
  starting transfers between devices  3 us (4%)
  other arithmetic  2.26 us (3%)
  between operations  0.83 us (1%)
    all_to_all x1, blocking collectives, replicated(): half = lax.all_to_all(copies, ('row', 'col'), 0, 0, tiled=True)  33.9 us
    pallas_call x1, Pallas kernels, filter_local(): pl.pallas_call(functools.partial(filter_kernel, n_row=n_row, n_col=n_col,...  24.7 us
    ppermute x1, waiting for transfers between devices, replicated(): lax.ppermute(sent, 'col', [(i, (i + shift) % n_col) for i in range(n_col)])  6.17 us
    ppermute x1, starting transfers between devices, replicated(): lax.ppermute(sent, 'col', [(i, (i + shift) % n_col) for i in range(n_col)])  2.99 us
    ppermute x1, waiting for transfers between devices, replicated(): other = lax.ppermute(half, 'vec', [(0, 1), (1, 0)])  2.84 us
  transfers between devices with their start and end apart: 2, of which 2 were waited for; matrix products, arithmetic and copies ran while one was open for 0% of the time, Pallas kernels for 0%

profile of v15, /device:TPU:0, one launch (start us, length us, event | category | flops | bytes accessed | tf_op | source)
XLA Modules:
  0.0 77.9 jit_solution(17840730673693350383)
XLA Ops:
  0.0 1.3 %dynamic_slice.28 = s32[1]{0:T(128)} dynamic-slice(s32[2]{0:T(128)} %param.7, s32[]{:T(128)S(6)} %select_n.51), dynamic_slice_sizes={1} | dynamic-slice | bytes 12 | tf_op jit(solution)/shard_map/jit(dynamic_index_in_dim)/dynamic_slice | solution.py:187
  1.3 0.7 fusion.22
  2.1 1.3 %fusion = f32[128]{0:T(128)S(1)} fusion(bf16[1,16,128,128]{3,2,1,0:T(8,128)(2,1)S(1)} %constant_dynamic-slice_fusion.1, bf16[16]{0:T(256)(128)(2,1)S(1)} %get-tuple-element.5), kind=kLoop, calls=%fused_computation.6 | loop fusion | flops 1048448 | bytes 524832 | tf_op jit(solution)/shard_map/kmn,kmn->m/dot_general | solution.py:196
  3.3 0.1 fusion.16
  3.4 0.4 convolution_bitcast_fusion
  3.8 0.1 concatenate.12
  3.9 0.1 broadcast_in_dim.6
  4.0 0.3 copy.13
  4.3 0.0 copy-start.3
  4.4 0.2 copy.14
  4.6 3.0 %collective-permute-start = (f32[64,1152]{1,0:T(8,128)S(1)}, f32[64,1152]{1,0:T(8,128)S(1)}, u32[]{:S(2)}, u32[]{:S(2)}) collective-permute-start(f32[64,1152]{1,0:T(8,128)S(1)} %bitcast.42), channel_id=1, source_target_pairs={{0,2},{2,0},{1,3},{3,1},{4,6},{6,4},{5,7},{7,5},{8,10},{10,8},{9,1... | collective-permute-start | bytes 884744 | tf_op jit(solution)/shard_map/ppermute | solution.py:203
  8.3 0.0 copy-done.3
  8.3 0.1 copy.24
  8.5 6.2 %collective-permute-done = f32[64,1152]{1,0:T(8,128)S(1)} collective-permute-done((f32[64,1152]{1,0:T(8,128)S(1)}, f32[64,1152]{1,0:T(8,128)S(1)}, u32[]{:S(2)}, u32[]{:S(2)}) %collective-permute-start) | collective-permute-done | bytes 294944 | tf_op jit(solution)/shard_map/ppermute | solution.py:203
  14.6 0.2 copy.15
  14.9 0.1 fusion.4
  15.0 0.1 maximum_maximum_fusion
  15.1 0.2 copy.17
  15.2 0.1 broadcast_in_dim.8
  15.4 33.9 %all_to_all.5 = bf16[8,64,1152]{2,1,0:T(8,128)(2,1)S(1)} all-to-all(bf16[8,64,1152]{2,1,0:T(8,128)(2,1)S(1)} %broadcast_in_dim.8), channel_id=1, replica_groups=mesh['grp'=2,'row'=4,'col'=2,'vec'=2] {'row','col'}, dimensions={0} | all-to-all | bytes 2359296 | tf_op jit(solution)/shard_map/all_to_all | solution.py:215
  49.3 0.0 collective-permute-start.1
  49.3 2.8 %collective-permute-done.1.other_ref = bf16[512,1152]{1,0:T(8,128)(2,1)S(1)} collective-permute-done((bf16[512,1152]{1,0:T(8,128)(2,1)S(1)}, bf16[512,1152]{1,0:T(8,128)(2,1)S(1)}, u32[]{:S(2)}, u32[]{:S(2)}) %collective-permute-start.1) | collective-permute-done | bytes 1179680 | tf_op jit(solution)/shard_map/ppermute | solution.py:217
  52.2 1.0 %copy-done.2 = bf16[512,1152]{1,0:T(8,128)(2,1)} copy-done((bf16[512,1152]{1,0:T(8,128)(2,1)}, bf16[512,1152]{1,0:T(8,128)(2,1)S(1)}, u32[]{:S(2)}) %copy-start.2) | copy-done | bytes 1179672
  53.2 24.7 %shard_map.46 = f32[32,256]{1,0:T(8,128)} custom-call(bf16[512,1152]{1,0:T(8,128)(2,1)} %bitcast.41, bf16[512,1152]{1,0:T(8,128)(2,1)} %copy-done.2), custom_call_target="tpu_custom_call" | custom-call | tf_op jit(solution)/shard_map/pallas_call | solution.py:123
  (14 shorter events, 0.2 us)
Async XLA Ops:
  0.0 2.0 %copy-start = (bf16[2,16,128,128]{3,2,1,0:T(8,128)(2,1)S(1)}, bf16[2,16,128,128]{3,2,1,0:T(8,128)(2,1)}, u32[]{:S(2)}) copy-start(bf16[2,16,128,128]{3,2,1,0:T(8,128)(2,1)} %param.5) | copy-start | bytes 3145732
  0.0 3.3 %copy-start.4 = (s32[2,32]{1,0:T(2,128)S(1)}, s32[2,32]{1,0:T(2,128)}, u32[]{:S(2)}) copy-start(s32[2,32]{1,0:T(2,128)} %param.6) | copy-start | bytes 772
  4.3 4.0 %copy-start.3 = (f32[32,256]{1,0:T(8,128)S(1)}, f32[32,256]{1,0:T(8,128)}, u32[]{:S(2)}) copy-start(f32[32,256]{1,0:T(8,128)} %param.4) | copy-start | bytes 98308
  4.6 10.0 %collective-permute-start = (f32[64,1152]{1,0:T(8,128)S(1)}, f32[64,1152]{1,0:T(8,128)S(1)}, u32[]{:S(2)}, u32[]{:S(2)}) collective-permute-start(f32[64,1152]{1,0:T(8,128)S(1)} %bitcast.42), channel_id=1, source_target_pairs={{0,2},{2,0},{1,3},{3,1},{4,6},{6,4},{5,7},{7,5},{8,10},{10,8},{9,1... | collective-permute-start | bytes 884744 | tf_op jit(solution)/shard_map/ppermute | solution.py:203
  49.3 2.9 %copy-start.1 = (bf16[8,64,1152]{2,1,0:T(8,128)(2,1)}, bf16[8,64,1152]{2,1,0:T(8,128)(2,1)S(1)}, u32[]{:S(2)}) copy-start(bf16[8,64,1152]{2,1,0:T(8,128)(2,1)S(1)} %all_to_all.5) | copy-start | bytes 3538948
  49.3 2.8 %collective-permute-start.1 = (bf16[512,1152]{1,0:T(8,128)(2,1)S(1)}, bf16[512,1152]{1,0:T(8,128)(2,1)S(1)}, u32[]{:S(2)}, u32[]{:S(2)}) collective-permute-start(bf16[512,1152]{1,0:T(8,128)(2,1)S(1)} %bitcast.40), channel_id=1, source_target_pairs={{0,1},{1,0},{2,3},{3,2},{4,5},{5,4},{6,7},{7,6},{8,9},{9,8},{10,11... | collective-permute-start | bytes 3538952 | tf_op jit(solution)/shard_map/ppermute | solution.py:217
  52.2 1.0 %copy-start.2 = (bf16[512,1152]{1,0:T(8,128)(2,1)}, bf16[512,1152]{1,0:T(8,128)(2,1)S(1)}, u32[]{:S(2)}) copy-start(bf16[512,1152]{1,0:T(8,128)(2,1)S(1)} %collective-permute-done.1.other_ref) | copy-start | bytes 3538948

commit v16 on v15

--- a/solution.py
+++ b/solution.py
@@ -93,10 +93,10 @@
 
     whole_ref[pl.ds(own_first, vec_cols), :] = decode(own_ref)
     whole_ref[pl.ds(other_first, vec_cols), :] = decode(other_ref)
-    w_ref[:half_rows, :half_rows] = own_ref[:, pl.ds(own_place, half_rows)]
-    w_ref[:half_rows, half_rows:] = own_ref[:, pl.ds(other_place, half_rows)]
-    w_ref[half_rows:, :half_rows] = other_ref[:, pl.ds(own_place, half_rows)]
-    w_ref[half_rows:, half_rows:] = other_ref[:, pl.ds(other_place, half_rows)]
+    w_ref[:half_rows, :half_rows] = own_ref[:, pl.ds(own_place, half_rows)].T
+    w_ref[half_rows:, :half_rows] = own_ref[:, pl.ds(other_place, half_rows)].T
+    w_ref[:half_rows, half_rows:] = other_ref[:, pl.ds(own_place, half_rows)].T
+    w_ref[half_rows:, half_rows:] = other_ref[:, pl.ds(other_place, half_rows)].T
     current = jnp.concatenate(
         [whole_ref[:, pl.ds(own_place, half_rows)], whole_ref[:, pl.ds(other_place, half_rows)]], axis=1
     )
@@ -105,7 +105,7 @@
         return lax.dot_general(
             values.astype(jnp.bfloat16),
             w_ref[...],
-            (((1,), (1,)), ((), ())),
+            (((1,), (0,)), ((), ())),
             preferred_element_type=jnp.float32,
         )
 

time: 78.1 us -> 74.8 us (0.958)
  Pallas kernels: 24.7 us -> 21.4 us
    pallas_call x1, Pallas kernels: 24.7 us -> 21.4 us  [filter_local(): pl.pallas_call(functools.partial(filter_kernel, n_row=n_row, n_col=n_col,...]
where the time goes in v16:
time: 74.8 us; the launch traced here: 74.6 us
  blocking collectives  33.9 us (45%)
  Pallas kernels  21.4 us (29%)
  waiting for transfers between devices  9.01 us (12%)
  local copies, waits for them, and re-layouts  3.78 us (5%)
  starting transfers between devices  3 us (4%)
  other arithmetic  2.26 us (3%)
  between operations  0.83 us (1%)
    all_to_all x1, blocking collectives, replicated(): half = lax.all_to_all(copies, ('row', 'col'), 0, 0, tiled=True)  33.9 us
    pallas_call x1, Pallas kernels, filter_local(): pl.pallas_call(functools.partial(filter_kernel, n_row=n_row, n_col=n_col,...  21.4 us
    ppermute x1, waiting for transfers between devices, replicated(): lax.ppermute(sent, 'col', [(i, (i + shift) % n_col) for i in range(n_col)])  6.17 us
    ppermute x1, starting transfers between devices, replicated(): lax.ppermute(sent, 'col', [(i, (i + shift) % n_col) for i in range(n_col)])  2.99 us
    ppermute x1, waiting for transfers between devices, replicated(): other = lax.ppermute(half, 'vec', [(0, 1), (1, 0)])  2.84 us
  transfers between devices with their start and end apart: 2, of which 2 were waited for; matrix products, arithmetic and copies ran while one was open for 0% of the time, Pallas kernels for 0%

profile of v16, /device:TPU:0, one launch (start us, length us, event | category | flops | bytes accessed | tf_op | source)
XLA Modules:
  0.0 74.6 jit_solution(6674240909199634830)
XLA Ops:
  0.0 0.0 copy-start
  0.0 1.3 %dynamic_slice.28 = s32[1]{0:T(128)} dynamic-slice(s32[2]{0:T(128)} %param.7, s32[]{:T(128)S(6)} %select_n.51), dynamic_slice_sizes={1} | dynamic-slice | bytes 12 | tf_op jit(solution)/shard_map/jit(dynamic_index_in_dim)/dynamic_slice | solution.py:187
  1.3 0.7 fusion.22
  2.1 1.3 %fusion = f32[128]{0:T(128)S(1)} fusion(bf16[1,16,128,128]{3,2,1,0:T(8,128)(2,1)S(1)} %constant_dynamic-slice_fusion.1, bf16[16]{0:T(256)(128)(2,1)S(1)} %get-tuple-element.5), kind=kLoop, calls=%fused_computation.6 | loop fusion | flops 1048448 | bytes 524832 | tf_op jit(solution)/shard_map/kmn,kmn->m/dot_general | solution.py:196
  3.3 0.1 fusion.16
  3.4 0.4 convolution_bitcast_fusion
  3.8 0.1 concatenate.12
  3.9 0.1 broadcast_in_dim.6
  4.0 0.3 copy.13
  4.3 0.0 copy-start.3
  4.4 0.2 copy.14
  4.6 3.0 %collective-permute-start = (f32[64,1152]{1,0:T(8,128)S(1)}, f32[64,1152]{1,0:T(8,128)S(1)}, u32[]{:S(2)}, u32[]{:S(2)}) collective-permute-start(f32[64,1152]{1,0:T(8,128)S(1)} %bitcast.42), channel_id=1, source_target_pairs={{0,2},{2,0},{1,3},{3,1},{4,6},{6,4},{5,7},{7,5},{8,10},{10,8},{9,1... | collective-permute-start | bytes 884744 | tf_op jit(solution)/shard_map/ppermute | solution.py:203
  8.3 0.1 copy.24
  8.5 6.2 %collective-permute-done = f32[64,1152]{1,0:T(8,128)S(1)} collective-permute-done((f32[64,1152]{1,0:T(8,128)S(1)}, f32[64,1152]{1,0:T(8,128)S(1)}, u32[]{:S(2)}, u32[]{:S(2)}) %collective-permute-start) | collective-permute-done | bytes 294944 | tf_op jit(solution)/shard_map/ppermute | solution.py:203
  14.6 0.2 copy.15
  14.9 0.1 fusion.4
  15.0 0.1 maximum_maximum_fusion
  15.1 0.2 copy.17
  15.2 0.1 broadcast_in_dim.8
  15.4 33.9 %all_to_all.5 = bf16[8,64,1152]{2,1,0:T(8,128)(2,1)S(1)} all-to-all(bf16[8,64,1152]{2,1,0:T(8,128)(2,1)S(1)} %broadcast_in_dim.8), channel_id=1, replica_groups=mesh['grp'=2,'row'=4,'col'=2,'vec'=2] {'row','col'}, dimensions={0} | all-to-all | bytes 2359296 | tf_op jit(solution)/shard_map/all_to_all | solution.py:215
  49.3 0.0 collective-permute-start.1
  49.3 2.8 %collective-permute-done.1.other_ref = bf16[512,1152]{1,0:T(8,128)(2,1)S(1)} collective-permute-done((bf16[512,1152]{1,0:T(8,128)(2,1)S(1)}, bf16[512,1152]{1,0:T(8,128)(2,1)S(1)}, u32[]{:S(2)}, u32[]{:S(2)}) %collective-permute-start.1) | collective-permute-done | bytes 1179680 | tf_op jit(solution)/shard_map/ppermute | solution.py:217
  52.2 1.0 %copy-done.2 = bf16[512,1152]{1,0:T(8,128)(2,1)} copy-done((bf16[512,1152]{1,0:T(8,128)(2,1)}, bf16[512,1152]{1,0:T(8,128)(2,1)S(1)}, u32[]{:S(2)}) %copy-start.2) | copy-done | bytes 1179672
  53.2 21.4 %shard_map.46 = f32[32,256]{1,0:T(8,128)} custom-call(bf16[512,1152]{1,0:T(8,128)(2,1)} %bitcast.41, bf16[512,1152]{1,0:T(8,128)(2,1)} %copy-done.2), custom_call_target="tpu_custom_call" | custom-call | tf_op jit(solution)/shard_map/pallas_call | solution.py:123
  (14 shorter events, 0.2 us)
Async XLA Ops:
  0.0 2.0 %copy-start = (bf16[2,16,128,128]{3,2,1,0:T(8,128)(2,1)S(1)}, bf16[2,16,128,128]{3,2,1,0:T(8,128)(2,1)}, u32[]{:S(2)}) copy-start(bf16[2,16,128,128]{3,2,1,0:T(8,128)(2,1)} %param.5) | copy-start | bytes 3145732
  0.0 3.3 %copy-start.4 = (s32[2,32]{1,0:T(2,128)S(1)}, s32[2,32]{1,0:T(2,128)}, u32[]{:S(2)}) copy-start(s32[2,32]{1,0:T(2,128)} %param.6) | copy-start | bytes 772
  4.3 4.0 %copy-start.3 = (f32[32,256]{1,0:T(8,128)S(1)}, f32[32,256]{1,0:T(8,128)}, u32[]{:S(2)}) copy-start(f32[32,256]{1,0:T(8,128)} %param.4) | copy-start | bytes 98308
  4.6 10.0 %collective-permute-start = (f32[64,1152]{1,0:T(8,128)S(1)}, f32[64,1152]{1,0:T(8,128)S(1)}, u32[]{:S(2)}, u32[]{:S(2)}) collective-permute-start(f32[64,1152]{1,0:T(8,128)S(1)} %bitcast.42), channel_id=1, source_target_pairs={{0,2},{2,0},{1,3},{3,1},{4,6},{6,4},{5,7},{7,5},{8,10},{10,8},{9,1... | collective-permute-start | bytes 884744 | tf_op jit(solution)/shard_map/ppermute | solution.py:203
  49.3 2.9 %copy-start.1 = (bf16[8,64,1152]{2,1,0:T(8,128)(2,1)}, bf16[8,64,1152]{2,1,0:T(8,128)(2,1)S(1)}, u32[]{:S(2)}) copy-start(bf16[8,64,1152]{2,1,0:T(8,128)(2,1)S(1)} %all_to_all.5) | copy-start | bytes 3538948
  49.3 2.8 %collective-permute-start.1 = (bf16[512,1152]{1,0:T(8,128)(2,1)S(1)}, bf16[512,1152]{1,0:T(8,128)(2,1)S(1)}, u32[]{:S(2)}, u32[]{:S(2)}) collective-permute-start(bf16[512,1152]{1,0:T(8,128)(2,1)S(1)} %bitcast.40), channel_id=1, source_target_pairs={{0,1},{1,0},{2,3},{3,2},{4,5},{5,4},{6,7},{7,6},{8,9},{9,8},{10,11... | collective-permute-start | bytes 3538952 | tf_op jit(solution)/shard_map/ppermute | solution.py:217
  52.2 1.0 %copy-start.2 = (bf16[512,1152]{1,0:T(8,128)(2,1)}, bf16[512,1152]{1,0:T(8,128)(2,1)S(1)}, u32[]{:S(2)}) copy-start(bf16[512,1152]{1,0:T(8,128)(2,1)S(1)} %collective-permute-done.1.other_ref) | copy-start | bytes 3538948

commit v17 on v16

--- a/solution.py
+++ b/solution.py
@@ -48,7 +48,6 @@
     rows = lax.broadcasted_iota(jnp.int32, (n, n), 0)
     cols = lax.broadcasted_iota(jnp.int32, (n, n), 1)
     inverse = (rows == cols).astype(jnp.float32)
-    diagonal = jnp.zeros((n, 1), jnp.float32)
     for k in range(n):
         top = (k // 8) * 8
         pivot = a[k : k + 1, k : k + 1]
@@ -61,7 +60,7 @@
             inverse = jnp.concatenate([inverse[:top], lower_inverse], axis=0)
         else:
             a, inverse = lower_a, lower_inverse
-        diagonal = jnp.where(rows[:, :1] == k, pivot, diagonal)
+    diagonal = jnp.sum(jnp.where(rows == cols, a, 0.0), axis=1, keepdims=True)
     inverse = inverse / jnp.sqrt(diagonal)
     return lax.dot_general(
         inverse, y, (((1,), (0,)), ((), ())), precision=hi, preferred_element_type=jnp.float32

time: 74.8 us -> 74.3 us (level)
  no operation moved by 1% of the time
where the time goes in v17:
time: 74.3 us; the launch traced here: 74.1 us
  blocking collectives  33.9 us (46%)
  Pallas kernels  20.9 us (28%)
  waiting for transfers between devices  9.01 us (12%)
  local copies, waits for them, and re-layouts  3.78 us (5%)
  starting transfers between devices  3 us (4%)
  other arithmetic  2.26 us (3%)
  between operations  0.83 us (1%)
    all_to_all x1, blocking collectives, replicated(): half = lax.all_to_all(copies, ('row', 'col'), 0, 0, tiled=True)  33.9 us
    pallas_call x1, Pallas kernels, filter_local(): pl.pallas_call(functools.partial(filter_kernel, n_row=n_row, n_col=n_col,...  20.9 us
    ppermute x1, waiting for transfers between devices, replicated(): lax.ppermute(sent, 'col', [(i, (i + shift) % n_col) for i in range(n_col)])  6.17 us
    ppermute x1, starting transfers between devices, replicated(): lax.ppermute(sent, 'col', [(i, (i + shift) % n_col) for i in range(n_col)])  2.99 us
    ppermute x1, waiting for transfers between devices, replicated(): other = lax.ppermute(half, 'vec', [(0, 1), (1, 0)])  2.84 us
  transfers between devices with their start and end apart: 2, of which 2 were waited for; matrix products, arithmetic and copies ran while one was open for 0% of the time, Pallas kernels for 0%

profile of v17, /device:TPU:0, one launch (start us, length us, event | category | flops | bytes accessed | tf_op | source)
XLA Modules:
  0.0 74.1 jit_solution(4391596622068201578)
XLA Ops:
  0.0 1.3 %dynamic_slice.28 = s32[1]{0:T(128)} dynamic-slice(s32[2]{0:T(128)} %param.7, s32[]{:T(128)S(6)} %select_n.51), dynamic_slice_sizes={1} | dynamic-slice | bytes 12 | tf_op jit(solution)/shard_map/jit(dynamic_index_in_dim)/dynamic_slice | solution.py:186
  1.3 0.7 fusion.22
  2.1 1.3 %fusion = f32[128]{0:T(128)S(1)} fusion(bf16[1,16,128,128]{3,2,1,0:T(8,128)(2,1)S(1)} %constant_dynamic-slice_fusion.1, bf16[16]{0:T(256)(128)(2,1)S(1)} %get-tuple-element.5), kind=kLoop, calls=%fused_computation.6 | loop fusion | flops 1048448 | bytes 524832 | tf_op jit(solution)/shard_map/kmn,kmn->m/dot_general | solution.py:195
  3.3 0.1 fusion.16
  3.4 0.4 convolution_bitcast_fusion
  3.8 0.1 concatenate.12
  3.9 0.1 broadcast_in_dim.6
  4.0 0.3 copy.13
  4.3 0.0 copy-start.3
  4.4 0.2 copy.14
  4.6 3.0 %collective-permute-start = (f32[64,1152]{1,0:T(8,128)S(1)}, f32[64,1152]{1,0:T(8,128)S(1)}, u32[]{:S(2)}, u32[]{:S(2)}) collective-permute-start(f32[64,1152]{1,0:T(8,128)S(1)} %bitcast.42), channel_id=1, source_target_pairs={{0,2},{2,0},{1,3},{3,1},{4,6},{6,4},{5,7},{7,5},{8,10},{10,8},{9,1... | collective-permute-start | bytes 884744 | tf_op jit(solution)/shard_map/ppermute | solution.py:202
  8.3 0.0 copy-done.3
  8.3 0.1 copy.24
  8.5 6.2 %collective-permute-done = f32[64,1152]{1,0:T(8,128)S(1)} collective-permute-done((f32[64,1152]{1,0:T(8,128)S(1)}, f32[64,1152]{1,0:T(8,128)S(1)}, u32[]{:S(2)}, u32[]{:S(2)}) %collective-permute-start) | collective-permute-done | bytes 294944 | tf_op jit(solution)/shard_map/ppermute | solution.py:202
  14.6 0.2 copy.15
  14.9 0.1 fusion.4
  15.0 0.1 maximum_maximum_fusion
  15.1 0.2 copy.17
  15.2 0.1 broadcast_in_dim.8
  15.4 33.9 %all_to_all.5 = bf16[8,64,1152]{2,1,0:T(8,128)(2,1)S(1)} all-to-all(bf16[8,64,1152]{2,1,0:T(8,128)(2,1)S(1)} %broadcast_in_dim.8), channel_id=1, replica_groups=mesh['grp'=2,'row'=4,'col'=2,'vec'=2] {'row','col'}, dimensions={0} | all-to-all | bytes 2359296 | tf_op jit(solution)/shard_map/all_to_all | solution.py:214
  49.3 0.0 collective-permute-start.1
  49.3 2.8 %collective-permute-done.1.other_ref = bf16[512,1152]{1,0:T(8,128)(2,1)S(1)} collective-permute-done((bf16[512,1152]{1,0:T(8,128)(2,1)S(1)}, bf16[512,1152]{1,0:T(8,128)(2,1)S(1)}, u32[]{:S(2)}, u32[]{:S(2)}) %collective-permute-start.1) | collective-permute-done | bytes 1179680 | tf_op jit(solution)/shard_map/ppermute | solution.py:216
  52.2 1.0 %copy-done.2 = bf16[512,1152]{1,0:T(8,128)(2,1)} copy-done((bf16[512,1152]{1,0:T(8,128)(2,1)}, bf16[512,1152]{1,0:T(8,128)(2,1)S(1)}, u32[]{:S(2)}) %copy-start.2) | copy-done | bytes 1179672
  53.2 20.9 %shard_map.46 = f32[32,256]{1,0:T(8,128)} custom-call(bf16[512,1152]{1,0:T(8,128)(2,1)} %bitcast.41, bf16[512,1152]{1,0:T(8,128)(2,1)} %copy-done.2), custom_call_target="tpu_custom_call" | custom-call | tf_op jit(solution)/shard_map/pallas_call | solution.py:122
  (14 shorter events, 0.2 us)
Async XLA Ops:
  0.0 2.0 %copy-start = (bf16[2,16,128,128]{3,2,1,0:T(8,128)(2,1)S(1)}, bf16[2,16,128,128]{3,2,1,0:T(8,128)(2,1)}, u32[]{:S(2)}) copy-start(bf16[2,16,128,128]{3,2,1,0:T(8,128)(2,1)} %param.5) | copy-start | bytes 3145732
  0.0 3.3 %copy-start.4 = (s32[2,32]{1,0:T(2,128)S(1)}, s32[2,32]{1,0:T(2,128)}, u32[]{:S(2)}) copy-start(s32[2,32]{1,0:T(2,128)} %param.6) | copy-start | bytes 772
  4.3 4.0 %copy-start.3 = (f32[32,256]{1,0:T(8,128)S(1)}, f32[32,256]{1,0:T(8,128)}, u32[]{:S(2)}) copy-start(f32[32,256]{1,0:T(8,128)} %param.4) | copy-start | bytes 98308
  4.6 10.0 %collective-permute-start = (f32[64,1152]{1,0:T(8,128)S(1)}, f32[64,1152]{1,0:T(8,128)S(1)}, u32[]{:S(2)}, u32[]{:S(2)}) collective-permute-start(f32[64,1152]{1,0:T(8,128)S(1)} %bitcast.42), channel_id=1, source_target_pairs={{0,2},{2,0},{1,3},{3,1},{4,6},{6,4},{5,7},{7,5},{8,10},{10,8},{9,1... | collective-permute-start | bytes 884744 | tf_op jit(solution)/shard_map/ppermute | solution.py:202
  49.3 2.9 %copy-start.1 = (bf16[8,64,1152]{2,1,0:T(8,128)(2,1)}, bf16[8,64,1152]{2,1,0:T(8,128)(2,1)S(1)}, u32[]{:S(2)}) copy-start(bf16[8,64,1152]{2,1,0:T(8,128)(2,1)S(1)} %all_to_all.5) | copy-start | bytes 3538948
  49.3 2.8 %collective-permute-start.1 = (bf16[512,1152]{1,0:T(8,128)(2,1)S(1)}, bf16[512,1152]{1,0:T(8,128)(2,1)S(1)}, u32[]{:S(2)}, u32[]{:S(2)}) collective-permute-start(bf16[512,1152]{1,0:T(8,128)(2,1)S(1)} %bitcast.40), channel_id=1, source_target_pairs={{0,1},{1,0},{2,3},{3,2},{4,5},{5,4},{6,7},{7,6},{8,9},{9,8},{10,11... | collective-permute-start | bytes 3538952 | tf_op jit(solution)/shard_map/ppermute | solution.py:216
  52.2 1.0 %copy-start.2 = (bf16[512,1152]{1,0:T(8,128)(2,1)}, bf16[512,1152]{1,0:T(8,128)(2,1)S(1)}, u32[]{:S(2)}) copy-start(bf16[512,1152]{1,0:T(8,128)(2,1)S(1)} %collective-permute-done.1.other_ref) | copy-start | bytes 3538948

commit v18 on v17

--- a/solution.py
+++ b/solution.py
@@ -179,7 +179,6 @@
     col_index = lax.axis_index("col")
     vec_index = lax.axis_index("vec")
 
-    own_tiles = lax.dynamic_index_in_dim(tiles, vec_index, 0, keepdims=False)
     own_pattern = lax.dynamic_slice_in_dim(
         lax.dynamic_index_in_dim(pattern, vec_index, 0, keepdims=False), col_index * kb_dev, kb_dev, 0
     )
@@ -188,11 +187,13 @@
     live = slot_ids < own_count
     position = (own_pattern % nb_dev) * n_row + own_pattern // nb_dev
     onehot = (position[:, None] == jnp.arange(nblk, dtype=jnp.int32)) & live[:, None]
+    own_block = (jnp.arange(nb_dev, dtype=jnp.int32) == vec_index)[:, None]
+    weights = (own_block[:, :, None] & onehot[None]).astype(jnp.bfloat16)
     dense = jnp.einsum(
-        "kj,kmn->mjn", onehot.astype(jnp.bfloat16), own_tiles, preferred_element_type=jnp.float32
+        "bkj,bkmn->mjn", weights, tiles, preferred_element_type=jnp.float32
     ).reshape(block, total_rows)
-    masked = own_tiles * live.astype(jnp.bfloat16)[:, None, None]
-    squares = jnp.einsum("kmn,kmn->m", masked, masked, preferred_element_type=jnp.float32)
+    masked = tiles * (own_block & live[None]).astype(jnp.bfloat16)[:, :, None, None]
+    squares = jnp.einsum("bkmn,bkmn->m", masked, masked, preferred_element_type=jnp.float32)
     squares = jnp.broadcast_to(squares[:, None], (block, 128))
     partial = jnp.concatenate([dense, squares], axis=1)
     chunks = partial.reshape(n_col, share, total_rows + 128)

time: 74.3 us -> 75.8 us (1.020)
  other arithmetic: 2.26 us -> 3.42 us
where the time goes in v18:
time: 75.8 us; the launch traced here: 75.5 us
  blocking collectives  33.9 us (45%)
  Pallas kernels  20.9 us (28%)
  waiting for transfers between devices  9.01 us (12%)
  local copies, waits for them, and re-layouts  3.74 us (5%)
  other arithmetic  3.42 us (5%)
  starting transfers between devices  3 us (4%)
  between operations  0.83 us (1%)
    all_to_all x1, blocking collectives, replicated(): half = lax.all_to_all(copies, ('row', 'col'), 0, 0, tiled=True)  33.9 us
    pallas_call x1, Pallas kernels, filter_local(): pl.pallas_call(functools.partial(filter_kernel, n_row=n_row, n_col=n_col,...  20.9 us
    ppermute x1, waiting for transfers between devices, replicated(): lax.ppermute(sent, 'col', [(i, (i + shift) % n_col) for i in range(n_col)])  6.17 us
    ppermute x1, starting transfers between devices, replicated(): lax.ppermute(sent, 'col', [(i, (i + shift) % n_col) for i in range(n_col)])  2.99 us
    ppermute x1, waiting for transfers between devices, replicated(): other = lax.ppermute(half, 'vec', [(0, 1), (1, 0)])  2.84 us
    dot_general x1, other arithmetic, replicated(): jnp.einsum('bkmn,bkmn->m', masked, masked, preferred_element_type=jnp.flo...  1.65 us
  transfers between devices with their start and end apart: 2, of which 2 were waited for; matrix products, arithmetic and copies ran while one was open for 0% of the time, Pallas kernels for 0%

profile of v18, /device:TPU:0, one launch (start us, length us, event | category | flops | bytes accessed | tf_op | source)
XLA Modules:
  0.0 75.5 jit_solution(12605973237634665424)
XLA Ops:
  0.0 0.0 copy-start
  0.0 1.3 %dynamic_slice.23 = s32[1]{0:T(128)} dynamic-slice(s32[2]{0:T(128)} %param.7, s32[]{:T(128)S(6)} %select_n.49), dynamic_slice_sizes={1} | dynamic-slice | bytes 12 | tf_op jit(solution)/shard_map/jit(dynamic_index_in_dim)/dynamic_slice | solution.py:185
  1.4 0.7 add_compare_fusion
  2.0 0.8 %fusion.14 = s32[16]{0:T(128)S(1)} fusion(s32[2,32]{1,0:T(2,128)} %param.6, s32[]{:T(128)S(6)} %select_n.50, s32[]{:T(128)S(6)} %select_n.52), kind=kLoop, calls=%fused_computation.32 | loop fusion | flops 336 | bytes 136 | tf_op jit(solution)/shard_map/add | solution.py:188
  2.8 0.1 and_convert_fusion
  2.9 1.6 %fusion = f32[128]{0:T(128)S(1)} fusion(bf16[2,16,128,128]{3,2,1,0:T(8,128)(2,1)} %param.5, bf16[2,16]{1,0:T(2,128)(2,1)S(1)} %and_convert_fusion), kind=kLoop, calls=%fused_computation.1 | loop fusion | flops 2097024 | bytes 1049152 | tf_op jit(solution)/shard_map/bkmn,bkmn->m/dot_general | solution.py:196
  4.5 0.1 broadcast_in_dim.6
  4.6 0.7 convolution_bitcast_fusion
  5.3 0.1 concatenate.12
  5.4 0.3 copy.13
  5.8 0.2 copy.14
  6.0 3.0 %collective-permute-start = (f32[64,1152]{1,0:T(8,128)S(1)}, f32[64,1152]{1,0:T(8,128)S(1)}, u32[]{:S(2)}, u32[]{:S(2)}) collective-permute-start(f32[64,1152]{1,0:T(8,128)S(1)} %bitcast.35), channel_id=1, source_target_pairs={{0,2},{2,0},{1,3},{3,1},{4,6},{6,4},{5,7},{7,5},{8,10},{10,8},{9,1... | collective-permute-start | bytes 884744 | tf_op jit(solution)/shard_map/ppermute | solution.py:203
  9.8 0.1 copy.25
  9.9 6.2 %collective-permute-done = f32[64,1152]{1,0:T(8,128)S(1)} collective-permute-done((f32[64,1152]{1,0:T(8,128)S(1)}, f32[64,1152]{1,0:T(8,128)S(1)}, u32[]{:S(2)}, u32[]{:S(2)}) %collective-permute-start) | collective-permute-done | bytes 294944 | tf_op jit(solution)/shard_map/ppermute | solution.py:203
  16.0 0.2 copy.15
  16.3 0.1 fusion.5
  16.4 0.1 maximum_maximum_fusion
  16.5 0.2 copy.17
  16.7 0.1 broadcast_in_dim.8
  16.8 33.9 %all_to_all.5 = bf16[8,64,1152]{2,1,0:T(8,128)(2,1)S(1)} all-to-all(bf16[8,64,1152]{2,1,0:T(8,128)(2,1)S(1)} %broadcast_in_dim.8), channel_id=1, replica_groups=mesh['grp'=2,'row'=4,'col'=2,'vec'=2] {'row','col'}, dimensions={0} | all-to-all | bytes 2359296 | tf_op jit(solution)/shard_map/all_to_all | solution.py:215
  50.8 0.0 collective-permute-start.1
  50.8 2.8 %collective-permute-done.1.other_ref = bf16[512,1152]{1,0:T(8,128)(2,1)S(1)} collective-permute-done((bf16[512,1152]{1,0:T(8,128)(2,1)S(1)}, bf16[512,1152]{1,0:T(8,128)(2,1)S(1)}, u32[]{:S(2)}, u32[]{:S(2)}) %collective-permute-start.1) | collective-permute-done | bytes 1179680 | tf_op jit(solution)/shard_map/ppermute | solution.py:217
  53.6 1.0 %copy-done.3 = bf16[512,1152]{1,0:T(8,128)(2,1)} copy-done((bf16[512,1152]{1,0:T(8,128)(2,1)}, bf16[512,1152]{1,0:T(8,128)(2,1)S(1)}, u32[]{:S(2)}) %copy-start.3) | copy-done | bytes 1179672
  54.6 20.9 %shard_map.46 = f32[32,256]{1,0:T(8,128)} custom-call(bf16[512,1152]{1,0:T(8,128)(2,1)} %bitcast.34, bf16[512,1152]{1,0:T(8,128)(2,1)} %copy-done.3), custom_call_target="tpu_custom_call" | custom-call | tf_op jit(solution)/shard_map/pallas_call | solution.py:122
  (14 shorter events, 0.2 us)
Async XLA Ops:
  0.0 9.7 %copy-start = (f32[32,256]{1,0:T(8,128)S(1)}, f32[32,256]{1,0:T(8,128)}, u32[]{:S(2)}) copy-start(f32[32,256]{1,0:T(8,128)} %param.4) | copy-start | bytes 98308
  0.0 4.6 %copy-start.2 = (bf16[2,16,128,128]{3,2,1,0:T(8,128)(2,1)S(1)}, bf16[2,16,128,128]{3,2,1,0:T(8,128)(2,1)}, u32[]{:S(2)}) copy-start(bf16[2,16,128,128]{3,2,1,0:T(8,128)(2,1)} %param.5) | copy-start | bytes 3145732
  6.0 10.0 %collective-permute-start = (f32[64,1152]{1,0:T(8,128)S(1)}, f32[64,1152]{1,0:T(8,128)S(1)}, u32[]{:S(2)}, u32[]{:S(2)}) collective-permute-start(f32[64,1152]{1,0:T(8,128)S(1)} %bitcast.35), channel_id=1, source_target_pairs={{0,2},{2,0},{1,3},{3,1},{4,6},{6,4},{5,7},{7,5},{8,10},{10,8},{9,1... | collective-permute-start | bytes 884744 | tf_op jit(solution)/shard_map/ppermute | solution.py:203
  50.8 2.9 %copy-start.1 = (bf16[8,64,1152]{2,1,0:T(8,128)(2,1)}, bf16[8,64,1152]{2,1,0:T(8,128)(2,1)S(1)}, u32[]{:S(2)}) copy-start(bf16[8,64,1152]{2,1,0:T(8,128)(2,1)S(1)} %all_to_all.5) | copy-start | bytes 3538948
  50.8 2.8 %collective-permute-start.1 = (bf16[512,1152]{1,0:T(8,128)(2,1)S(1)}, bf16[512,1152]{1,0:T(8,128)(2,1)S(1)}, u32[]{:S(2)}, u32[]{:S(2)}) collective-permute-start(bf16[512,1152]{1,0:T(8,128)(2,1)S(1)} %bitcast.33), channel_id=1, source_target_pairs={{0,1},{1,0},{2,3},{3,2},{4,5},{5,4},{6,7},{7,6},{8,9},{9,8},{10,11... | collective-permute-start | bytes 3538952 | tf_op jit(solution)/shard_map/ppermute | solution.py:217
  53.6 1.0 %copy-start.3 = (bf16[512,1152]{1,0:T(8,128)(2,1)}, bf16[512,1152]{1,0:T(8,128)(2,1)S(1)}, u32[]{:S(2)}) copy-start(bf16[512,1152]{1,0:T(8,128)(2,1)S(1)} %collective-permute-done.1.other_ref) | copy-start | bytes 3538948

commit v19 on v17

--- a/solution.py
+++ b/solution.py
@@ -40,7 +40,7 @@
     return lax.dynamic_slice_in_dim(solved, lax.axis_index("vec") * width, width, 0)
 
 
-def orthonormal_value(y):
+def orthonormal_factor(y):
     n, total = y.shape
     hi = lax.Precision.HIGHEST
     a = lax.dot_general(y, y, (((1,), (1,)), ((), ())), precision=hi, preferred_element_type=jnp.float32)
@@ -61,13 +61,17 @@
         else:
             a, inverse = lower_a, lower_inverse
     diagonal = jnp.sum(jnp.where(rows == cols, a, 0.0), axis=1, keepdims=True)
-    inverse = inverse / jnp.sqrt(diagonal)
+    return inverse / jnp.sqrt(diagonal)
+
+
+def orthonormal_value(y):
     return lax.dot_general(
-        inverse, y, (((1,), (0,)), ((), ())), precision=hi, preferred_element_type=jnp.float32
-    )
-
-
-def filter_kernel(own_ref, other_ref, x_ref, whole_ref, w_ref, *, n_row, n_col, vec_cols):
+        orthonormal_factor(y), y, (((1,), (0,)), ((), ())),
+        precision=lax.Precision.HIGHEST, preferred_element_type=jnp.float32,
+    )
+
+
+def filter_kernel(own_ref, other_ref, x_ref, whole_ref, w_ref, inverse_ref, *, n_row, n_col, vec_cols):
     half_rows = own_ref.shape[0]
     total = 2 * half_rows
     block = own_ref.shape[1] - total
@@ -108,12 +112,18 @@
             preferred_element_type=jnp.float32,
         )
 
-    for outer in range(ITERS):
+    for outer in range(ITERS - 1):
         current = orthonormal_value(chebyshev(current, apply))
-    whole_ref[...] = current
+    filtered = chebyshev(current, apply)
+    inverse_ref[...] = orthonormal_factor(filtered)
+    whole_ref[...] = filtered
+    mine = inverse_ref[pl.ds(own_first, vec_cols), :]
     for local in range(nb_dev):
         place = pl.multiple_of((((local + core) % 2) * n_row + row) * block, 128)
-        x_ref[:, local * block : (local + 1) * block] = whole_ref[pl.ds(own_first, vec_cols), pl.ds(place, block)]
+        x_ref[:, local * block : (local + 1) * block] = lax.dot_general(
+            mine, whole_ref[:, pl.ds(place, block)], (((1,), (0,)), ((), ())),
+            precision=lax.Precision.HIGHEST, preferred_element_type=jnp.float32,
+        )
 
 def filter_local(own, other, n_row, n_col, vec_cols):
     total = 2 * own.shape[0]
@@ -127,6 +137,7 @@
         scratch_shapes=[
             pltpu.VMEM((2 * vec_cols, total), jnp.float32),
             pltpu.VMEM((total, total), jnp.bfloat16),
+            pltpu.VMEM((2 * vec_cols, 2 * vec_cols), jnp.float32),
         ],
     )(own, other)
 

time: 74.3 us -> 74 us (level)
  no operation moved by 1% of the time
where the time goes in v19:
time: 74 us; the launch traced here: 73.8 us
  blocking collectives  33.9 us (46%)
  Pallas kernels  20.6 us (28%)
  waiting for transfers between devices  9.01 us (12%)
  local copies, waits for them, and re-layouts  3.78 us (5%)
  starting transfers between devices  3 us (4%)
  other arithmetic  2.26 us (3%)
  between operations  0.83 us (1%)
    all_to_all x1, blocking collectives, replicated(): half = lax.all_to_all(copies, ('row', 'col'), 0, 0, tiled=True)  33.9 us
    pallas_call x1, Pallas kernels, filter_local(): pl.pallas_call(functools.partial(filter_kernel, n_row=n_row, n_col=n_col,...  20.6 us
    ppermute x1, waiting for transfers between devices, replicated(): lax.ppermute(sent, 'col', [(i, (i + shift) % n_col) for i in range(n_col)])  6.17 us
    ppermute x1, starting transfers between devices, replicated(): lax.ppermute(sent, 'col', [(i, (i + shift) % n_col) for i in range(n_col)])  2.99 us
    ppermute x1, waiting for transfers between devices, replicated(): other = lax.ppermute(half, 'vec', [(0, 1), (1, 0)])  2.84 us
  transfers between devices with their start and end apart: 2, of which 2 were waited for; matrix products, arithmetic and copies ran while one was open for 0% of the time, Pallas kernels for 0%

profile of v19, /device:TPU:0, one launch (start us, length us, event | category | flops | bytes accessed | tf_op | source)
XLA Modules:
  0.0 73.8 jit_solution(8172474000827800069)
XLA Ops:
  0.0 1.3 %dynamic_slice.28 = s32[1]{0:T(128)} dynamic-slice(s32[2]{0:T(128)} %param.7, s32[]{:T(128)S(6)} %select_n.51), dynamic_slice_sizes={1} | dynamic-slice | bytes 12 | tf_op jit(solution)/shard_map/jit(dynamic_index_in_dim)/dynamic_slice | solution.py:197
  1.3 0.7 fusion.22
  2.1 1.3 %fusion = f32[128]{0:T(128)S(1)} fusion(bf16[1,16,128,128]{3,2,1,0:T(8,128)(2,1)S(1)} %constant_dynamic-slice_fusion.1, bf16[16]{0:T(256)(128)(2,1)S(1)} %get-tuple-element.5), kind=kLoop, calls=%fused_computation.6 | loop fusion | flops 1048448 | bytes 524832 | tf_op jit(solution)/shard_map/kmn,kmn->m/dot_general | solution.py:206
  3.3 0.1 fusion.16
  3.4 0.4 convolution_bitcast_fusion
  3.8 0.1 concatenate.12
  3.9 0.1 broadcast_in_dim.6
  4.0 0.3 copy.13
  4.3 0.0 copy-start.3
  4.4 0.2 copy.14
  4.6 3.0 %collective-permute-start = (f32[64,1152]{1,0:T(8,128)S(1)}, f32[64,1152]{1,0:T(8,128)S(1)}, u32[]{:S(2)}, u32[]{:S(2)}) collective-permute-start(f32[64,1152]{1,0:T(8,128)S(1)} %bitcast.42), channel_id=1, source_target_pairs={{0,2},{2,0},{1,3},{3,1},{4,6},{6,4},{5,7},{7,5},{8,10},{10,8},{9,1... | collective-permute-start | bytes 884744 | tf_op jit(solution)/shard_map/ppermute | solution.py:213
  8.3 0.0 copy-done.3
  8.3 0.1 copy.24
  8.5 6.2 %collective-permute-done = f32[64,1152]{1,0:T(8,128)S(1)} collective-permute-done((f32[64,1152]{1,0:T(8,128)S(1)}, f32[64,1152]{1,0:T(8,128)S(1)}, u32[]{:S(2)}, u32[]{:S(2)}) %collective-permute-start) | collective-permute-done | bytes 294944 | tf_op jit(solution)/shard_map/ppermute | solution.py:213
  14.6 0.2 copy.15
  14.9 0.1 fusion.4
  15.0 0.1 maximum_maximum_fusion
  15.1 0.2 copy.17
  15.2 0.1 broadcast_in_dim.8
  15.4 33.9 %all_to_all.5 = bf16[8,64,1152]{2,1,0:T(8,128)(2,1)S(1)} all-to-all(bf16[8,64,1152]{2,1,0:T(8,128)(2,1)S(1)} %broadcast_in_dim.8), channel_id=1, replica_groups=mesh['grp'=2,'row'=4,'col'=2,'vec'=2] {'row','col'}, dimensions={0} | all-to-all | bytes 2359296 | tf_op jit(solution)/shard_map/all_to_all | solution.py:225
  49.3 0.0 collective-permute-start.1
  49.3 2.8 %collective-permute-done.1.other_ref = bf16[512,1152]{1,0:T(8,128)(2,1)S(1)} collective-permute-done((bf16[512,1152]{1,0:T(8,128)(2,1)S(1)}, bf16[512,1152]{1,0:T(8,128)(2,1)S(1)}, u32[]{:S(2)}, u32[]{:S(2)}) %collective-permute-start.1) | collective-permute-done | bytes 1179680 | tf_op jit(solution)/shard_map/ppermute | solution.py:227
  52.2 1.0 %copy-done.2 = bf16[512,1152]{1,0:T(8,128)(2,1)} copy-done((bf16[512,1152]{1,0:T(8,128)(2,1)}, bf16[512,1152]{1,0:T(8,128)(2,1)S(1)}, u32[]{:S(2)}) %copy-start.2) | copy-done | bytes 1179672
  53.2 20.6 %shard_map.46 = f32[32,256]{1,0:T(8,128)} custom-call(bf16[512,1152]{1,0:T(8,128)(2,1)} %bitcast.41, bf16[512,1152]{1,0:T(8,128)(2,1)} %copy-done.2), custom_call_target="tpu_custom_call" | custom-call | tf_op jit(solution)/shard_map/pallas_call | solution.py:132
  (14 shorter events, 0.2 us)
Async XLA Ops:
  0.0 2.0 %copy-start = (bf16[2,16,128,128]{3,2,1,0:T(8,128)(2,1)S(1)}, bf16[2,16,128,128]{3,2,1,0:T(8,128)(2,1)}, u32[]{:S(2)}) copy-start(bf16[2,16,128,128]{3,2,1,0:T(8,128)(2,1)} %param.5) | copy-start | bytes 3145732
  0.0 3.3 %copy-start.4 = (s32[2,32]{1,0:T(2,128)S(1)}, s32[2,32]{1,0:T(2,128)}, u32[]{:S(2)}) copy-start(s32[2,32]{1,0:T(2,128)} %param.6) | copy-start | bytes 772
  4.3 4.0 %copy-start.3 = (f32[32,256]{1,0:T(8,128)S(1)}, f32[32,256]{1,0:T(8,128)}, u32[]{:S(2)}) copy-start(f32[32,256]{1,0:T(8,128)} %param.4) | copy-start | bytes 98308
  4.6 10.0 %collective-permute-start = (f32[64,1152]{1,0:T(8,128)S(1)}, f32[64,1152]{1,0:T(8,128)S(1)}, u32[]{:S(2)}, u32[]{:S(2)}) collective-permute-start(f32[64,1152]{1,0:T(8,128)S(1)} %bitcast.42), channel_id=1, source_target_pairs={{0,2},{2,0},{1,3},{3,1},{4,6},{6,4},{5,7},{7,5},{8,10},{10,8},{9,1... | collective-permute-start | bytes 884744 | tf_op jit(solution)/shard_map/ppermute | solution.py:213
  49.3 2.9 %copy-start.1 = (bf16[8,64,1152]{2,1,0:T(8,128)(2,1)}, bf16[8,64,1152]{2,1,0:T(8,128)(2,1)S(1)}, u32[]{:S(2)}) copy-start(bf16[8,64,1152]{2,1,0:T(8,128)(2,1)S(1)} %all_to_all.5) | copy-start | bytes 3538948
  49.3 2.8 %collective-permute-start.1 = (bf16[512,1152]{1,0:T(8,128)(2,1)S(1)}, bf16[512,1152]{1,0:T(8,128)(2,1)S(1)}, u32[]{:S(2)}, u32[]{:S(2)}) collective-permute-start(bf16[512,1152]{1,0:T(8,128)(2,1)S(1)} %bitcast.40), channel_id=1, source_target_pairs={{0,1},{1,0},{2,3},{3,2},{4,5},{5,4},{6,7},{7,6},{8,9},{9,8},{10,11... | collective-permute-start | bytes 3538952 | tf_op jit(solution)/shard_map/ppermute | solution.py:227
  52.2 1.0 %copy-start.2 = (bf16[512,1152]{1,0:T(8,128)(2,1)}, bf16[512,1152]{1,0:T(8,128)(2,1)S(1)}, u32[]{:S(2)}) copy-start(bf16[512,1152]{1,0:T(8,128)(2,1)S(1)} %collective-permute-done.1.other_ref) | copy-start | bytes 3538948

commit v20 on v19

--- a/solution.py
+++ b/solution.py
@@ -199,18 +199,25 @@
     live = slot_ids < own_count
     position = (own_pattern % nb_dev) * n_row + own_pattern // nb_dev
     onehot = (position[:, None] == jnp.arange(nblk, dtype=jnp.int32)) & live[:, None]
-    dense = jnp.einsum(
-        "kj,kmn->mjn", onehot.astype(jnp.bfloat16), own_tiles, preferred_element_type=jnp.float32
-    ).reshape(block, total_rows)
-    masked = own_tiles * live.astype(jnp.bfloat16)[:, None, None]
-    squares = jnp.einsum("kmn,kmn->m", masked, masked, preferred_element_type=jnp.float32)
-    squares = jnp.broadcast_to(squares[:, None], (block, 128))
-    partial = jnp.concatenate([dense, squares], axis=1)
-    chunks = partial.reshape(n_col, share, total_rows + 128)
-    summed = lax.dynamic_index_in_dim(chunks, col_index, 0, keepdims=False)
+    weights = onehot.astype(jnp.bfloat16)
+    live_bf16 = live.astype(jnp.bfloat16)[:, None, None]
+
+    def chunk(index):
+        part = lax.dynamic_slice_in_dim(own_tiles, index * share, share, 1)
+        dense = jnp.einsum(
+            "kj,kmn->mjn", weights, part, preferred_element_type=jnp.float32
+        ).reshape(share, total_rows)
+        masked = part * live_bf16
+        squares = jnp.einsum("kmn,kmn->m", masked, masked, preferred_element_type=jnp.float32)
+        return jnp.concatenate([dense, jnp.broadcast_to(squares[:, None], (share, 128))], axis=1)
+
+    received = []
     for shift in range(1, n_col):
-        sent = lax.dynamic_index_in_dim(chunks, (col_index + shift) % n_col, 0, keepdims=False)
-        summed = summed + lax.ppermute(sent, "col", [(i, (i + shift) % n_col) for i in range(n_col)])
+        sent = chunk((col_index + shift) % n_col)
+        received.append(lax.ppermute(sent, "col", [(i, (i + shift) % n_col) for i in range(n_col)]))
+    summed = chunk(col_index)
+    for part in received:
+        summed = summed + part
 
     entries = (own_count * block).astype(jnp.float32)
     scale = lax.rsqrt(summed[:, total_rows] / entries + EPSILON) / jnp.sqrt(entries) / HALF_WIDTH

time: 74 us -> 74.5 us (level)
    dynamic_slice x2 -> x1, local copies, waits for them, and re-layouts: 0.26 us -> 1.22 us  [chunk(): part = lax.dynamic_slice_in_dim(own_tiles, index * share, share, 1)]
  transfers between devices with their start and end apart: 2 -> 2, of which waited for: 2 -> 2; matrix products, arithmetic and copies ran while one was open for 0% -> 1% of each run, Pallas kernels for 0% -> 0%
where the time goes in v20:
time: 74.5 us; the launch traced here: 74.2 us
  blocking collectives  33.9 us (46%)
  Pallas kernels  20.6 us (28%)
  waiting for transfers between devices  8.51 us (11%)
  local copies, waits for them, and re-layouts  4.51 us (6%)
  starting transfers between devices  3 us (4%)
  other arithmetic  2.38 us (3%)
  between operations  0.81 us (1%)
    all_to_all x1, blocking collectives, replicated(): half = lax.all_to_all(copies, ('row', 'col'), 0, 0, tiled=True)  33.9 us
    pallas_call x1, Pallas kernels, filter_local(): pl.pallas_call(functools.partial(filter_kernel, n_row=n_row, n_col=n_col,...  20.6 us
    ppermute x1, waiting for transfers between devices, replicated(): lax.ppermute(sent, 'col', [(i, (i + shift) % n_col) for i in range(n_col)])  5.67 us
    ppermute x1, starting transfers between devices, replicated(): lax.ppermute(sent, 'col', [(i, (i + shift) % n_col) for i in range(n_col)])  3 us
    ppermute x1, waiting for transfers between devices, replicated(): other = lax.ppermute(half, 'vec', [(0, 1), (1, 0)])  2.84 us
  transfers between devices with their start and end apart: 2, of which 2 were waited for; matrix products, arithmetic and copies ran while one was open for 1% of the time, Pallas kernels for 0%

profile of v20, /device:TPU:0, one launch (start us, length us, event | category | flops | bytes accessed | tf_op | source)
XLA Modules:
  0.0 74.2 jit_solution(14191138103938254842)
XLA Ops:
  0.0 0.0 copy-start
  0.0 1.2 %dynamic_slice.30 = s32[1]{0:T(128)} dynamic-slice(s32[2]{0:T(128)} %param.7, s32[]{:T(128)S(6)} %select_n.54), dynamic_slice_sizes={1} | dynamic-slice | bytes 12 | tf_op jit(solution)/shard_map/jit(dynamic_index_in_dim)/dynamic_slice | solution.py:197
  1.2 0.7 fusion.26
  1.9 0.8 %fusion.20 = s32[16]{0:T(128)S(1)} fusion(s32[2,32]{1,0:T(2,128)} %param.6, s32[]{:T(128)S(6)} %select_n.55, s32[]{:T(128)S(6)} %select_n.59), kind=kLoop, calls=%fused_computation.39 | loop fusion | flops 336 | bytes 136 | tf_op jit(solution)/shard_map/add | solution.py:200
  2.7 1.2 %constant_dynamic-slice_fusion.1 = (bf16[1,16,64,128]{3,2,1,0:T(8,128)(2,1)S(1)}, bf16[1,16,64,128]{3,2,1,0:T(8,128)(2,1)S(1)}) fusion(bf16[2,16,128,128]{3,2,1,0:T(8,128)(2,1)} %param.5, s32[]{:T(128)S(6)} %select_n.55, s32[]{:T(128)S(6)} %select_n.64, s32[]{:T(128)S(6)} %select_n.57), kind=kLoop, calls=%fused_computation.36 | loop fusion | bytes 1048588 | tf_op jit(solution)/shard_map/dynamic_slice | solution.py:206
  3.9 0.3 fusion.3
  4.2 0.7 fusion.2
  4.9 0.1 broadcast_in_dim.7
  5.0 3.0 %collective-permute-start = (f32[64,1152]{1,0:T(8,128)S(1)}, f32[64,1152]{1,0:T(8,128)S(1)}, u32[]{:S(2)}, u32[]{:S(2)}) collective-permute-start(f32[64,1152]{1,0:T(8,128)S(1)} %pad_maximum_fusion), channel_id=1, source_target_pairs={{0,2},{2,0},{1,3},{3,1},{4,6},{6,4},{5,7},{7,5},{8,10},{10,8},{9,1... | collective-permute-start | bytes 884744 | tf_op jit(solution)/shard_map/ppermute | solution.py:217
  8.7 0.3 convolution_bitcast_fusion
  9.0 0.1 copy.33
  9.1 0.2 copy.16
  9.4 5.7 %collective-permute-done = f32[64,1152]{1,0:T(8,128)S(1)} collective-permute-done((f32[64,1152]{1,0:T(8,128)S(1)}, f32[64,1152]{1,0:T(8,128)S(1)}, u32[]{:S(2)}, u32[]{:S(2)}) %collective-permute-start) | collective-permute-done | bytes 294944 | tf_op jit(solution)/shard_map/ppermute | solution.py:217
  15.1 0.2 copy.18
  15.3 0.1 maximum_add_fusion
  15.4 0.1 maximum_maximum_fusion
  15.5 0.2 copy.20
  15.7 0.1 broadcast_in_dim.8
  15.8 33.9 %all_to_all.5 = bf16[8,64,1152]{2,1,0:T(8,128)(2,1)S(1)} all-to-all(bf16[8,64,1152]{2,1,0:T(8,128)(2,1)S(1)} %broadcast_in_dim.8), channel_id=1, replica_groups=mesh['grp'=2,'row'=4,'col'=2,'vec'=2] {'row','col'}, dimensions={0} | all-to-all | bytes 2359296 | tf_op jit(solution)/shard_map/all_to_all | solution.py:232
  49.8 0.0 collective-permute-start.1
  49.8 2.8 %collective-permute-done.1.other_ref = bf16[512,1152]{1,0:T(8,128)(2,1)S(1)} collective-permute-done((bf16[512,1152]{1,0:T(8,128)(2,1)S(1)}, bf16[512,1152]{1,0:T(8,128)(2,1)S(1)}, u32[]{:S(2)}, u32[]{:S(2)}) %collective-permute-start.1) | collective-permute-done | bytes 1179680 | tf_op jit(solution)/shard_map/ppermute | solution.py:234
  52.6 0.0 copy-done.1
  52.6 1.0 %copy-done.2 = bf16[512,1152]{1,0:T(8,128)(2,1)} copy-done((bf16[512,1152]{1,0:T(8,128)(2,1)}, bf16[512,1152]{1,0:T(8,128)(2,1)S(1)}, u32[]{:S(2)}) %copy-start.2) | copy-done | bytes 1179672
  53.7 20.6 %shard_map.46 = f32[32,256]{1,0:T(8,128)} custom-call(bf16[512,1152]{1,0:T(8,128)(2,1)} %bitcast.56, bf16[512,1152]{1,0:T(8,128)(2,1)} %copy-done.2), custom_call_target="tpu_custom_call" | custom-call | tf_op jit(solution)/shard_map/pallas_call | solution.py:132
  (10 shorter events, 0.2 us)
Async XLA Ops:
  0.0 9.0 %copy-start = (f32[32,256]{1,0:T(8,128)S(1)}, f32[32,256]{1,0:T(8,128)}, u32[]{:S(2)}) copy-start(f32[32,256]{1,0:T(8,128)} %param.4) | copy-start | bytes 98308
  5.0 10.0 %collective-permute-start = (f32[64,1152]{1,0:T(8,128)S(1)}, f32[64,1152]{1,0:T(8,128)S(1)}, u32[]{:S(2)}, u32[]{:S(2)}) collective-permute-start(f32[64,1152]{1,0:T(8,128)S(1)} %pad_maximum_fusion), channel_id=1, source_target_pairs={{0,2},{2,0},{1,3},{3,1},{4,6},{6,4},{5,7},{7,5},{8,10},{10,8},{9,1... | collective-permute-start | bytes 884744 | tf_op jit(solution)/shard_map/ppermute | solution.py:217
  49.8 2.9 %copy-start.1 = (bf16[8,64,1152]{2,1,0:T(8,128)(2,1)}, bf16[8,64,1152]{2,1,0:T(8,128)(2,1)S(1)}, u32[]{:S(2)}) copy-start(bf16[8,64,1152]{2,1,0:T(8,128)(2,1)S(1)} %all_to_all.5) | copy-start | bytes 3538948
  49.8 2.8 %collective-permute-start.1 = (bf16[512,1152]{1,0:T(8,128)(2,1)S(1)}, bf16[512,1152]{1,0:T(8,128)(2,1)S(1)}, u32[]{:S(2)}, u32[]{:S(2)}) collective-permute-start(bf16[512,1152]{1,0:T(8,128)(2,1)S(1)} %bitcast.55), channel_id=1, source_target_pairs={{0,1},{1,0},{2,3},{3,2},{4,5},{5,4},{6,7},{7,6},{8,9},{9,8},{10,11... | collective-permute-start | bytes 3538952 | tf_op jit(solution)/shard_map/ppermute | solution.py:234
  52.6 1.0 %copy-start.2 = (bf16[512,1152]{1,0:T(8,128)(2,1)}, bf16[512,1152]{1,0:T(8,128)(2,1)S(1)}, u32[]{:S(2)}) copy-start(bf16[512,1152]{1,0:T(8,128)(2,1)S(1)} %collective-permute-done.1.other_ref) | copy-start | bytes 3538948
